TPU v7x, 128 devices: a whole 4x4x4 slice. The times are simulated.
128 devices in a mesh: pipe: 2 (over x_hi), ctx: 32 (over y, z, core), tp: 2 (over x_lo).
Axes of the slice: x: 4 (x_hi: 2, x_lo: 2; x = x_hi * 2 + x_lo), y: 4, z: 4, core: 2. Of those that a mesh axis runs over, the one named last changes fastest.
Arguments:
- resid_in: bfloat16 [4096, 4096], P('ctx', 'tp'), may hold values from -6 to 6
- ssm_input: bfloat16 [4096, 8192], P('ctx', 'tp'), may hold values from -6 to 6
- ssm_gate: bfloat16 [4096, 8192], P('ctx', 'tp'), may hold values from -6 to 6
- ssm_in_b: bfloat16 [4096, 512], P('ctx', 'tp'), may hold values from -0.5 to 0.5
- ssm_out_c: bfloat16 [4096, 512], P('ctx', 'tp'), may hold values from -6 to 6
- step_size: float32 [4096, 128], P('ctx', 'tp'), as said below
- decay_rate: float32 [128], P('tp'), may hold values from 0.0001 to 1, as said below
- skip_gain: float32 [128], P('tp'), may hold values from 0.5 to 1.5
- norm_gain: float32 [8192], P('tp'), may hold values from 0.1 to 1.9
- queries: bfloat16 [4096, 8192], P('ctx', 'tp'), may hold values from -6 to 6
- keys: bfloat16 [4096, 512], P('ctx', 'tp'), may hold values from -6 to 6
- values: bfloat16 [4096, 512], P('ctx', 'tp'), may hold values from -6 to 6
- out_weights: bfloat16 [2, 8192, 4096], P('pipe', 'tp', 'ctx'), may hold values from -0.0625 to 0.0625
Outputs:
- sections_out: bfloat16 [2, 4096, 4096], P('pipe', 'ctx', 'tp')
Inputs may be any that keep to these rules, and one draw needn't show every extreme that they name: `step_size`: step sizes are positive. `decay_rate`: rates are positive.
All inputs are finite; a program needn't handle non-finite values.
Results may differ from a plain program's by a relative error of at most 0.015.
Values may be sent and summed in bfloat16 or wider, within the bound.
No kernel may reach another device: no remote copies, remote signals or barrier semaphores. Data moves between devices by JAX's collectives and lax.ppermute only.
A program may use at most 256 MiB of HBM per device.

v0:
```python
import math

import jax
import jax.numpy as jnp
from jax import lax
from jax.sharding import PartitionSpec as P

MHEAD_DIM = 64
STATE = 128
SCAN_BLOCK = 128
HEAD_DIM = 128


exact_mode = lax.Precision.HIGHEST
norm_eps = 1e-05


def entering_2(x, axis, combine, identity):
    peers, position = (lax.axis_size(axis), lax.axis_index(axis))
    everything = jax.tree.map(
        lambda part, kind: lax.all_gather(part.astype(kind), axis), x, (jnp.bfloat16, jnp.bfloat16)
    )
    start = jax.tree.map(
        lambda part, zero: jnp.broadcast_to(jnp.asarray(zero, part.dtype), part.shape), x, identity
    )

    def turn(k, before):
        reached = k < position
        new = combine(
            before, jax.tree.map(lambda part, own: part[k].astype(own.dtype), everything, x)
        )
        return jax.tree.map(lambda a, b: jnp.where(reached, a, b), new, before)

    return lax.fori_loop(0, peers, turn, start)


def from_partner(block, axis, distance):
    count = lax.axis_size(axis)
    route = []
    for low in range(count):
        high = low | 1 << distance
        if high != low and high < count:
            route += [(low, high), (high, low)]
    return lax.ppermute(block, axis, route)


def shifted(x, axis, by):
    peers = lax.axis_size(axis)
    pairs = [(i, i + by) for i in range(peers) if 0 <= i + by < peers]
    return lax.ppermute(x, axis, pairs)


def block_scan(state_now, inputs_x, input_b, output_c, step_rows, log_decay):
    width = inputs_x.shape[0]
    groups = inputs_x.shape[1]
    per_group = inputs_x.shape[2]
    running = jnp.cumsum(log_decay, axis=0)
    spread = running[:, None, :] - running[None, :, :]
    causal = (
        jnp.arange(width, dtype=jnp.int32)[:, None] >= jnp.arange(width, dtype=jnp.int32)[None, :]
    )
    decay_mat = jnp.exp(jnp.where(causal[:, :, None], spread, -jnp.inf))
    decay_mat = decay_mat.reshape(width, width, groups, per_group).transpose(2, 3, 0, 1)
    cross_cb = jnp.einsum("tgn,sgn->gts", output_c, input_b, precision=exact_mode)
    step_cols = step_rows.reshape(width, groups, per_group).transpose(1, 2, 0)
    mixing = cross_cb[:, None, :, :] * decay_mat * step_cols[:, :, None, :]
    within = jnp.einsum("gjts,sgjp->tgjp", mixing, inputs_x, precision=exact_mode)
    entry = jnp.exp(running).reshape(width, groups, per_group)
    carried = (
        jnp.einsum("tgn,gjpn->tgjp", output_c, state_now, precision=exact_mode)
        * entry[:, :, :, None]
    )
    tail_weight = (jnp.exp(running[-1][None, :] - running) * step_rows).reshape(
        width, groups, per_group
    )
    leaving = jnp.exp(running[-1]).reshape(groups, per_group)
    state_next = leaving[:, :, None, None] * state_now + jnp.einsum(
        "sgj,sgjp,sgn->gjpn", tail_weight, inputs_x, input_b, precision=exact_mode
    )
    return (state_next, within + carried)


def gate_norm(values_y, gate_in, gains, groups):
    rows_here = values_y.shape[0]
    gated = values_y * jax.nn.silu(gate_in.astype(jnp.float32))
    grouped = gated.reshape(rows_here, groups, -1)
    meansq = jnp.mean(grouped * grouped, axis=-1, keepdims=True)
    scaled = (grouped * lax.rsqrt(meansq + norm_eps)).reshape(rows_here, -1)
    return (scaled * gains[None, :]).astype(jnp.bfloat16)


def join_states(earlier, later):
    return (earlier[0] * later[0], later[0][:, :, None, None] * earlier[1] + later[1])


def mamba_mixer(
    ssm_input, ssm_gate, ssm_in_b, ssm_out_c, step_size, decay_rate, skip_gain, norm_gain
):
    rows_here = ssm_input.shape[0]
    head_count = decay_rate.shape[0]
    groups = ssm_in_b.shape[1] // STATE
    per_group = head_count // groups
    block_count = rows_here // SCAN_BLOCK
    log_decay = -step_size * decay_rate[None, :]
    inputs_x = ssm_input.reshape(block_count, SCAN_BLOCK, groups, per_group, MHEAD_DIM)
    input_b = ssm_in_b.reshape(block_count, SCAN_BLOCK, groups, STATE)
    output_c = ssm_out_c.reshape(block_count, SCAN_BLOCK, groups, STATE)

    def block_turn(state_now, block_data):
        part_x, part_b, part_c, part_step, part_log = block_data
        return block_scan(
            state_now,
            part_x.astype(jnp.float32),
            part_b.astype(jnp.float32),
            part_c.astype(jnp.float32),
            part_step,
            part_log,
        )

    start_state = jnp.zeros((groups, per_group, MHEAD_DIM, STATE), jnp.float32)
    local_state, pieces = lax.scan(
        block_turn,
        start_state,
        (
            inputs_x,
            input_b,
            output_c,
            step_size.reshape(block_count, SCAN_BLOCK, head_count),
            log_decay.reshape(block_count, SCAN_BLOCK, head_count),
        ),
    )
    running = jnp.cumsum(log_decay, axis=0)
    through = jnp.exp(running[-1]).reshape(groups, per_group)
    prior = entering_2(
        (through, local_state),
        "ctx",
        join_states,
        (jnp.ones_like(through), jnp.zeros_like(local_state)),
    )
    entering = prior[1]
    output_all = ssm_out_c.astype(jnp.float32).reshape(rows_here, groups, STATE)
    carried = (
        jnp.einsum("tgn,gjpn->tgjp", output_all, entering, precision=exact_mode)
        * jnp.exp(running).reshape(rows_here, groups, per_group)[:, :, :, None]
    )
    skipped = (
        ssm_input.astype(jnp.float32).reshape(rows_here, groups, per_group, MHEAD_DIM)
        * skip_gain.reshape(groups, per_group)[None, :, :, None]
    )
    values_y = pieces.reshape(rows_here, groups, per_group, MHEAD_DIM) + carried + skipped
    return gate_norm(values_y.reshape(rows_here, -1), ssm_gate, norm_gain, groups)


def attention(queries, keys, values, ctx_rank):
    rows_here = queries.shape[0]
    kv_count = keys.shape[1] // HEAD_DIM
    per_key = queries.shape[1] // HEAD_DIM // kv_count
    query_groups = queries.reshape(rows_here, kv_count, per_key, HEAD_DIM)
    query_pos = ctx_rank * rows_here + jnp.arange(rows_here, dtype=jnp.int32)
    last_query = query_pos[-1]
    score_scale = 1.0 / math.sqrt(HEAD_DIM)

    def key_block(running, block_data):
        key_rows, value_rows, first_key = block_data

        def absorb(held):
            row_max, row_sum, weighted = held
            scores = (
                jnp.einsum(
                    "qgjd,kgd->gjqk", query_groups, key_rows, preferred_element_type=jnp.float32
                )
                * score_scale
            )
            key_pos = first_key + jnp.arange(key_rows.shape[0], dtype=jnp.int32)
            allowed = key_pos[None, :] <= query_pos[:, None]
            scores = jnp.where(allowed, scores, -1e30)
            new_max = jnp.maximum(row_max, jnp.max(scores, axis=-1))
            rescale = jnp.exp(row_max - new_max)
            weights_exp = jnp.where(allowed, jnp.exp(scores - new_max[..., None]), 0.0)
            row_sum = row_sum * rescale + jnp.sum(weights_exp, axis=-1)
            weighted = weighted * rescale[..., None] + jnp.einsum(
                "gjqk,kgd->gjqd",
                weights_exp.astype(jnp.bfloat16),
                value_rows,
                preferred_element_type=jnp.float32,
            )
            return (new_max, row_sum, weighted)

        return (lax.cond(first_key <= last_query, absorb, lambda held: held, running), None)

    start_state = (
        jnp.full((kv_count, per_key, rows_here), -1e30, jnp.float32),
        jnp.zeros((kv_count, per_key, rows_here), jnp.float32),
        jnp.zeros((kv_count, per_key, rows_here, HEAD_DIM), jnp.float32),
    )
    running = start_state
    key_piece = lax.all_gather(keys, "ctx", axis=0, tiled=True)
    value_piece = lax.all_gather(values, "ctx", axis=0, tiled=True)
    count = key_piece.shape[0]
    width = math.gcd(count, 1024)
    blocks = count // width
    key_rows = key_piece.reshape(blocks, width, kv_count, HEAD_DIM)
    value_rows = value_piece.reshape(blocks, width, kv_count, HEAD_DIM)
    starts = width * jnp.arange(blocks, dtype=jnp.int32)
    running, unused = lax.scan(key_block, running, (key_rows, value_rows, starts))
    row_max, row_sum, weighted = running
    mixed = (weighted / row_sum[..., None]).transpose(2, 0, 1, 3).reshape(rows_here, -1)
    return mixed.astype(jnp.bfloat16)


def take_half(array, axis_dim, section):
    width = array.shape[axis_dim] // 2
    return lax.dynamic_slice_in_dim(array, section * width, width, axis_dim)


def per_device(
    resid_in,
    ssm_input,
    ssm_gate,
    ssm_in_b,
    ssm_out_c,
    step_size,
    decay_rate,
    skip_gain,
    norm_gain,
    queries,
    keys,
    values,
    out_weights,
):
    section = lax.axis_index("pipe")
    ctx_rank = lax.axis_index("ctx")
    mamba_part = mamba_mixer(
        take_half(ssm_input, 1, section),
        take_half(ssm_gate, 1, section),
        take_half(ssm_in_b, 1, section),
        take_half(ssm_out_c, 1, section),
        take_half(step_size, 1, section),
        take_half(decay_rate, 0, section),
        take_half(skip_gain, 0, section),
        take_half(norm_gain, 0, section),
    )
    attn_part = attention(
        take_half(queries, 1, section),
        take_half(keys, 1, section),
        take_half(values, 1, section),
        ctx_rank,
    )
    outgoing = jnp.where(section == 0, attn_part, mamba_part)
    kept_half = jnp.where(section == 0, mamba_part, attn_part)
    incoming = from_partner(outgoing, "pipe", 0)
    mixed_rows = jnp.where(
        section == 0,
        jnp.concatenate([kept_half, incoming], axis=1),
        jnp.concatenate([incoming, kept_half], axis=1),
    )
    partial_value = jnp.dot(
        mixed_rows,
        lax.all_gather(out_weights, "ctx", axis=2, tiled=True)[0],
        preferred_element_type=jnp.float32,
    )
    projected = lax.psum_scatter(
        partial_value.astype(jnp.bfloat16), "tp", scatter_dimension=1, tiled=True
    ).astype(jnp.float32)
    own_section = (resid_in.astype(jnp.float32) + projected).astype(jnp.bfloat16)
    received = shifted(own_section, "pipe", 1)
    second_section = (received.astype(jnp.float32) + projected).astype(jnp.bfloat16)
    return jnp.where(section == 0, own_section, second_section)[None]


def solution(mesh):
    return jax.shard_map(
        per_device,
        mesh=mesh,
        in_specs=(
            P("ctx", "tp"),
            P("ctx", "tp"),
            P("ctx", "tp"),
            P("ctx", "tp"),
            P("ctx", "tp"),
            P("ctx", "tp"),
            P("tp"),
            P("tp"),
            P("tp"),
            P("ctx", "tp"),
            P("ctx", "tp"),
            P("ctx", "tp"),
            P("pipe", "tp", "ctx"),
        ),
        out_specs=P("pipe", "ctx", "tp"),
        check_vma=False,
    )
```

profile of v0, /device:TPU:30, one launch (start us, length us, event | category | flops | bytes accessed | tf_op | source)
XLA Modules:
  0.0 365.3 jit_solution(17626709086863027747)
XLA Ops:
  6.6 1.4 constant_dynamic-slice_fusion.2
  8.0 1.4 constant_dynamic-slice_fusion
  12.9 2.3 fusion.47
  17.3 1.3 copy.64
  19.3 22.0 %all-gather.2 = bf16[32,1,32]{2,1,0:T(2,128)(2,1)S(1)} all-gather(bf16[1,1,32]{2,1,0:T(2,128)(2,1)S(1)} %get-tuple-element.398), channel_id=2, replica_groups=mesh['pipe'=2,'ctx'=32,'tp'=2] {'ctx'}, dimensions={0}, use_global_device_ids=true | all-gather | bytes 2112 | tf_op jit(solution)/shard_map/all_gather | solution.py:21
  41.5 4.4 %fusion.39 = f32[128,1,32,64]{0,3,2,1:T(8,128)} fusion(bf16[128,32,64]{0,2,1:T(8,128)(2,1)} %bitcast.158, f32[32,128]{1,0:T(8,128)S(1)} %fusion.92, f32[128,32]{0,1:T(8,128)S(1)} %copy.55, f32[128,128]{1,0:T(8,128)S(1)} %fusion.78, pred[128,128]{1,0:T(8,128)(4,1)S(1)} %iota_compare_fusion), kind=kOutput, calls=%fused_computation.42 | convolution fusion | flops 404750336 | bytes 1687552 | tf_op jit(solution)/shard_map/while/body/eval_jaxpr/gjts,sgjp->tgjp/dot_general | solution.py:67
  45.9 8.1 %all-gather.8.cloned.1.call-done = bf16[4096,128]{1,0:T(8,128)(2,1)} async-done(((bf16[128,128]{1,0:T(8,128)(2,1)}), bf16[4096,128]{1,0:T(8,128)(2,1)}) %all-gather.8.cloned.1.call-update) | async-done | bytes 1048592 | tf_op jit(solution)/shard_map/all_gather | solution.py:197
  54.1 44.2 %all-gather.10.cloned.1.call-done = bf16[4096,128]{1,0:T(8,128)(2,1)} async-done(((bf16[128,128]{1,0:T(8,128)(2,1)}), bf16[4096,128]{1,0:T(8,128)(2,1)}) %all-gather.10.cloned.1.call-update) | async-done | bytes 1048592 | tf_op jit(solution)/shard_map/all_gather | solution.py:198
  99.4 47.7 %while.34 = (s32[]{:T(128)}, f32[1,16,128]{2,1,0:T(8,128)S(1)}, f32[1,16,128]{2,1,0:T(8,128)S(1)}, f32[1,16,128,128]{3,2,1,0:T(8,128)}, s32[4]{0:T(128)S(1)}, /*...) while((s32[]{:T(128)}, f32[1,16,128]{2,1,0:T(8,128)S(1)}, ...), condition=%wide.region_9.10_spmd.clone, body=%wide.region_4.9_spmd.clone.sunk | while | flops 1101667456 | bytes 37367120 | solution.py:205
  101.4 10.0 %conditional.3 = ((f32[1,16,128]{2,1,0:T(8,128)S(1)}, f32[1,16,128]{2,1,0:T(8,128)S(1)}, f32[1,16,128,128]{3,2,1,0:T(8,128)})) conditional(s32[]{:T(128)} %convert_element_type.170, (f32[1,16,128]{2,1,0:T(8,128)S(1)}, f32[1,16,128]{2,1,0:T(8,128)S(1)}, f32[1,16,128,128]{3,2,1,0:T(8,128)}) %tuple.77, (s32[]{:T(128)}, s32[]{:T(128)}, ...), branch_computations={%region_5.5_spmd, %region_6.8_spmd} | conditional | flops 1101667456 | bytes 37366368 | solution.py:189
  102.3 2.3 fusion.2
  104.7 2.0 fusion.4
  106.7 3.6 fusion.12
  113.3 10.0 %conditional.3 = ((f32[1,16,128]{2,1,0:T(8,128)S(1)}, f32[1,16,128]{2,1,0:T(8,128)S(1)}, f32[1,16,128,128]{3,2,1,0:T(8,128)})) conditional(s32[]{:T(128)} %convert_element_type.170, (f32[1,16,128]{2,1,0:T(8,128)S(1)}, f32[1,16,128]{2,1,0:T(8,128)S(1)}, f32[1,16,128,128]{3,2,1,0:T(8,128)}) %tuple.77, (s32[]{:T(128)}, s32[]{:T(128)}, ...), branch_computations={%region_5.5_spmd, %region_6.8_spmd} | conditional | flops 1101667456 | bytes 37366368 | solution.py:189
  114.2 2.3 fusion.2
  116.6 2.0 fusion.4
  118.6 3.6 fusion.12
  125.2 10.0 %conditional.3 = ((f32[1,16,128]{2,1,0:T(8,128)S(1)}, f32[1,16,128]{2,1,0:T(8,128)S(1)}, f32[1,16,128,128]{3,2,1,0:T(8,128)})) conditional(s32[]{:T(128)} %convert_element_type.170, (f32[1,16,128]{2,1,0:T(8,128)S(1)}, f32[1,16,128]{2,1,0:T(8,128)S(1)}, f32[1,16,128,128]{3,2,1,0:T(8,128)}) %tuple.77, (s32[]{:T(128)}, s32[]{:T(128)}, ...), branch_computations={%region_5.5_spmd, %region_6.8_spmd} | conditional | flops 1101667456 | bytes 37366368 | solution.py:189
  126.1 2.3 fusion.2
  128.5 2.0 fusion.4
  130.5 3.6 fusion.12
  137.1 10.0 %conditional.3 = ((f32[1,16,128]{2,1,0:T(8,128)S(1)}, f32[1,16,128]{2,1,0:T(8,128)S(1)}, f32[1,16,128,128]{3,2,1,0:T(8,128)})) conditional(s32[]{:T(128)} %convert_element_type.170, (f32[1,16,128]{2,1,0:T(8,128)S(1)}, f32[1,16,128]{2,1,0:T(8,128)S(1)}, f32[1,16,128,128]{3,2,1,0:T(8,128)}) %tuple.77, (s32[]{:T(128)}, s32[]{:T(128)}, ...), branch_computations={%region_5.5_spmd, %region_6.8_spmd} | conditional | flops 1101667456 | bytes 37366368 | solution.py:189
  138.1 2.3 fusion.2
  140.4 2.0 fusion.4
  142.5 3.6 fusion.12
  147.1 1.6 fusion.73
  149.8 23.0 %all-gather.14.cloned.1.call-done = bf16[1024,64,128]{2,1,0:T(8,128)(2,1)} async-done(((bf16[32,64,128]{2,1,0:T(8,128)(2,1)}), bf16[1024,64,128]{2,1,0:T(8,128)(2,1)}) %all-gather.14.cloned.1.call-update) | async-done | bytes 16777232 | tf_op jit(solution)/shard_map/all_gather | solution.py:21
  172.8 43.0 %while.35 = (s32[]{:T(128)}, f32[1,32,64,128]{3,2,1,0:T(8,128)S(1)}, s32[]{:T(128)}, bf16[32,1,32]{2,1,0:T(2,128)(2,1)S(1)}, bf16[32,1,32,64,128]{4,3,2,1,0:T(8,128)(2,1)}, /*index=5*/s32[]{:T(128)}, s32[]{:T(128)}) while((s32[]{:T(128)}, f32[1,32,64,128]{3,2,1,0:T(8,128)S(1)}, s32[]{:T(128)}, bf16[32,1,32]{2,1,0:T(2,128)(2,1)S(1)}, ...), condition=%wide.region_2.3_spmd.clone, body=%wide.region_1.2_spmd.clone.sunk | while | flops 1310756 | bytes 2621865 | solution.py:34
  172.8 1.3 fusion.94
  174.2 1.3 fusion.94
  176.9 1.3 fusion.94
  178.2 1.3 fusion.94
  179.5 1.3 fusion.94
  180.9 1.3 fusion.94
  183.6 1.4 fusion.94
  184.9 1.3 fusion.94
  186.3 1.3 fusion.94
  187.7 1.3 fusion.94
  190.4 1.3 fusion.94
  191.7 1.3 fusion.94
  193.1 1.3 fusion.94
  194.4 1.3 fusion.94
  195.7 1.3 fusion.94
  197.1 1.3 fusion.94
  199.8 1.3 fusion.94
  201.1 1.3 fusion.94
  202.5 1.3 fusion.94
  203.8 1.3 fusion.94
  205.2 1.3 fusion.94
  206.5 1.3 fusion.94
  207.9 1.3 fusion.94
  209.2 1.3 fusion.94
  210.5 1.3 fusion.94
  213.2 1.3 fusion.94
  216.5 1.8 fusion.45
  218.6 1.7 multiply_reduce_fusion
  220.3 1.8 bitcast_select_fusion.2
  222.1 1.8 collective-permute-start
  223.9 14.1 %collective-permute-done = bf16[128,2048]{1,0:T(8,128)(2,1)S(1)} collective-permute-done((bf16[128,2048]{1,0:T(8,128)(2,1)S(1)}, bf16[128,2048]{1,0:T(8,128)(2,1)S(1)}, u32[]{:S(2)}, u32[]{:S(2)}) %collective-permute-start) | collective-permute-done | bytes 524320 | tf_op jit(solution)/shard_map/ppermute | solution.py:44
  238.0 61.1 %all-gather.12.cloned.1.call-done = bf16[1,4096,4096]{2,1,0:T(8,128)(2,1)} async-done(((bf16[1,4096,128]{2,1,0:T(8,128)(2,1)}), bf16[1,4096,4096]{2,1,0:T(8,128)(2,1)}) %all-gather.12.cloned.1.call-update) | async-done | bytes 33554448 | tf_op jit(solution)/shard_map/all_gather | solution.py:259
  299.1 16.1 %fusion.30 = bf16[128,4096]{1,0:T(8,128)(2,1)} fusion(bf16[1,4096,4096]{2,1,0:T(8,128)(2,1)} %all-gather.12.cloned.1.call-done, bf16[128,2048]{1,0:T(8,128)(2,1)S(1)} %collective-permute-done, bf16[128,2048]{1,0:T(8,128)(2,1)S(1)} %get-tuple-element.393, pred[]{:T(512)S(6)} %eq.2), kind=kOutput, calls=%fused_computation.34 | convolution fusion | flops 4300210176 | bytes 35651584 | tf_op jit(solution)/shard_map/dot_general | solution.py:257
  315.3 23.4 %reduce-scatter.2.cloned.1.call-done = bf16[128,2048]{1,0:T(8,128)(2,1)} async-done(((bf16[128,4096]{1,0:T(8,128)(2,1)}), bf16[128,2048]{1,0:T(8,128)(2,1)}) %reduce-scatter.2.cloned.1.call-update) | async-done | bytes 524304 | tf_op jit(solution)/shard_map/reduce_scatter | solution.py:262
  341.2 15.6 %collective-permute-done.1 = bf16[128,2048]{1,0:T(8,128)(2,1)S(1)} collective-permute-done((bf16[128,2048]{1,0:T(8,128)(2,1)S(1)}, bf16[128,2048]{1,0:T(8,128)(2,1)S(1)}, u32[]{:S(2)}, u32[]{:S(2)}) %collective-permute-start.1) | collective-permute-done | bytes 524320 | tf_op jit(solution)/shard_map/ppermute | solution.py:50
  356.7 2.1 fusion.70
  (142 shorter events, 30.4 us)
Async XLA Ops:
  6.5 34.8 %copy-start = (bf16[128,256]{1,0:T(8,128)(2,1)S(1)}, bf16[128,256]{1,0:T(8,128)(2,1)}, u32[]{:S(2)}) copy-start(bf16[128,256]{1,0:T(8,128)(2,1)} %param.23) | copy-start | bytes 196612
  6.5 34.8 %copy-start.6 = (f32[128,64]{0,1:T(8,128)S(1)}, f32[128,64]{0,1:T(8,128)}, u32[]{:S(2)}) copy-start(f32[128,64]{0,1:T(8,128)} %param.24) | copy-start | bytes 98308
  6.5 34.8 %copy-start.5 = (bf16[128,256]{1,0:T(8,128)(2,1)S(1)}, bf16[128,256]{1,0:T(8,128)(2,1)}, u32[]{:S(2)}) copy-start(bf16[128,256]{1,0:T(8,128)(2,1)} %param.22) | copy-start | bytes 196612
  6.5 9.6 %copy-start.7 = (f32[64]{0:T(128)S(1)}, f32[64]{0:T(128)}, u32[]{:S(2)}) copy-start(f32[64]{0:T(128)} %param.26) | copy-start | bytes 772
  6.5 47.5 %all-gather.8.cloned.1.call-start = ((), (), s32[]{:S(2)}) async-start(), calls=%async_computation.1 | async-start | bytes 1081344 | tf_op jit(solution)/shard_map/all_gather | solution.py:197
  8.0 90.3 %all-gather.10.cloned.1.call-start = ((), (), s32[]{:S(2)}) async-start(), calls=%async_computation.2 | async-start | bytes 1081344 | tf_op jit(solution)/shard_map/all_gather | solution.py:198
  9.4 163.4 %all-gather.14.cloned.1.call-start = ((), (), s32[]{:S(2)}) async-start(), calls=%async_computation.5 | async-start | bytes 17301504 | tf_op jit(solution)/shard_map/all_gather | solution.py:21
  12.9 2.9 copy-start.3
  15.2 283.9 %all-gather.12.cloned.1.call-start = ((), (), s32[]{:S(2)}) async-start(), calls=%async_computation.3 | async-start | bytes 34603008 | tf_op jit(solution)/shard_map/all_gather | solution.py:259
  15.8 322.9 %reduce-scatter.2.cloned.1.call-start = ((), (), s32[]{:S(2)}) async-start(), calls=%async_computation.4 | async-start | bytes 1572864 | tf_op jit(solution)/shard_map/reduce_scatter | solution.py:262
  102.3 4.4 %copy-start.1 = (f32[1,16,128,128]{3,2,1,0:T(8,128)S(1)}, f32[1,16,128,128]{3,2,1,0:T(8,128)}, u32[]{:S(2)}) copy-start(f32[1,16,128,128]{3,2,1,0:T(8,128)} %get-tuple-element.240) | copy-start | bytes 3145732 | tf_op jit(solution)/shard_map/while/body/eval_jaxpr/cond
  110.3 1.0 copy-start.2
  114.2 4.4 %copy-start.1 = (f32[1,16,128,128]{3,2,1,0:T(8,128)S(1)}, f32[1,16,128,128]{3,2,1,0:T(8,128)}, u32[]{:S(2)}) copy-start(f32[1,16,128,128]{3,2,1,0:T(8,128)} %get-tuple-element.240) | copy-start | bytes 3145732 | tf_op jit(solution)/shard_map/while/body/eval_jaxpr/cond
  122.2 1.0 copy-start.2
  126.1 4.4 %copy-start.1 = (f32[1,16,128,128]{3,2,1,0:T(8,128)S(1)}, f32[1,16,128,128]{3,2,1,0:T(8,128)}, u32[]{:S(2)}) copy-start(f32[1,16,128,128]{3,2,1,0:T(8,128)} %get-tuple-element.240) | copy-start | bytes 3145732 | tf_op jit(solution)/shard_map/while/body/eval_jaxpr/cond
  134.1 1.0 copy-start.2
  138.0 4.4 %copy-start.1 = (f32[1,16,128,128]{3,2,1,0:T(8,128)S(1)}, f32[1,16,128,128]{3,2,1,0:T(8,128)}, u32[]{:S(2)}) copy-start(f32[1,16,128,128]{3,2,1,0:T(8,128)} %get-tuple-element.240) | copy-start | bytes 3145732 | tf_op jit(solution)/shard_map/while/body/eval_jaxpr/cond
  146.1 1.0 copy-start.2
  172.8 47.5 %dynamic-slice-start = ((f32[4096]{0:T(1024)}, s32[]{:T(128)}), f32[2048]{0:T(1024)S(1)}, s32[]{:S(2)}) async-start(f32[4096]{0:T(1024)} %param.27, s32[]{:T(128)} %select_n.88), calls=%async_computation.6 | async-start | bytes 16896 | tf_op jit(solution)/shard_map/dynamic_slice | solution.py:213
  222.1 15.9 %collective-permute-start = (bf16[128,2048]{1,0:T(8,128)(2,1)S(1)}, bf16[128,2048]{1,0:T(8,128)(2,1)S(1)}, u32[]{:S(2)}, u32[]{:S(2)}) collective-permute-start(bf16[128,2048]{1,0:T(8,128)(2,1)S(1)} %get-tuple-element.394), channel_id=1, source_target_pairs={{0,64},{64,0},{1,65},{65,1},{2,66},{66,2},{3,67},{67,3},{4,68},{68... | collective-permute-start | bytes 1572872 | tf_op jit(solution)/shard_map/ppermute | solution.py:44
  299.1 39.6 %copy-start.4 = (bf16[128,2048]{1,0:T(8,128)(2,1)S(1)}, bf16[128,2048]{1,0:T(8,128)(2,1)}, u32[]{:S(2)}) copy-start(bf16[128,2048]{1,0:T(8,128)(2,1)} %param.19) | copy-start | bytes 1572868
  339.9 16.9 %collective-permute-start.1 = (bf16[128,2048]{1,0:T(8,128)(2,1)S(1)}, bf16[128,2048]{1,0:T(8,128)(2,1)S(1)}, u32[]{:S(2)}, u32[]{:S(2)}) collective-permute-start(bf16[128,2048]{1,0:T(8,128)(2,1)S(1)} %fusion.52), channel_id=1, source_target_pairs={{0,64},{1,65},{2,66},{3,67},{4,68},{5,69},{6,70},{7,71},{8,72},{9,... | collective-permute-start | bytes 1572872 | tf_op jit(solution)/shard_map/ppermute | solution.py:50
Sparse Core Ops, SparseCore 0:
  9.6 44.3 all-gather.7
  56.3 41.9 all-gather.9
  100.6 72.2 all-gather.13
  174.9 124.1 all-gather.11
  315.4 23.2 reduce-scatter.1
where the time goes:
time: 369 us; the launch traced here: 365 us
  waiting for transfers between devices  190 us (51%)
  other arithmetic  62.3 us (17%)
  matrix products  49.1 us (13%)
  blocking collectives  22 us (6%)
  local copies, waits for them, and re-layouts  18.6 us (5%)
  between operations  13.3 us (4%)
  loops' own time  6.57 us (2%)
    all_gather x1, waiting for transfers between devices, per_device(): lax.all_gather(out_weights, 'ctx', axis=2, tiled=True)[0]  61.1 us
    all_gather x1, waiting for transfers between devices, attention(): value_piece = lax.all_gather(values, 'ctx', axis=0, tiled=True)  44.2 us
    select_n x32, other arithmetic, turn(): return jax.tree.map(lambda a, b: jnp.where(reached, a, b), new, before)  41.8 us
    reduce_scatter x1, waiting for transfers between devices, per_device(): lax.psum_scatter(partial_value.astype(jnp.bfloat16), 'tp', scatter_dimens...  23.4 us
    all_gather x1, waiting for transfers between devices, entering_2(): lax.all_gather(part.astype(kind), axis)  23 us
    all_gather x1, blocking collectives, entering_2(): lax.all_gather(part.astype(kind), axis)  22 us
    dot_general x1, matrix products, per_device(): jnp.dot(mixed_rows, lax.all_gather(out_weights, 'ctx', axis=2, tiled=True...  16.1 us
    ppermute x1, waiting for transfers between devices, shifted(): return lax.ppermute(x, axis, pairs)  15.6 us
  transfers between devices with their start and end apart: 7, of which 7 were waited for; matrix products, arithmetic and copies ran while one was open for 29% of the time, Pallas kernels for 0%

commit v1 on v0

--- a/solution.py
+++ b/solution.py
@@ -32,6 +32,47 @@
         return jax.tree.map(lambda a, b: jnp.where(reached, a, b), new, before)
 
     return lax.fori_loop(0, peers, turn, start)
+
+
+CTX = ("y", "zc")
+
+
+def gathered(x, axis):
+    peers = lax.axis_size(axis)
+    spread = jnp.broadcast_to(x[None], (peers,) + x.shape)
+    return lax.all_to_all(spread, axis, 0, 0)
+
+
+def entering_states(through_log, local_state):
+    outer = lax.axis_size("y")
+    inner = lax.axis_size("zc")
+    peers = outer * inner
+    rank = lax.axis_index("y") * inner + lax.axis_index("zc")
+    logs = gathered(through_log, CTX)
+    logs = logs.reshape((peers,) + through_log.shape)
+    places = jnp.arange(peers, dtype=jnp.int32)
+
+    def span_weight(k, upto):
+        inside = (places[None, :] > k[:, None]) & (places[None, :] < upto)
+        summed = jnp.sum(jnp.where(inside[:, :, None, None], logs[None], 0.0), axis=1)
+        return jnp.where((k < upto)[:, None, None], jnp.exp(summed), 0.0)
+
+    first = lax.axis_index("y") * inner
+    near = gathered(local_state.astype(jnp.bfloat16), "zc").astype(jnp.float32)
+    near_ids = first + jnp.arange(inner, dtype=jnp.int32)
+    own_part = jnp.einsum(
+        "kgj,kgjpn->gjpn", span_weight(near_ids, rank), near, precision=exact_mode
+    )
+    group_end = first + inner
+    group_total = jnp.einsum(
+        "kgj,kgjpn->gjpn", span_weight(near_ids, group_end), near, precision=exact_mode
+    )
+    far = gathered(group_total.astype(jnp.bfloat16), "y").astype(jnp.float32)
+    far_ends = (jnp.arange(outer, dtype=jnp.int32) + 1) * inner - 1
+    far_weight = span_weight(far_ends, rank)
+    far_weight = jnp.where((far_ends < first)[:, None, None], far_weight, 0.0)
+    far_part = jnp.einsum("kgj,kgjpn->gjpn", far_weight, far, precision=exact_mode)
+    return own_part + far_part
 
 
 def from_partner(block, axis, distance):
@@ -130,14 +171,7 @@
         ),
     )
     running = jnp.cumsum(log_decay, axis=0)
-    through = jnp.exp(running[-1]).reshape(groups, per_group)
-    prior = entering_2(
-        (through, local_state),
-        "ctx",
-        join_states,
-        (jnp.ones_like(through), jnp.zeros_like(local_state)),
-    )
-    entering = prior[1]
+    entering = entering_states(running[-1].reshape(groups, per_group), local_state)
     output_all = ssm_out_c.astype(jnp.float32).reshape(rows_here, groups, STATE)
     carried = (
         jnp.einsum("tgn,gjpn->tgjp", output_all, entering, precision=exact_mode)
@@ -194,8 +228,10 @@
         jnp.zeros((kv_count, per_key, rows_here, HEAD_DIM), jnp.float32),
     )
     running = start_state
-    key_piece = lax.all_gather(keys, "ctx", axis=0, tiled=True)
-    value_piece = lax.all_gather(values, "ctx", axis=0, tiled=True)
+    both = gathered(jnp.concatenate([keys, values], axis=1), CTX)
+    both = both.reshape(-1, both.shape[-1])
+    key_piece = both[:, : keys.shape[1]]
+    value_piece = both[:, keys.shape[1] :]
     count = key_piece.shape[0]
     width = math.gcd(count, 1024)
     blocks = count // width
@@ -229,7 +265,7 @@
     out_weights,
 ):
     section = lax.axis_index("pipe")
-    ctx_rank = lax.axis_index("ctx")
+    ctx_rank = lax.axis_index("y") * lax.axis_size("zc") + lax.axis_index("zc")
     mamba_part = mamba_mixer(
         take_half(ssm_input, 1, section),
         take_half(ssm_gate, 1, section),
@@ -256,12 +292,14 @@
     )
     partial_value = jnp.dot(
         mixed_rows,
-        lax.all_gather(out_weights, "ctx", axis=2, tiled=True)[0],
+        lax.all_gather(out_weights, CTX, axis=2, tiled=True)[0],
         preferred_element_type=jnp.float32,
     )
-    projected = lax.psum_scatter(
-        partial_value.astype(jnp.bfloat16), "tp", scatter_dimension=1, tiled=True
-    ).astype(jnp.float32)
+    half = partial_value.shape[1] // 2
+    tp_rank = lax.axis_index("tp")
+    kept = jnp.where(tp_rank == 0, partial_value[:, :half], partial_value[:, half:])
+    sent = jnp.where(tp_rank == 0, partial_value[:, half:], partial_value[:, :half])
+    projected = kept + from_partner(sent.astype(jnp.bfloat16), "tp", 0).astype(jnp.float32)
     own_section = (resid_in.astype(jnp.float32) + projected).astype(jnp.bfloat16)
     received = shifted(own_section, "pipe", 1)
     second_section = (received.astype(jnp.float32) + projected).astype(jnp.bfloat16)
@@ -269,24 +307,29 @@
 
 
 def solution(mesh):
+    pipe, ctx, tp = (mesh.shape[name] for name in ("pipe", "ctx", "tp"))
+    outer = 4 if ctx % 4 == 0 else 1
+    split = jax.sharding.Mesh(
+        mesh.devices.reshape(pipe, outer, ctx // outer, tp), ("pipe", "y", "zc", "tp")
+    )
     return jax.shard_map(
         per_device,
-        mesh=mesh,
+        mesh=split,
         in_specs=(
-            P("ctx", "tp"),
-            P("ctx", "tp"),
-            P("ctx", "tp"),
-            P("ctx", "tp"),
-            P("ctx", "tp"),
-            P("ctx", "tp"),
+            P(CTX, "tp"),
+            P(CTX, "tp"),
+            P(CTX, "tp"),
+            P(CTX, "tp"),
+            P(CTX, "tp"),
+            P(CTX, "tp"),
             P("tp"),
             P("tp"),
             P("tp"),
-            P("ctx", "tp"),
-            P("ctx", "tp"),
-            P("ctx", "tp"),
-            P("pipe", "tp", "ctx"),
+            P(CTX, "tp"),
+            P(CTX, "tp"),
+            P(CTX, "tp"),
+            P("pipe", "tp", CTX),
         ),
-        out_specs=P("pipe", "ctx", "tp"),
+        out_specs=P("pipe", CTX, "tp"),
         check_vma=False,
     )

time: 369 us -> 295 us (0.80)
  other arithmetic: 62.3 us -> 17.4 us
  waiting for transfers between devices: 190 us -> 146 us
  starting transfers between devices: 3.24 us -> 31.2 us
  blocking collectives: 22 us -> 0 us
  matrix products: 49.1 us -> 62 us
    all_gather x4 -> x1, waiting for transfers between devices: 136 us -> 0.01 us  [per_device(): lax.all_gather(out_weights, CTX, axis=2, tiled=True)[0]]
    all_to_all x0 -> x4, waiting for transfers between devices: none -> 108 us  [gathered(): return lax.all_to_all(spread, axis, 0, 0)]
    select_n x32 -> x3, other arithmetic: 41.8 us -> 0.21 us  [the longest x2 0.13 us: span_weight(): return jnp.where((k < upto)[:, None, None], jnp.exp(summed), 0.0)]
    all_to_all x0 -> x4, starting transfers between devices: none -> 27.7 us  [gathered(): return lax.all_to_all(spread, axis, 0, 0)]
    reduce_scatter x1 -> x0, waiting for transfers between devices: 23.4 us -> none  [per_device(): lax.psum_scatter(partial_value.astype(jnp.bfloat16), 'tp', scatter_dimens...]
    all_gather x1 -> x0, blocking collectives: 22 us -> none  [entering_2(): lax.all_gather(part.astype(kind), axis)]
    dot_general x1 -> x4, matrix products: 16.1 us -> 33.1 us  [the longest x1 13 us: per_device(): jnp.dot(mixed_rows, lax.all_gather(out_weights, CTX, axis=2, tiled=True)[...]
    ppermute x1 -> x2, waiting for transfers between devices: 14.1 us -> 24.3 us  [from_partner(): return lax.ppermute(block, axis, route)]
  transfers between devices with their start and end apart: 7 -> 8, of which waited for: 7 -> 6; matrix products, arithmetic and copies ran while one was open for 29% -> 28% of each run, Pallas kernels for 0% -> 0%
where the time goes in v1:
time: 295 us; the launch traced here: 293 us
  waiting for transfers between devices  146 us (49%)
  matrix products  62 us (21%)
  starting transfers between devices  31.2 us (11%)
  local copies, waits for them, and re-layouts  17.8 us (6%)
  other arithmetic  17.4 us (6%)
  between operations  13.8 us (5%)
  loops' own time  5.2 us (2%)
    all_to_all x4, waiting for transfers between devices, gathered(): return lax.all_to_all(spread, axis, 0, 0)  108 us
    all_to_all x4, starting transfers between devices, gathered(): return lax.all_to_all(spread, axis, 0, 0)  27.7 us
    ppermute x2, waiting for transfers between devices, from_partner(): return lax.ppermute(block, axis, route)  24.3 us
    dot_general x4, matrix products, absorb(): jnp.einsum('gjqk,kgd->gjqd', weights_exp.astype(jnp.bfloat16), value_rows...  14.4 us
    ppermute x1, waiting for transfers between devices, shifted(): return lax.ppermute(x, axis, pairs)  13.2 us
    dot_general x1, matrix products, per_device(): jnp.dot(mixed_rows, lax.all_gather(out_weights, CTX, axis=2, tiled=True)[...  13 us
    dot_general x4, matrix products, absorb(): jnp.einsum('qgjd,kgd->gjqk', query_groups, key_rows, preferred_element_ty...  9.04 us
    reduce_sum x4, other arithmetic, absorb(): row_sum = row_sum * rescale + jnp.sum(weights_exp, axis=-1)  8.01 us
  transfers between devices with their start and end apart: 8, of which 6 were waited for; matrix products, arithmetic and copies ran while one was open for 28% of the time, Pallas kernels for 0%

profile of v1, /device:TPU:30, one launch (start us, length us, event | category | flops | bytes accessed | tf_op | source)
XLA Modules:
  0.0 293.2 jit_solution(3043856634190309302)
XLA Ops:
  6.5 0.7 all-gather.2.cloned.1.call-update
  7.3 0.7 constant_dynamic-slice_fusion.3
  8.1 0.7 dynamic_slice.71
  9.0 0.6 broadcast_in_dim.214
  9.6 8.4 %all-to-all-start = ((f32[32,1,32]{2,1,0:T(1,128)}), f32[32,1,32]{2,1,0:T(1,128)S(1)}, u32[]{:S(2)}, u32[]{:S(2)}) async-start(f32[32,1,32]{2,1,0:T(1,128)} %broadcast_in_dim.214), calls=%async_computation | async-start | bytes 32768 | tf_op jit(solution)/shard_map/all_to_all | solution.py:43
  18.1 1.3 constant_dynamic-slice_fusion
  19.7 0.7 fusion.49
  20.3 3.1 %all-to-all-done = f32[32,1,32]{2,1,0:T(1,128)S(1)} async-done(((f32[32,1,32]{2,1,0:T(1,128)}), f32[32,1,32]{2,1,0:T(1,128)S(1)}, u32[]{:S(2)}, u32[]{:S(2)}) %all-to-all-start) | async-done | bytes 4128 | tf_op jit(solution)/shard_map/all_to_all | solution.py:43
  23.4 3.0 %broadcast_in_dim.220 = bf16[8,1,32,64,128]{4,3,2,1,0:T(8,128)(2,1)} broadcast(bf16[32,64,128]{2,1,0:T(8,128)(2,1)S(1)} %fusion.49), dimensions={2,3,4} | broadcast | bytes 4718592 | tf_op jit(solution)/shard_map/broadcast_in_dim | solution.py:42
  26.5 4.7 %all-to-all-start.1 = ((bf16[8,1,32,64,128]{4,3,2,1,0:T(8,128)(2,1)}), bf16[8,1,32,64,128]{4,3,2,1,0:T(8,128)(2,1)}, u32[]{:S(2)}, u32[]{:S(2)}) async-start(bf16[8,1,32,64,128]{4,3,2,1,0:T(8,128)(2,1)} %broadcast_in_dim.220), calls=%async_computation.1 | async-start | bytes 8388608 | tf_op jit(solution)/shard_map/all_to_all | solution.py:43
  31.2 1.2 copy.70
  33.2 0.6 slice.24
  34.1 68.9 %all-to-all-done.1 = bf16[8,1,32,64,128]{4,3,2,1,0:T(8,128)(2,1)} async-done(((bf16[8,1,32,64,128]{4,3,2,1,0:T(8,128)(2,1)}), bf16[8,1,32,64,128]{4,3,2,1,0:T(8,128)(2,1)}, u32[]{:S(2)}, u32[]{:S(2)}) %all-to-all-start.1) | async-done | bytes 4194336 | tf_op jit(solution)/shard_map/all_to_all | solution.py:43
  103.0 1.5 broadcast_in_dim.233
  104.5 8.1 %all-to-all-start.3 = ((bf16[32,128,256]{2,1,0:T(8,128)(2,1)}), bf16[32,128,256]{2,1,0:T(8,128)(2,1)S(1)}, u32[]{:S(2)}, u32[]{:S(2)}) async-start(bf16[32,128,256]{2,1,0:T(8,128)(2,1)} %broadcast_in_dim.233), calls=%async_computation.3 | async-start | bytes 4194304 | tf_op jit(solution)/shard_map/all_to_all | solution.py:43
  112.7 3.4 %fusion.41 = f32[128,1,32,64]{0,3,2,1:T(8,128)} fusion(bf16[128,32,64]{0,2,1:T(8,128)(2,1)S(1)} %bitcast.161, f32[32,128]{1,0:T(8,128)S(1)} %fusion.99, f32[128,32]{0,1:T(8,128)S(1)} %copy.65, f32[128,128]{1,0:T(8,128)S(1)} %fusion.78, pred[128,128]{1,0:T(8,128)(4,1)S(1)} %iota_compare_fusion), kind=kOutput, calls=%fused_computation.44 | convolution fusion | flops 404750336 | bytes 1687552 | tf_op jit(solution)/shard_map/while/body/eval_jaxpr/gjts,sgjp->tgjp/dot_general | solution.py:108
  116.9 7.3 %fusion.29 = f32[32,1,64,128]{3,1,2,0:T(1,128)S(1)} fusion(f32[8,32,1,1]{0,2,3,1:T(1,128)S(1)} %copy.79, bf16[8,32,64,128]{3,2,1,0:T(8,128)(2,1)} %bitcast.28), kind=kOutput, calls=%fused_computation.31 | convolution fusion | flops 25165824 | bytes 5243904 | tf_op jit(solution)/shard_map/kgj,kgjpn->gjpn/dot_general | solution.py:67
  124.4 35.6 %all-to-all-done.3 = bf16[32,128,256]{2,1,0:T(8,128)(2,1)S(1)} async-done(((bf16[32,128,256]{2,1,0:T(8,128)(2,1)}), bf16[32,128,256]{2,1,0:T(8,128)(2,1)S(1)}, u32[]{:S(2)}, u32[]{:S(2)}) %all-to-all-start.3) | async-done | bytes 2097184 | tf_op jit(solution)/shard_map/all_to_all | solution.py:43
  160.0 1.9 broadcast_in_dim.229
  161.9 6.5 %all-to-all-start.2 = ((bf16[4,1,32,64,128]{4,3,2,1,0:T(8,128)(2,1)}), bf16[4,1,32,64,128]{4,3,2,1,0:T(8,128)(2,1)}, u32[]{:S(2)}, u32[]{:S(2)}) async-start(bf16[4,1,32,64,128]{4,3,2,1,0:T(8,128)(2,1)} %broadcast_in_dim.229), calls=%async_computation.2 | async-start | bytes 4194304 | tf_op jit(solution)/shard_map/all_to_all | solution.py:43
  168.4 1.4 fusion.93
  170.0 42.1 %while.4 = (s32[]{:T(128)}, f32[1,16,128]{2,1,0:T(8,128)S(1)}, f32[1,16,128]{2,1,0:T(8,128)S(1)}, f32[1,16,128,128]{3,2,1,0:T(8,128)S(1)}, s32[4]{0:T(128)S(1)},...) while((s32[]{:T(128)}, f32[1,16,128]{2,1,0:T(8,128)S(1)}, ...), condition=%wide.region_10.11_spmd.clone, body=%wide.region_5.10_spmd.clone.sunk | while | flops 1101667456 | bytes 28978456 | solution.py:241
  170.0 0.6 dynamic_slice.120
  171.8 8.7 %conditional.3 = ((f32[1,16,128]{2,1,0:T(8,128)S(1)}, f32[1,16,128]{2,1,0:T(8,128)S(1)}, f32[1,16,128,128]{3,2,1,0:T(8,128)S(1)})) conditional(s32[]{:T(128)} %convert_element_type.127, (f32[1,16,128]{2,1,0:T(8,128)S(1)}, f32[1,16,128]{2,1,0:T(8,128)S(1)}, f32[1,16,128,128]{3,2,1,0:T(8,128)S(1)}) %tuple.53, (s32[]{:T(128)}, s32[]{:T(128)}, ...), branch_computations={%region_6.6_spmd, %region_7.9_spmd} | conditional | flops 1101667456 | bytes 28977704 | solution.py:223
  171.8 0.6 iota_add_fusion
  172.6 2.3 fusion.2
  174.9 2.0 fusion.4
  176.9 3.6 %fusion.12 = f32[1,16,128,128]{3,2,1,0:T(8,128)S(1)} fusion(f32[1024,128,16]{1,0,2:T(8,128)S(1)} %get-tuple-element.261, f32[16,128]{1,0:T(8,128)S(1)} %bitcast.158, pred[128,1024]{0,1:T(8,128)(4,1)S(1)} %broadcast_compare_fusion, f32[1,16,128,128]{3,2,1,0:T(8,128)S(1)} %get-tuple-element.147, f32[16,128]{1,0:T(8,128)S(1)} %get-tuple-element.258, ...), kind=kOutput, calls=%fused_computation.10 | convolution fusion | flops 547880960 | bytes 10895872 | tf_op jit(solution)/shard_map/while/body/eval_jaxpr/cond/branch_1_fun/gjqk,kgd->gjqd/dot_general | solution.py:215
  180.5 0.6 dynamic_slice.120
  182.3 8.7 %conditional.3 = ((f32[1,16,128]{2,1,0:T(8,128)S(1)}, f32[1,16,128]{2,1,0:T(8,128)S(1)}, f32[1,16,128,128]{3,2,1,0:T(8,128)S(1)})) conditional(s32[]{:T(128)} %convert_element_type.127, (f32[1,16,128]{2,1,0:T(8,128)S(1)}, f32[1,16,128]{2,1,0:T(8,128)S(1)}, f32[1,16,128,128]{3,2,1,0:T(8,128)S(1)}) %tuple.53, (s32[]{:T(128)}, s32[]{:T(128)}, ...), branch_computations={%region_6.6_spmd, %region_7.9_spmd} | conditional | flops 1101667456 | bytes 28977704 | solution.py:223
  182.3 0.6 iota_add_fusion
  183.1 2.3 fusion.2
  185.4 2.0 fusion.4
  187.4 3.6 %fusion.12 = f32[1,16,128,128]{3,2,1,0:T(8,128)S(1)} fusion(f32[1024,128,16]{1,0,2:T(8,128)S(1)} %get-tuple-element.261, f32[16,128]{1,0:T(8,128)S(1)} %bitcast.158, pred[128,1024]{0,1:T(8,128)(4,1)S(1)} %broadcast_compare_fusion, f32[1,16,128,128]{3,2,1,0:T(8,128)S(1)} %get-tuple-element.147, f32[16,128]{1,0:T(8,128)S(1)} %get-tuple-element.258, ...), kind=kOutput, calls=%fused_computation.10 | convolution fusion | flops 547880960 | bytes 10895872 | tf_op jit(solution)/shard_map/while/body/eval_jaxpr/cond/branch_1_fun/gjqk,kgd->gjqd/dot_general | solution.py:215
  191.1 0.6 dynamic_slice.120
  192.9 8.7 %conditional.3 = ((f32[1,16,128]{2,1,0:T(8,128)S(1)}, f32[1,16,128]{2,1,0:T(8,128)S(1)}, f32[1,16,128,128]{3,2,1,0:T(8,128)S(1)})) conditional(s32[]{:T(128)} %convert_element_type.127, (f32[1,16,128]{2,1,0:T(8,128)S(1)}, f32[1,16,128]{2,1,0:T(8,128)S(1)}, f32[1,16,128,128]{3,2,1,0:T(8,128)S(1)}) %tuple.53, (s32[]{:T(128)}, s32[]{:T(128)}, ...), branch_computations={%region_6.6_spmd, %region_7.9_spmd} | conditional | flops 1101667456 | bytes 28977704 | solution.py:223
  192.9 0.6 iota_add_fusion
  193.7 2.3 fusion.2
  195.9 2.0 fusion.4
  198.0 3.6 %fusion.12 = f32[1,16,128,128]{3,2,1,0:T(8,128)S(1)} fusion(f32[1024,128,16]{1,0,2:T(8,128)S(1)} %get-tuple-element.261, f32[16,128]{1,0:T(8,128)S(1)} %bitcast.158, pred[128,1024]{0,1:T(8,128)(4,1)S(1)} %broadcast_compare_fusion, f32[1,16,128,128]{3,2,1,0:T(8,128)S(1)} %get-tuple-element.147, f32[16,128]{1,0:T(8,128)S(1)} %get-tuple-element.258, ...), kind=kOutput, calls=%fused_computation.10 | convolution fusion | flops 547880960 | bytes 10895872 | tf_op jit(solution)/shard_map/while/body/eval_jaxpr/cond/branch_1_fun/gjqk,kgd->gjqd/dot_general | solution.py:215
  201.6 0.6 dynamic_slice.120
  203.4 8.7 %conditional.3 = ((f32[1,16,128]{2,1,0:T(8,128)S(1)}, f32[1,16,128]{2,1,0:T(8,128)S(1)}, f32[1,16,128,128]{3,2,1,0:T(8,128)S(1)})) conditional(s32[]{:T(128)} %convert_element_type.127, (f32[1,16,128]{2,1,0:T(8,128)S(1)}, f32[1,16,128]{2,1,0:T(8,128)S(1)}, f32[1,16,128,128]{3,2,1,0:T(8,128)S(1)}) %tuple.53, (s32[]{:T(128)}, s32[]{:T(128)}, ...), branch_computations={%region_6.6_spmd, %region_7.9_spmd} | conditional | flops 1101667456 | bytes 28977704 | solution.py:223
  203.4 0.6 iota_add_fusion
  204.2 2.3 fusion.2
  206.5 2.0 fusion.4
  208.5 3.6 %fusion.12 = f32[1,16,128,128]{3,2,1,0:T(8,128)S(1)} fusion(f32[1024,128,16]{1,0,2:T(8,128)S(1)} %get-tuple-element.261, f32[16,128]{1,0:T(8,128)S(1)} %bitcast.158, pred[128,1024]{0,1:T(8,128)(4,1)S(1)} %broadcast_compare_fusion, f32[1,16,128,128]{3,2,1,0:T(8,128)S(1)} %get-tuple-element.147, f32[16,128]{1,0:T(8,128)S(1)} %get-tuple-element.258, ...), kind=kOutput, calls=%fused_computation.10 | convolution fusion | flops 547880960 | bytes 10895872 | tf_op jit(solution)/shard_map/while/body/eval_jaxpr/cond/branch_1_fun/gjqk,kgd->gjqd/dot_general | solution.py:215
  212.1 0.3 fusion.73
  212.5 0.3 copy.74
  212.8 7.1 %fusion.31 = f32[32,1,64,128]{3,1,2,0:T(1,128)S(1)} fusion(f32[8,32,1,1]{0,2,3,1:T(1,128)S(1)} %copy.76, bf16[8,32,64,128]{3,2,1,0:T(8,128)(2,1)} %bitcast.28), kind=kOutput, calls=%fused_computation.33 | convolution fusion | flops 25165824 | bytes 5243904 | tf_op jit(solution)/shard_map/kgj,kgjpn->gjpn/dot_general | solution.py:63
  220.0 5.6 %fusion.39 = f32[32,1,64,128]{3,1,2,0:T(1,128)S(1)} fusion(f32[4,32,1,1]{0,2,3,1:T(1,128)S(1)} %copy.81, bf16[4,32,64,128]{3,2,1,0:T(8,128)(2,1)} %bitcast.35), kind=kOutput, calls=%fused_computation.42 | convolution fusion | flops 12582912 | bytes 3146240 | tf_op jit(solution)/shard_map/kgj,kgjpn->gjpn/dot_general | solution.py:74
  225.7 0.7 fusion.48
  226.4 0.6 fusion.47
  227.0 0.3 copy.71
  227.3 1.5 multiply_reduce_fusion
  228.9 1.8 bitcast_select_fusion.2
  230.7 1.4 collective-permute-start
  232.1 13.1 %collective-permute-done = bf16[128,2048]{1,0:T(8,128)(2,1)S(1)} collective-permute-done((bf16[128,2048]{1,0:T(8,128)(2,1)S(1)}, bf16[128,2048]{1,0:T(8,128)(2,1)S(1)}, u32[]{:S(2)}, u32[]{:S(2)}) %collective-permute-start) | collective-permute-done | bytes 524320 | tf_op jit(solution)/shard_map/ppermute | solution.py:85
  245.2 13.0 %fusion.27 = f32[128,4096]{1,0:T(8,128)S(1)} fusion(bf16[1,4096,4096]{2,1,0:T(8,128)(2,1)} %all-gather.2.cloned.1.call-done, bf16[128,2048]{1,0:T(8,128)(2,1)S(1)} %collective-permute-done, bf16[128,2048]{1,0:T(8,128)(2,1)S(1)} %get-tuple-element.262, pred[]{:T(512)S(6)} %eq.4), kind=kOutput, calls=%fused_computation.29 | convolution fusion | flops 4299685888 | bytes 36700160 | tf_op jit(solution)/shard_map/dot_general | solution.py:293
  258.2 0.8 collective-permute-start.1
  259.0 11.3 %collective-permute-done.1 = bf16[128,2048]{1,0:T(8,128)(2,1)S(1)} collective-permute-done((bf16[128,2048]{1,0:T(8,128)(2,1)S(1)}, bf16[128,2048]{1,0:T(8,128)(2,1)S(1)}, u32[]{:S(2)}, u32[]{:S(2)}) %collective-permute-start.1) | collective-permute-done | bytes 524320 | tf_op jit(solution)/shard_map/ppermute | solution.py:85
  270.3 0.3 add_convert_fusion.1
  270.6 1.3 collective-permute-start.2
  271.9 13.2 %collective-permute-done.2 = bf16[128,2048]{1,0:T(8,128)(2,1)S(1)} collective-permute-done((bf16[128,2048]{1,0:T(8,128)(2,1)S(1)}, bf16[128,2048]{1,0:T(8,128)(2,1)S(1)}, u32[]{:S(2)}, u32[]{:S(2)}) %collective-permute-start.2) | collective-permute-done | bytes 524320 | tf_op jit(solution)/shard_map/ppermute | solution.py:91
  285.2 1.2 fusion.70
  (89 shorter events, 3.8 us)
Async XLA Ops:
  6.5 27.3 %copy-start = (bf16[128,256]{1,0:T(8,128)(2,1)S(1)}, bf16[128,256]{1,0:T(8,128)(2,1)}, u32[]{:S(2)}) copy-start(bf16[128,256]{1,0:T(8,128)(2,1)} %param.21) | copy-start | bytes 196612
  6.5 13.1 %copy-start.4 = (bf16[128,256]{1,0:T(8,128)(2,1)S(1)}, bf16[128,256]{1,0:T(8,128)(2,1)}, u32[]{:S(2)}) copy-start(bf16[128,256]{1,0:T(8,128)(2,1)} %param.20) | copy-start | bytes 196612
  6.5 238.6 %all-gather.2.cloned.1.call-start = ((), (), s32[]{:S(2)}) async-start(), calls=%async_computation.4 | async-start | bytes 34603008 | tf_op jit(solution)/shard_map/all_gather | solution.py:295
  9.6 13.8 %all-to-all-start = ((f32[32,1,32]{2,1,0:T(1,128)}), f32[32,1,32]{2,1,0:T(1,128)S(1)}, u32[]{:S(2)}, u32[]{:S(2)}) async-start(f32[32,1,32]{2,1,0:T(1,128)} %broadcast_in_dim.214), calls=%async_computation | async-start | bytes 32768 | tf_op jit(solution)/shard_map/all_to_all | solution.py:43
  26.5 6.0 %copy-start.8 = (f32[64]{0:T(128)S(1)}, f32[64]{0:T(128)}, u32[]{:S(2)}) copy-start(f32[64]{0:T(128)} %param.24) | copy-start | bytes 772
  26.5 7.4 %copy-start.5 = (f32[128,64]{0,1:T(8,128)S(1)}, f32[128,64]{0,1:T(8,128)}, u32[]{:S(2)}) copy-start(f32[128,64]{0,1:T(8,128)} %param.22) | copy-start | bytes 98308
  26.5 7.5 %copy-start.6 = (bf16[128,256]{1,0:T(8,128)(2,1)S(1)}, bf16[128,256]{1,0:T(8,128)(2,1)}, u32[]{:S(2)}) copy-start(bf16[128,256]{1,0:T(8,128)(2,1)} %param.28) | copy-start | bytes 196612
  26.5 7.6 %copy-start.7 = (bf16[128,256]{1,0:T(8,128)(2,1)S(1)}, bf16[128,256]{1,0:T(8,128)(2,1)}, u32[]{:S(2)}) copy-start(bf16[128,256]{1,0:T(8,128)(2,1)} %param.27) | copy-start | bytes 196612
  26.5 76.5 %all-to-all-start.1 = ((bf16[8,1,32,64,128]{4,3,2,1,0:T(8,128)(2,1)}), bf16[8,1,32,64,128]{4,3,2,1,0:T(8,128)(2,1)}, u32[]{:S(2)}, u32[]{:S(2)}) async-start(bf16[8,1,32,64,128]{4,3,2,1,0:T(8,128)(2,1)} %broadcast_in_dim.220), calls=%async_computation.1 | async-start | bytes 8388608 | tf_op jit(solution)/shard_map/all_to_all | solution.py:43
  104.5 55.4 %all-to-all-start.3 = ((bf16[32,128,256]{2,1,0:T(8,128)(2,1)}), bf16[32,128,256]{2,1,0:T(8,128)(2,1)S(1)}, u32[]{:S(2)}, u32[]{:S(2)}) async-start(bf16[32,128,256]{2,1,0:T(8,128)(2,1)} %broadcast_in_dim.233), calls=%async_computation.3 | async-start | bytes 4194304 | tf_op jit(solution)/shard_map/all_to_all | solution.py:43
  161.9 58.1 %all-to-all-start.2 = ((bf16[4,1,32,64,128]{4,3,2,1,0:T(8,128)(2,1)}), bf16[4,1,32,64,128]{4,3,2,1,0:T(8,128)(2,1)}, u32[]{:S(2)}, u32[]{:S(2)}) async-start(bf16[4,1,32,64,128]{4,3,2,1,0:T(8,128)(2,1)} %broadcast_in_dim.229), calls=%async_computation.2 | async-start | bytes 4194304 | tf_op jit(solution)/shard_map/all_to_all | solution.py:43
  220.0 6.4 %copy-start.1 = (f32[128,2048]{0,1:T(8,128)S(1)}, f32[128,2048]{0,1:T(8,128)}, u32[]{:S(2)}) copy-start(f32[128,2048]{0,1:T(8,128)} %copy.70) | copy-start | bytes 3145732
  220.0 6.4 %copy-start.2 = (f32[128,1,32,64]{0,3,2,1:T(8,128)S(1)}, f32[128,1,32,64]{0,3,2,1:T(8,128)}, u32[]{:S(2)}) copy-start(f32[128,1,32,64]{0,3,2,1:T(8,128)} %fusion.41) | copy-start | bytes 3145732
  226.3 2.5 dynamic-slice-start
  230.7 14.4 %collective-permute-start = (bf16[128,2048]{1,0:T(8,128)(2,1)S(1)}, bf16[128,2048]{1,0:T(8,128)(2,1)S(1)}, u32[]{:S(2)}, u32[]{:S(2)}) collective-permute-start(bf16[128,2048]{1,0:T(8,128)(2,1)S(1)} %get-tuple-element.263), channel_id=1, source_target_pairs={{0,64},{64,0},{1,65},{65,1},{2,66},{66,2},{3,67},{67,3},{4,68},{68... | collective-permute-start | bytes 1572872 | tf_op jit(solution)/shard_map/ppermute | solution.py:85
  245.2 25.2 %copy-start.3 = (bf16[128,2048]{1,0:T(8,128)(2,1)S(1)}, bf16[128,2048]{1,0:T(8,128)(2,1)}, u32[]{:S(2)}) copy-start(bf16[128,2048]{1,0:T(8,128)(2,1)} %param.17) | copy-start | bytes 1572868
  258.2 12.1 %collective-permute-start.1 = (bf16[128,2048]{1,0:T(8,128)(2,1)S(1)}, bf16[128,2048]{1,0:T(8,128)(2,1)S(1)}, u32[]{:S(2)}, u32[]{:S(2)}) collective-permute-start(bf16[128,2048]{1,0:T(8,128)(2,1)S(1)} %select_convert_fusion), channel_id=1, source_target_pairs={{0,1},{1,0},{2,3},{3,2},{4,5},{5,4},{6,7},{7,6},{8,9},{9,8},{10,11... | collective-permute-start | bytes 1572872 | tf_op jit(solution)/shard_map/ppermute | solution.py:85
  270.6 14.5 %collective-permute-start.2 = (bf16[128,2048]{1,0:T(8,128)(2,1)S(1)}, bf16[128,2048]{1,0:T(8,128)(2,1)S(1)}, u32[]{:S(2)}, u32[]{:S(2)}) collective-permute-start(bf16[128,2048]{1,0:T(8,128)(2,1)S(1)} %add_convert_fusion.1), channel_id=1, source_target_pairs={{0,64},{1,65},{2,66},{3,67},{4,68},{5,69},{6,70},{7,71},{8,72},{9,... | collective-permute-start | bytes 1572872 | tf_op jit(solution)/shard_map/ppermute | solution.py:91
Sparse Core Ops, SparseCore 0:
  9.5 201.1 all-gather.1

commit v2 on v1

--- a/solution.py
+++ b/solution.py
@@ -290,16 +290,20 @@
         jnp.concatenate([kept_half, incoming], axis=1),
         jnp.concatenate([incoming, kept_half], axis=1),
     )
-    partial_value = jnp.dot(
-        mixed_rows,
-        lax.all_gather(out_weights, CTX, axis=2, tiled=True)[0],
-        preferred_element_type=jnp.float32,
+    inner = lax.axis_size("zc")
+    tp_rank = lax.axis_index("tp")
+    rows = gathered(mixed_rows, "zc").reshape(-1, mixed_rows.shape[1])
+    columns = lax.all_gather(out_weights[0], "y", axis=0)
+    partial_value = jnp.einsum(
+        "tc,ycr->tyr", rows, columns, preferred_element_type=jnp.float32
     )
     half = partial_value.shape[1] // 2
-    tp_rank = lax.axis_index("tp")
     kept = jnp.where(tp_rank == 0, partial_value[:, :half], partial_value[:, half:])
     sent = jnp.where(tp_rank == 0, partial_value[:, half:], partial_value[:, :half])
-    projected = kept + from_partner(sent.astype(jnp.bfloat16), "tp", 0).astype(jnp.float32)
+    summed = kept + from_partner(sent.astype(jnp.bfloat16), "tp", 0).astype(jnp.float32)
+    pieces = summed.reshape((inner, -1) + summed.shape[1:]).astype(jnp.bfloat16)
+    pieces = lax.all_to_all(pieces, "zc", 0, 0)
+    projected = pieces.transpose(1, 2, 0, 3).reshape(pieces.shape[1], -1).astype(jnp.float32)
     own_section = (resid_in.astype(jnp.float32) + projected).astype(jnp.bfloat16)
     received = shifted(own_section, "pipe", 1)
     second_section = (received.astype(jnp.float32) + projected).astype(jnp.bfloat16)

time: 295 us -> 366 us (1.24)
  waiting for transfers between devices: 146 us -> 209 us
  local copies, waits for them, and re-layouts: 17.8 us -> 25.9 us
  starting transfers between devices: 31.2 us -> 38.3 us
  matrix products: 62 us -> 57.7 us
    all_gather x1, waiting for transfers between devices: 0.01 us -> 49.6 us  [per_device(): columns = lax.all_gather(out_weights[0], 'y', axis=0)]
    all_to_all x0 -> x1, waiting for transfers between devices: none -> 9.95 us  [per_device(): pieces = lax.all_to_all(pieces, 'zc', 0, 0)]
    dot_general x1, matrix products: 13 us -> 8.15 us  [per_device(): jnp.einsum('tc,ycr->tyr', rows, columns, preferred_element_type=jnp.float32)]
    broadcast_in_dim x5 -> x6, local copies, waits for them, and re-layouts: 7.14 us -> 11.5 us  [gathered(): spread = jnp.broadcast_to(x[None], (peers,) + x.shape)]
    all_to_all x4 -> x5, starting transfers between devices: 27.7 us -> 31.1 us  [gathered(): return lax.all_to_all(spread, axis, 0, 0)]
    all_to_all x4 -> x5, waiting for transfers between devices: 108 us -> 107 us  [gathered(): return lax.all_to_all(spread, axis, 0, 0)]
  transfers between devices with their start and end apart: 8 -> 10, of which waited for: 6 -> 9; matrix products, arithmetic and copies ran while one was open for 28% -> 18% of each run, Pallas kernels for 0% -> 0%
where the time goes in v2:
time: 366 us; the launch traced here: 365 us
  waiting for transfers between devices  209 us (57%)
  matrix products  57.7 us (16%)
  starting transfers between devices  38.3 us (10%)
  local copies, waits for them, and re-layouts  25.9 us (7%)
  other arithmetic  14.8 us (4%)
  between operations  13.9 us (4%)
  loops' own time  5.34 us (1%)
    all_to_all x5, waiting for transfers between devices, gathered(): return lax.all_to_all(spread, axis, 0, 0)  107 us
    all_gather x1, waiting for transfers between devices, per_device(): columns = lax.all_gather(out_weights[0], 'y', axis=0)  49.6 us
    all_to_all x5, starting transfers between devices, gathered(): return lax.all_to_all(spread, axis, 0, 0)  31.1 us
    ppermute x2, waiting for transfers between devices, from_partner(): return lax.ppermute(block, axis, route)  25.9 us
    ppermute x1, waiting for transfers between devices, shifted(): return lax.ppermute(x, axis, pairs)  15.5 us
    dot_general x4, matrix products, absorb(): jnp.einsum('gjqk,kgd->gjqd', weights_exp.astype(jnp.bfloat16), value_rows...  14.3 us
    broadcast_in_dim x6, local copies, waits for them, and re-layouts, gathered(): spread = jnp.broadcast_to(x[None], (peers,) + x.shape)  11.5 us
    all_to_all x1, waiting for transfers between devices, per_device(): pieces = lax.all_to_all(pieces, 'zc', 0, 0)  9.95 us
  transfers between devices with their start and end apart: 10, of which 9 were waited for; matrix products, arithmetic and copies ran while one was open for 18% of the time, Pallas kernels for 0%

profile of v2, /device:TPU:30, one launch (start us, length us, event | category | flops | bytes accessed | tf_op | source)
XLA Modules:
  0.0 364.6 jit_solution(11986000666019512132)
XLA Ops:
  6.5 0.8 constant_dynamic-slice_fusion.4
  7.4 0.7 dynamic_slice.71
  8.4 0.6 broadcast_in_dim.220
  9.0 8.4 %all-to-all-start = ((f32[32,1,32]{2,1,0:T(1,128)}), f32[32,1,32]{2,1,0:T(1,128)S(1)}, u32[]{:S(2)}, u32[]{:S(2)}) async-start(f32[32,1,32]{2,1,0:T(1,128)} %broadcast_in_dim.220), calls=%async_computation | async-start | bytes 32768 | tf_op jit(solution)/shard_map/all_to_all | solution.py:43
  17.8 1.4 fusion.47
  19.3 3.5 all-to-all-done
  22.8 3.1 broadcast_in_dim.226
  25.9 4.7 %all-to-all-start.1 = ((bf16[8,1,32,64,128]{4,3,2,1,0:T(8,128)(2,1)}), bf16[8,1,32,64,128]{4,3,2,1,0:T(8,128)(2,1)}, u32[]{:S(2)}, u32[]{:S(2)}) async-start(bf16[8,1,32,64,128]{4,3,2,1,0:T(8,128)(2,1)} %broadcast_in_dim.226), calls=%async_computation.1 | async-start | bytes 8388608 | tf_op jit(solution)/shard_map/all_to_all | solution.py:43
  30.7 1.3 copy.93
  32.1 1.1 constant_dynamic-slice_fusion
  33.3 1.0 copy.112
  34.8 0.6 slice.24
  35.8 44.4 %all-to-all-done.1 = bf16[8,1,32,64,128]{4,3,2,1,0:T(8,128)(2,1)} async-done(((bf16[8,1,32,64,128]{4,3,2,1,0:T(8,128)(2,1)}), bf16[8,1,32,64,128]{4,3,2,1,0:T(8,128)(2,1)}, u32[]{:S(2)}, u32[]{:S(2)}) %all-to-all-start.1) | async-done | bytes 4194336 | tf_op jit(solution)/shard_map/all_to_all | solution.py:43
  80.2 1.6 broadcast_in_dim.239
  81.8 5.9 %all-to-all-start.3 = ((bf16[32,128,256]{2,1,0:T(8,128)(2,1)}), bf16[32,128,256]{2,1,0:T(8,128)(2,1)S(1)}, u32[]{:S(2)}, u32[]{:S(2)}) async-start(bf16[32,128,256]{2,1,0:T(8,128)(2,1)} %broadcast_in_dim.239), calls=%async_computation.3 | async-start | bytes 4194304 | tf_op jit(solution)/shard_map/all_to_all | solution.py:43
  87.8 3.4 fusion.39
  92.0 7.2 %fusion.27 = f32[32,1,64,128]{3,1,2,0:T(1,128)S(1)} fusion(f32[8,32,1,1]{0,2,3,1:T(1,128)S(1)} %copy.106, bf16[8,32,64,128]{3,2,1,0:T(8,128)(2,1)} %bitcast.28), kind=kOutput, calls=%fused_computation.29 | convolution fusion | flops 25165824 | bytes 5243904 | tf_op jit(solution)/shard_map/kgj,kgjpn->gjpn/dot_general | solution.py:67
  99.3 14.8 %all-to-all-done.3 = bf16[32,128,256]{2,1,0:T(8,128)(2,1)S(1)} async-done(((bf16[32,128,256]{2,1,0:T(8,128)(2,1)}), bf16[32,128,256]{2,1,0:T(8,128)(2,1)S(1)}, u32[]{:S(2)}, u32[]{:S(2)}) %all-to-all-start.3) | async-done | bytes 2097184 | tf_op jit(solution)/shard_map/all_to_all | solution.py:43
  114.1 1.9 broadcast_in_dim.235
  116.0 7.2 %all-to-all-start.2 = ((bf16[4,1,32,64,128]{4,3,2,1,0:T(8,128)(2,1)}), bf16[4,1,32,64,128]{4,3,2,1,0:T(8,128)(2,1)}, u32[]{:S(2)}, u32[]{:S(2)}) async-start(bf16[4,1,32,64,128]{4,3,2,1,0:T(8,128)(2,1)} %broadcast_in_dim.235), calls=%async_computation.2 | async-start | bytes 4194304 | tf_op jit(solution)/shard_map/all_to_all | solution.py:43
  123.2 1.5 fusion.85
  124.8 42.5 %while.4 = (s32[]{:T(128)}, f32[1,16,128]{2,1,0:T(8,128)S(1)}, f32[1,16,128]{2,1,0:T(8,128)S(1)}, f32[1,16,128,128]{3,2,1,0:T(8,128)S(1)}, s32[4]{0:T(128)S(1)},...) while((s32[]{:T(128)}, f32[1,16,128]{2,1,0:T(8,128)S(1)}, ...), condition=%wide.region_10.11_spmd.clone, body=%wide.region_5.10_spmd.clone.sunk | while | flops 1101667456 | bytes 28978456 | solution.py:241
  124.8 0.6 dynamic_slice.114
  126.6 8.8 %conditional.3 = ((f32[1,16,128]{2,1,0:T(8,128)S(1)}, f32[1,16,128]{2,1,0:T(8,128)S(1)}, f32[1,16,128,128]{3,2,1,0:T(8,128)S(1)})) conditional(s32[]{:T(128)} %convert_element_type.150, (f32[1,16,128]{2,1,0:T(8,128)S(1)}, f32[1,16,128]{2,1,0:T(8,128)S(1)}, f32[1,16,128,128]{3,2,1,0:T(8,128)S(1)}) %tuple.54, (s32[]{:T(128)}, s32[]{:T(128)}, ...), branch_computations={%region_6.6_spmd, %region_7.9_spmd} | conditional | flops 1101667456 | bytes 28977704 | solution.py:223
  126.6 0.6 iota_add_fusion
  127.5 2.3 fusion.2
  129.8 2.0 fusion.4
  131.8 3.6 fusion.12
  137.3 8.8 %conditional.3 = ((f32[1,16,128]{2,1,0:T(8,128)S(1)}, f32[1,16,128]{2,1,0:T(8,128)S(1)}, f32[1,16,128,128]{3,2,1,0:T(8,128)S(1)})) conditional(s32[]{:T(128)} %convert_element_type.150, (f32[1,16,128]{2,1,0:T(8,128)S(1)}, f32[1,16,128]{2,1,0:T(8,128)S(1)}, f32[1,16,128,128]{3,2,1,0:T(8,128)S(1)}) %tuple.54, (s32[]{:T(128)}, s32[]{:T(128)}, ...), branch_computations={%region_6.6_spmd, %region_7.9_spmd} | conditional | flops 1101667456 | bytes 28977704 | solution.py:223
  137.3 0.6 iota_add_fusion
  138.1 2.3 fusion.2
  140.4 2.0 fusion.4
  142.4 3.6 fusion.12
  147.9 8.8 %conditional.3 = ((f32[1,16,128]{2,1,0:T(8,128)S(1)}, f32[1,16,128]{2,1,0:T(8,128)S(1)}, f32[1,16,128,128]{3,2,1,0:T(8,128)S(1)})) conditional(s32[]{:T(128)} %convert_element_type.150, (f32[1,16,128]{2,1,0:T(8,128)S(1)}, f32[1,16,128]{2,1,0:T(8,128)S(1)}, f32[1,16,128,128]{3,2,1,0:T(8,128)S(1)}) %tuple.54, (s32[]{:T(128)}, s32[]{:T(128)}, ...), branch_computations={%region_6.6_spmd, %region_7.9_spmd} | conditional | flops 1101667456 | bytes 28977704 | solution.py:223
  147.9 0.6 iota_add_fusion
  148.8 2.3 fusion.2
  151.1 2.0 fusion.4
  153.1 3.6 fusion.12
  158.5 8.8 %conditional.3 = ((f32[1,16,128]{2,1,0:T(8,128)S(1)}, f32[1,16,128]{2,1,0:T(8,128)S(1)}, f32[1,16,128,128]{3,2,1,0:T(8,128)S(1)})) conditional(s32[]{:T(128)} %convert_element_type.150, (f32[1,16,128]{2,1,0:T(8,128)S(1)}, f32[1,16,128]{2,1,0:T(8,128)S(1)}, f32[1,16,128,128]{3,2,1,0:T(8,128)S(1)}) %tuple.54, (s32[]{:T(128)}, s32[]{:T(128)}, ...), branch_computations={%region_6.6_spmd, %region_7.9_spmd} | conditional | flops 1101667456 | bytes 28977704 | solution.py:223
  158.6 0.6 iota_add_fusion
  159.4 2.3 fusion.2
  161.7 2.0 fusion.4
  163.7 3.6 fusion.12
  168.0 7.1 %fusion.29 = f32[32,1,64,128]{3,1,2,0:T(1,128)S(1)} fusion(f32[8,32,1,1]{0,2,3,1:T(1,128)S(1)} %copy.103, bf16[8,32,64,128]{3,2,1,0:T(8,128)(2,1)} %bitcast.28), kind=kOutput, calls=%fused_computation.31 | convolution fusion | flops 25165824 | bytes 5243904 | tf_op jit(solution)/shard_map/kgj,kgjpn->gjpn/dot_general | solution.py:63
  175.2 5.6 %fusion.37 = f32[32,1,64,128]{3,1,2,0:T(1,128)S(1)} fusion(f32[4,32,1,1]{0,2,3,1:T(1,128)S(1)} %copy.108, bf16[4,32,64,128]{3,2,1,0:T(8,128)(2,1)} %bitcast.35), kind=kOutput, calls=%fused_computation.40 | convolution fusion | flops 12582912 | bytes 3146240 | tf_op jit(solution)/shard_map/kgj,kgjpn->gjpn/dot_general | solution.py:74
  180.8 0.7 fusion.46
  181.5 0.6 fusion.45
  182.6 0.8 bitcast_select_fusion.2
  183.4 1.5 collective-permute-start
  184.9 13.3 %collective-permute-done = bf16[128,2048]{0,1:T(8,128)(2,1)S(1)} collective-permute-done((bf16[128,2048]{0,1:T(8,128)(2,1)S(1)}, bf16[128,2048]{0,1:T(8,128)(2,1)S(1)}, u32[]{:S(2)}, u32[]{:S(2)}) %collective-permute-start) | collective-permute-done | bytes 524320 | tf_op jit(solution)/shard_map/ppermute | solution.py:85
  199.0 4.3 %broadcast_in_dim.240 = bf16[8,128,4096]{2,1,0:T(8,128)(2,1)} broadcast(bf16[128,4096]{1,0:T(8,128)(2,1)S(1)} %copy.98), dimensions={1,2} | broadcast | bytes 9437184 | tf_op jit(solution)/shard_map/broadcast_in_dim | solution.py:42
  203.3 5.0 %all-to-all-start.4 = ((bf16[8,128,4096]{2,1,0:T(8,128)(2,1)}), bf16[8,128,4096]{2,1,0:T(8,128)(2,1)}, u32[]{:S(2)}, u32[]{:S(2)}) async-start(bf16[8,128,4096]{2,1,0:T(8,128)(2,1)} %broadcast_in_dim.240), calls=%async_computation.4 | async-start | bytes 16777216 | tf_op jit(solution)/shard_map/all_to_all | solution.py:43
  208.3 0.7 all-gather.2.cloned.1.call-update
  209.0 49.6 %all-gather.2.cloned.1.call-done = bf16[4,4096,128]{2,1,0:T(8,128)(2,1)} async-done(((bf16[1,4096,128]{2,1,0:T(8,128)(2,1)}), bf16[4,4096,128]{2,1,0:T(8,128)(2,1)}) %all-gather.2.cloned.1.call-update) | async-done | bytes 4194320 | tf_op jit(solution)/shard_map/all_gather | solution.py:296
  258.6 44.3 %all-to-all-done.4 = bf16[8,128,4096]{2,1,0:T(8,128)(2,1)} async-done(((bf16[8,128,4096]{2,1,0:T(8,128)(2,1)}), bf16[8,128,4096]{2,1,0:T(8,128)(2,1)}, u32[]{:S(2)}, u32[]{:S(2)}) %all-to-all-start.4) | async-done | bytes 8388640 | tf_op jit(solution)/shard_map/all_to_all | solution.py:43
  302.8 8.1 %fusion.87 = f32[1024,4,128]{2,0,1:T(8,128)S(1)} fusion(bf16[1024,4096,1]{1,0,2:T(8,128)(2,1)} %bitcast.51, bf16[4,4096,128]{2,1,0:T(8,128)(2,1)} %all-gather.2.cloned.1.call-done), kind=kOutput, calls=%fused_computation.134 | convolution fusion | flops 4294967296 | bytes 14680064 | tf_op jit(solution)/shard_map/tc,ycr->tyr/dot_general | solution.py:297
  311.1 0.9 collective-permute-start.1
  312.0 12.5 %collective-permute-done.1 = bf16[1024,2,128]{2,0,1:T(8,128)(2,1)S(1)} collective-permute-done((bf16[1024,2,128]{2,0,1:T(8,128)(2,1)S(1)}, bf16[1024,2,128]{2,0,1:T(8,128)(2,1)S(1)}, u32[]{:S(2)}, u32[]{:S(2)}) %collective-permute-start.1) | collective-permute-done | bytes 524320 | tf_op jit(solution)/shard_map/ppermute | solution.py:85
  324.7 0.8 copy.99
  325.6 3.5 all-to-all-start.5
  329.4 10.0 %all-to-all-done.5 = bf16[8,128,2,128]{3,1,2,0:T(8,128)(2,1)S(1)} async-done(((bf16[8,128,2,128]{3,1,2,0:T(8,128)(2,1)}), bf16[8,128,2,128]{3,1,2,0:T(8,128)(2,1)S(1)}, u32[]{:S(2)}, u32[]{:S(2)}) %all-to-all-start.5) | async-done | bytes 524320 | tf_op jit(solution)/shard_map/all_to_all | solution.py:305
  339.7 1.3 collective-permute-start.2
  341.0 15.5 %collective-permute-done.2 = bf16[128,2048]{0,1:T(8,128)(2,1)S(1)} collective-permute-done((bf16[128,2048]{0,1:T(8,128)(2,1)S(1)}, bf16[128,2048]{0,1:T(8,128)(2,1)S(1)}, u32[]{:S(2)}, u32[]{:S(2)}) %collective-permute-start.2) | collective-permute-done | bytes 524320 | tf_op jit(solution)/shard_map/ppermute | solution.py:91
  356.7 1.0 copy.101
  (114 shorter events, 8.5 us)
Async XLA Ops:
  6.5 10.9 %copy-start = (bf16[128,4096]{1,0:T(8,128)(2,1)S(1)}, bf16[128,4096]{1,0:T(8,128)(2,1)}, u32[]{:S(2)}) copy-start(bf16[128,4096]{1,0:T(8,128)(2,1)} %param.18) | copy-start | bytes 3145732
  9.0 13.8 %all-to-all-start = ((f32[32,1,32]{2,1,0:T(1,128)}), f32[32,1,32]{2,1,0:T(1,128)S(1)}, u32[]{:S(2)}, u32[]{:S(2)}) async-start(f32[32,1,32]{2,1,0:T(1,128)} %broadcast_in_dim.220), calls=%async_computation | async-start | bytes 32768 | tf_op jit(solution)/shard_map/all_to_all | solution.py:43
  17.8 8.1 %copy-start.4 = (bf16[128,2048]{0,1:T(8,128)(2,1)}, bf16[128,2048]{0,1:T(8,128)(2,1)S(1)}, u32[]{:S(2)}) copy-start(bf16[128,2048]{0,1:T(8,128)(2,1)S(1)} %copy.86) | copy-start | bytes 1572868
  25.9 6.2 %copy-start.14 = (f32[64]{0:T(128)S(1)}, f32[64]{0:T(128)}, u32[]{:S(2)}) copy-start(f32[64]{0:T(128)} %param.24) | copy-start | bytes 772
  25.9 6.2 %copy-start.8 = (bf16[128,4096]{1,0:T(8,128)(2,1)S(1)}, bf16[128,4096]{1,0:T(8,128)(2,1)}, u32[]{:S(2)}) copy-start(bf16[128,4096]{1,0:T(8,128)(2,1)} %param.26) | copy-start | bytes 3145732
  25.9 54.3 %all-to-all-start.1 = ((bf16[8,1,32,64,128]{4,3,2,1,0:T(8,128)(2,1)}), bf16[8,1,32,64,128]{4,3,2,1,0:T(8,128)(2,1)}, u32[]{:S(2)}, u32[]{:S(2)}) async-start(bf16[8,1,32,64,128]{4,3,2,1,0:T(8,128)(2,1)} %broadcast_in_dim.226), calls=%async_computation.1 | async-start | bytes 8388608 | tf_op jit(solution)/shard_map/all_to_all | solution.py:43
  30.6 4.9 %copy-start.11 = (f32[128,64]{0,1:T(8,128)S(1)}, f32[128,64]{0,1:T(8,128)}, u32[]{:S(2)}) copy-start(f32[128,64]{0,1:T(8,128)} %param.22) | copy-start | bytes 98308
  30.6 5.0 %copy-start.9 = (bf16[128,256]{1,0:T(8,128)(2,1)S(1)}, bf16[128,256]{1,0:T(8,128)(2,1)}, u32[]{:S(2)}) copy-start(bf16[128,256]{1,0:T(8,128)(2,1)} %param.21) | copy-start | bytes 196612
  30.6 5.0 %copy-start.10 = (bf16[128,256]{1,0:T(8,128)(2,1)S(1)}, bf16[128,256]{1,0:T(8,128)(2,1)}, u32[]{:S(2)}) copy-start(bf16[128,256]{1,0:T(8,128)(2,1)} %param.20) | copy-start | bytes 196612
  30.6 5.1 %copy-start.12 = (bf16[128,256]{1,0:T(8,128)(2,1)S(1)}, bf16[128,256]{1,0:T(8,128)(2,1)}, u32[]{:S(2)}) copy-start(bf16[128,256]{1,0:T(8,128)(2,1)} %param.28) | copy-start | bytes 196612
  30.6 5.1 %copy-start.13 = (bf16[128,256]{1,0:T(8,128)(2,1)S(1)}, bf16[128,256]{1,0:T(8,128)(2,1)}, u32[]{:S(2)}) copy-start(bf16[128,256]{1,0:T(8,128)(2,1)} %param.27) | copy-start | bytes 196612
  34.5 53.2 %copy-start.5 = (bf16[128,2048]{0,1:T(8,128)(2,1)S(1)}, bf16[128,2048]{0,1:T(8,128)(2,1)}, u32[]{:S(2)}) copy-start(bf16[128,2048]{0,1:T(8,128)(2,1)} %copy-done.4) | copy-start | bytes 1572868
  81.8 32.3 %all-to-all-start.3 = ((bf16[32,128,256]{2,1,0:T(8,128)(2,1)}), bf16[32,128,256]{2,1,0:T(8,128)(2,1)S(1)}, u32[]{:S(2)}, u32[]{:S(2)}) async-start(bf16[32,128,256]{2,1,0:T(8,128)(2,1)} %broadcast_in_dim.239), calls=%async_computation.3 | async-start | bytes 4194304 | tf_op jit(solution)/shard_map/all_to_all | solution.py:43
  116.0 59.1 %all-to-all-start.2 = ((bf16[4,1,32,64,128]{4,3,2,1,0:T(8,128)(2,1)}), bf16[4,1,32,64,128]{4,3,2,1,0:T(8,128)(2,1)}, u32[]{:S(2)}, u32[]{:S(2)}) async-start(bf16[4,1,32,64,128]{4,3,2,1,0:T(8,128)(2,1)} %broadcast_in_dim.235), calls=%async_computation.2 | async-start | bytes 4194304 | tf_op jit(solution)/shard_map/all_to_all | solution.py:43
  175.1 6.4 %copy-start.3 = (f32[128,2048]{0,1:T(8,128)S(1)}, f32[128,2048]{0,1:T(8,128)}, u32[]{:S(2)}) copy-start(f32[128,2048]{0,1:T(8,128)} %copy.93) | copy-start | bytes 3145732
  175.1 6.4 %copy-start.6 = (f32[128,1,32,64]{0,3,2,1:T(8,128)S(1)}, f32[128,1,32,64]{0,3,2,1:T(8,128)}, u32[]{:S(2)}) copy-start(f32[128,1,32,64]{0,3,2,1:T(8,128)} %fusion.39) | copy-start | bytes 3145732
  180.8 1.3 copy-start.2
  180.8 1.7 dynamic-slice-start
  183.4 14.8 %collective-permute-start = (bf16[128,2048]{0,1:T(8,128)(2,1)S(1)}, bf16[128,2048]{0,1:T(8,128)(2,1)S(1)}, u32[]{:S(2)}, u32[]{:S(2)}) collective-permute-start(bf16[128,2048]{0,1:T(8,128)(2,1)S(1)} %get-tuple-element.273), channel_id=1, source_target_pairs={{0,64},{64,0},{1,65},{65,1},{2,66},{66,2},{3,67},{67,3},{4,68},{68... | collective-permute-start | bytes 1572872 | tf_op jit(solution)/shard_map/ppermute | solution.py:85
  203.3 99.6 %all-to-all-start.4 = ((bf16[8,128,4096]{2,1,0:T(8,128)(2,1)}), bf16[8,128,4096]{2,1,0:T(8,128)(2,1)}, u32[]{:S(2)}, u32[]{:S(2)}) async-start(bf16[8,128,4096]{2,1,0:T(8,128)(2,1)} %broadcast_in_dim.240), calls=%async_computation.4 | async-start | bytes 16777216 | tf_op jit(solution)/shard_map/all_to_all | solution.py:43
  208.3 50.3 %all-gather.2.cloned.1.call-start = ((), (), s32[]{:S(2)}) async-start(), calls=%async_computation.6 | async-start | bytes 5242880 | tf_op jit(solution)/shard_map/all_gather | solution.py:296
  311.0 18.1 %copy-start.7 = (bf16[128,2048]{1,0:T(8,128)(2,1)S(1)}, bf16[128,2048]{1,0:T(8,128)(2,1)}, u32[]{:S(2)}) copy-start(bf16[128,2048]{1,0:T(8,128)(2,1)} %param.17) | copy-start | bytes 1572868
  311.1 13.5 %collective-permute-start.1 = (bf16[1024,2,128]{2,0,1:T(8,128)(2,1)S(1)}, bf16[1024,2,128]{2,0,1:T(8,128)(2,1)S(1)}, u32[]{:S(2)}, u32[]{:S(2)}) collective-permute-start(bf16[1024,2,128]{2,0,1:T(8,128)(2,1)S(1)} %select_convert_fusion), channel_id=1, source_target_pairs={{0,1},{1,0},{2,3},{3,2},{4,5},{5,4},{6,7},{7,6},{8,9},{9,8},{10,11... | collective-permute-start | bytes 1572872 | tf_op jit(solution)/shard_map/ppermute | solution.py:85
  324.7 33.0 %copy-start.1 = (bf16[128,4096]{1,0:T(8,128)(2,1)S(1)}, bf16[128,4096]{1,0:T(8,128)(2,1)}, u32[]{:S(2)}) copy-start(bf16[128,4096]{1,0:T(8,128)(2,1)} %param.18) | copy-start | bytes 3145732
  325.6 13.7 %all-to-all-start.5 = ((bf16[8,128,2,128]{3,1,2,0:T(8,128)(2,1)}), bf16[8,128,2,128]{3,1,2,0:T(8,128)(2,1)S(1)}, u32[]{:S(2)}, u32[]{:S(2)}) async-start(bf16[8,128,2,128]{3,1,2,0:T(8,128)(2,1)} %copy.99), calls=%async_computation.5 | async-start | bytes 1048576 | tf_op jit(solution)/shard_map/all_to_all | solution.py:305
  339.7 16.8 %collective-permute-start.2 = (bf16[128,2048]{0,1:T(8,128)(2,1)S(1)}, bf16[128,2048]{0,1:T(8,128)(2,1)S(1)}, u32[]{:S(2)}, u32[]{:S(2)}) collective-permute-start(bf16[128,2048]{0,1:T(8,128)(2,1)S(1)} %fusion.52), channel_id=1, source_target_pairs={{0,64},{1,65},{2,66},{3,67},{4,68},{5,69},{6,70},{7,71},{8,72},{9,... | collective-permute-start | bytes 1572872 | tf_op jit(solution)/shard_map/ppermute | solution.py:91
Sparse Core Ops, SparseCore 0:
  210.7 47.7 all-gather.1

commit v3 on v2

--- a/solution.py
+++ b/solution.py
@@ -293,7 +293,7 @@
     inner = lax.axis_size("zc")
     tp_rank = lax.axis_index("tp")
     rows = gathered(mixed_rows, "zc").reshape(-1, mixed_rows.shape[1])
-    columns = lax.all_gather(out_weights[0], "y", axis=0)
+    columns = gathered(out_weights[0], "y")
     partial_value = jnp.einsum(
         "tc,ycr->tyr", rows, columns, preferred_element_type=jnp.float32
     )

time: 366 us -> 378 us (1.033)
  waiting for transfers between devices: 209 us -> 224 us
  between operations: 13.9 us -> 0.55 us
  starting transfers between devices: 38.3 us -> 43.6 us
    all_to_all x5 -> x6, waiting for transfers between devices: 107 us -> 173 us  [gathered(): return lax.all_to_all(spread, axis, 0, 0)]
    all_gather x1 -> x0, waiting for transfers between devices: 49.6 us -> none  [per_device(): columns = lax.all_gather(out_weights[0], 'y', axis=0)]
    all_to_all x5 -> x6, starting transfers between devices: 31.1 us -> 36.2 us  [gathered(): return lax.all_to_all(spread, axis, 0, 0)]
    broadcast_in_dim x6 -> x7, local copies, waits for them, and re-layouts: 11.5 us -> 14.1 us  [gathered(): spread = jnp.broadcast_to(x[None], (peers,) + x.shape)]
  transfers between devices with their start and end apart: 10 -> 10, of which waited for: 9 -> 9; matrix products, arithmetic and copies ran while one was open for 18% -> 20% of each run, Pallas kernels for 0% -> 0%
where the time goes in v3:
time: 378 us; the launch traced here: 374 us
  waiting for transfers between devices  224 us (59%)
  matrix products  57.8 us (15%)
  starting transfers between devices  43.6 us (12%)
  local copies, waits for them, and re-layouts  28.4 us (8%)
  other arithmetic  14.6 us (4%)
  loops' own time  5.34 us (1%)
    all_to_all x6, waiting for transfers between devices, gathered(): return lax.all_to_all(spread, axis, 0, 0)  173 us
    all_to_all x6, starting transfers between devices, gathered(): return lax.all_to_all(spread, axis, 0, 0)  36.2 us
    ppermute x2, waiting for transfers between devices, from_partner(): return lax.ppermute(block, axis, route)  25.9 us
    ppermute x1, waiting for transfers between devices, shifted(): return lax.ppermute(x, axis, pairs)  15.5 us
    dot_general x4, matrix products, absorb(): jnp.einsum('gjqk,kgd->gjqd', weights_exp.astype(jnp.bfloat16), value_rows...  14.3 us
    broadcast_in_dim x7, local copies, waits for them, and re-layouts, gathered(): spread = jnp.broadcast_to(x[None], (peers,) + x.shape)  14.1 us
    all_to_all x1, waiting for transfers between devices, per_device(): pieces = lax.all_to_all(pieces, 'zc', 0, 0)  9.95 us
    dot_general x4, matrix products, absorb(): jnp.einsum('qgjd,kgd->gjqk', query_groups, key_rows, preferred_element_ty...  9.05 us
  transfers between devices with their start and end apart: 10, of which 9 were waited for; matrix products, arithmetic and copies ran while one was open for 20% of the time, Pallas kernels for 0%

profile of v3, /device:TPU:30, one launch (start us, length us, event | category | flops | bytes accessed | tf_op | source)
XLA Modules:
  0.0 374.1 jit_solution(4393091135134514397)
XLA Ops:
  0.0 0.8 constant_dynamic-slice_fusion.4
  0.9 0.7 dynamic_slice.71
  1.8 0.6 broadcast_in_dim.227
  2.5 8.4 %all-to-all-start = ((f32[32,1,32]{2,1,0:T(1,128)}), f32[32,1,32]{2,1,0:T(1,128)S(1)}, u32[]{:S(2)}, u32[]{:S(2)}) async-start(f32[32,1,32]{2,1,0:T(1,128)} %broadcast_in_dim.227), calls=%async_computation | async-start | bytes 32768 | tf_op jit(solution)/shard_map/all_to_all | solution.py:43
  11.3 1.4 fusion.47
  12.7 3.5 all-to-all-done
  16.2 3.1 broadcast_in_dim.233
  19.3 4.7 %all-to-all-start.1 = ((bf16[8,1,32,64,128]{4,3,2,1,0:T(8,128)(2,1)}), bf16[8,1,32,64,128]{4,3,2,1,0:T(8,128)(2,1)}, u32[]{:S(2)}, u32[]{:S(2)}) async-start(bf16[8,1,32,64,128]{4,3,2,1,0:T(8,128)(2,1)} %broadcast_in_dim.233), calls=%async_computation.1 | async-start | bytes 8388608 | tf_op jit(solution)/shard_map/all_to_all | solution.py:43
  24.1 1.2 copy.93
  25.5 1.1 constant_dynamic-slice_fusion
  26.6 1.0 copy.112
  28.2 0.6 slice.24
  28.9 44.8 %all-to-all-done.1 = bf16[8,1,32,64,128]{4,3,2,1,0:T(8,128)(2,1)} async-done(((bf16[8,1,32,64,128]{4,3,2,1,0:T(8,128)(2,1)}), bf16[8,1,32,64,128]{4,3,2,1,0:T(8,128)(2,1)}, u32[]{:S(2)}, u32[]{:S(2)}) %all-to-all-start.1) | async-done | bytes 4194336 | tf_op jit(solution)/shard_map/all_to_all | solution.py:43
  73.7 1.6 broadcast_in_dim.246
  75.3 5.9 %all-to-all-start.3 = ((bf16[32,128,256]{2,1,0:T(8,128)(2,1)}), bf16[32,128,256]{2,1,0:T(8,128)(2,1)S(1)}, u32[]{:S(2)}, u32[]{:S(2)}) async-start(bf16[32,128,256]{2,1,0:T(8,128)(2,1)} %broadcast_in_dim.246), calls=%async_computation.3 | async-start | bytes 4194304 | tf_op jit(solution)/shard_map/all_to_all | solution.py:43
  81.4 3.4 fusion.39
  85.4 7.1 %fusion.27 = f32[32,1,64,128]{3,1,2,0:T(1,128)S(1)} fusion(f32[8,32,1,1]{0,2,3,1:T(1,128)S(1)} %copy.106, bf16[8,32,64,128]{3,2,1,0:T(8,128)(2,1)} %bitcast.28), kind=kOutput, calls=%fused_computation.29 | convolution fusion | flops 25165824 | bytes 5243904 | tf_op jit(solution)/shard_map/kgj,kgjpn->gjpn/dot_general | solution.py:67
  92.7 14.9 %all-to-all-done.3 = bf16[32,128,256]{2,1,0:T(8,128)(2,1)S(1)} async-done(((bf16[32,128,256]{2,1,0:T(8,128)(2,1)}), bf16[32,128,256]{2,1,0:T(8,128)(2,1)S(1)}, u32[]{:S(2)}, u32[]{:S(2)}) %all-to-all-start.3) | async-done | bytes 2097184 | tf_op jit(solution)/shard_map/all_to_all | solution.py:43
  107.6 1.9 broadcast_in_dim.242
  109.4 7.2 %all-to-all-start.2 = ((bf16[4,1,32,64,128]{4,3,2,1,0:T(8,128)(2,1)}), bf16[4,1,32,64,128]{4,3,2,1,0:T(8,128)(2,1)}, u32[]{:S(2)}, u32[]{:S(2)}) async-start(bf16[4,1,32,64,128]{4,3,2,1,0:T(8,128)(2,1)} %broadcast_in_dim.242), calls=%async_computation.2 | async-start | bytes 4194304 | tf_op jit(solution)/shard_map/all_to_all | solution.py:43
  117.0 1.5 fusion.85
  118.7 42.5 %while.4 = (s32[]{:T(128)}, f32[1,16,128]{2,1,0:T(8,128)S(1)}, f32[1,16,128]{2,1,0:T(8,128)S(1)}, f32[1,16,128,128]{3,2,1,0:T(8,128)S(1)}, s32[4]{0:T(128)S(1)},...) while((s32[]{:T(128)}, f32[1,16,128]{2,1,0:T(8,128)S(1)}, ...), condition=%wide.region_10.11_spmd.clone, body=%wide.region_5.10_spmd.clone.sunk | while | flops 1101667456 | bytes 28978456 | solution.py:241
  118.7 0.6 dynamic_slice.114
  120.5 8.8 %conditional.3 = ((f32[1,16,128]{2,1,0:T(8,128)S(1)}, f32[1,16,128]{2,1,0:T(8,128)S(1)}, f32[1,16,128,128]{3,2,1,0:T(8,128)S(1)})) conditional(s32[]{:T(128)} %convert_element_type.150, (f32[1,16,128]{2,1,0:T(8,128)S(1)}, f32[1,16,128]{2,1,0:T(8,128)S(1)}, f32[1,16,128,128]{3,2,1,0:T(8,128)S(1)}) %tuple.54, (s32[]{:T(128)}, s32[]{:T(128)}, ...), branch_computations={%region_6.6_spmd, %region_7.9_spmd} | conditional | flops 1101667456 | bytes 28977704 | solution.py:223
  120.5 0.6 iota_add_fusion
  121.4 2.3 fusion.2
  123.7 2.0 fusion.4
  125.7 3.6 fusion.12
  131.1 8.8 %conditional.3 = ((f32[1,16,128]{2,1,0:T(8,128)S(1)}, f32[1,16,128]{2,1,0:T(8,128)S(1)}, f32[1,16,128,128]{3,2,1,0:T(8,128)S(1)})) conditional(s32[]{:T(128)} %convert_element_type.150, (f32[1,16,128]{2,1,0:T(8,128)S(1)}, f32[1,16,128]{2,1,0:T(8,128)S(1)}, f32[1,16,128,128]{3,2,1,0:T(8,128)S(1)}) %tuple.54, (s32[]{:T(128)}, s32[]{:T(128)}, ...), branch_computations={%region_6.6_spmd, %region_7.9_spmd} | conditional | flops 1101667456 | bytes 28977704 | solution.py:223
  131.2 0.6 iota_add_fusion
  132.0 2.3 fusion.2
  134.3 2.0 fusion.4
  136.3 3.6 fusion.12
  141.8 8.8 %conditional.3 = ((f32[1,16,128]{2,1,0:T(8,128)S(1)}, f32[1,16,128]{2,1,0:T(8,128)S(1)}, f32[1,16,128,128]{3,2,1,0:T(8,128)S(1)})) conditional(s32[]{:T(128)} %convert_element_type.150, (f32[1,16,128]{2,1,0:T(8,128)S(1)}, f32[1,16,128]{2,1,0:T(8,128)S(1)}, f32[1,16,128,128]{3,2,1,0:T(8,128)S(1)}) %tuple.54, (s32[]{:T(128)}, s32[]{:T(128)}, ...), branch_computations={%region_6.6_spmd, %region_7.9_spmd} | conditional | flops 1101667456 | bytes 28977704 | solution.py:223
  141.8 0.6 iota_add_fusion
  142.6 2.3 fusion.2
  144.9 2.0 fusion.4
  147.0 3.6 fusion.12
  152.4 8.8 %conditional.3 = ((f32[1,16,128]{2,1,0:T(8,128)S(1)}, f32[1,16,128]{2,1,0:T(8,128)S(1)}, f32[1,16,128,128]{3,2,1,0:T(8,128)S(1)})) conditional(s32[]{:T(128)} %convert_element_type.150, (f32[1,16,128]{2,1,0:T(8,128)S(1)}, f32[1,16,128]{2,1,0:T(8,128)S(1)}, f32[1,16,128,128]{3,2,1,0:T(8,128)S(1)}) %tuple.54, (s32[]{:T(128)}, s32[]{:T(128)}, ...), branch_computations={%region_6.6_spmd, %region_7.9_spmd} | conditional | flops 1101667456 | bytes 28977704 | solution.py:223
  152.4 0.6 iota_add_fusion
  153.3 2.3 fusion.2
  155.6 2.0 fusion.4
  157.6 3.6 fusion.12
  161.9 2.6 broadcast_in_dim.249
  164.4 5.0 %all-to-all-start.5 = ((bf16[4,4096,128]{2,1,0:T(8,128)(2,1)}), bf16[4,4096,128]{2,1,0:T(8,128)(2,1)}, u32[]{:S(2)}, u32[]{:S(2)}) async-start(bf16[4,4096,128]{2,1,0:T(8,128)(2,1)} %broadcast_in_dim.249), calls=%async_computation.5 | async-start | bytes 8388608 | tf_op jit(solution)/shard_map/all_to_all | solution.py:43
  169.5 7.1 %fusion.29 = f32[32,1,64,128]{3,1,2,0:T(1,128)S(1)} fusion(f32[8,32,1,1]{0,2,3,1:T(1,128)S(1)} %copy.103, bf16[8,32,64,128]{3,2,1,0:T(8,128)(2,1)} %bitcast.28), kind=kOutput, calls=%fused_computation.31 | convolution fusion | flops 25165824 | bytes 5243904 | tf_op jit(solution)/shard_map/kgj,kgjpn->gjpn/dot_general | solution.py:63
  176.7 5.6 %fusion.37 = f32[32,1,64,128]{3,1,2,0:T(1,128)S(1)} fusion(f32[4,32,1,1]{0,2,3,1:T(1,128)S(1)} %copy.108, bf16[4,32,64,128]{3,2,1,0:T(8,128)(2,1)} %bitcast.35), kind=kOutput, calls=%fused_computation.40 | convolution fusion | flops 12582912 | bytes 3146240 | tf_op jit(solution)/shard_map/kgj,kgjpn->gjpn/dot_general | solution.py:74
  182.3 0.7 fusion.46
  183.0 0.6 fusion.45
  184.7 1.7 collective-permute-start
  186.4 13.3 %collective-permute-done = bf16[128,2048]{0,1:T(8,128)(2,1)S(1)} collective-permute-done((bf16[128,2048]{0,1:T(8,128)(2,1)S(1)}, bf16[128,2048]{0,1:T(8,128)(2,1)S(1)}, u32[]{:S(2)}, u32[]{:S(2)}) %collective-permute-start) | collective-permute-done | bytes 524320 | tf_op jit(solution)/shard_map/ppermute | solution.py:85
  200.6 14.8 %all-to-all-done.5 = bf16[4,4096,128]{2,1,0:T(8,128)(2,1)} async-done(((bf16[4,4096,128]{2,1,0:T(8,128)(2,1)}), bf16[4,4096,128]{2,1,0:T(8,128)(2,1)}, u32[]{:S(2)}, u32[]{:S(2)}) %all-to-all-start.5) | async-done | bytes 4194336 | tf_op jit(solution)/shard_map/all_to_all | solution.py:43
  215.4 4.3 %broadcast_in_dim.247 = bf16[8,128,4096]{2,1,0:T(8,128)(2,1)} broadcast(bf16[128,4096]{1,0:T(8,128)(2,1)S(1)} %copy.98), dimensions={1,2} | broadcast | bytes 9437184 | tf_op jit(solution)/shard_map/broadcast_in_dim | solution.py:42
  219.6 5.0 %all-to-all-start.4 = ((bf16[8,128,4096]{2,1,0:T(8,128)(2,1)}), bf16[8,128,4096]{2,1,0:T(8,128)(2,1)}, u32[]{:S(2)}, u32[]{:S(2)}) async-start(bf16[8,128,4096]{2,1,0:T(8,128)(2,1)} %broadcast_in_dim.247), calls=%async_computation.4 | async-start | bytes 16777216 | tf_op jit(solution)/shard_map/all_to_all | solution.py:43
  224.6 94.6 %all-to-all-done.4 = bf16[8,128,4096]{2,1,0:T(8,128)(2,1)} async-done(((bf16[8,128,4096]{2,1,0:T(8,128)(2,1)}), bf16[8,128,4096]{2,1,0:T(8,128)(2,1)}, u32[]{:S(2)}, u32[]{:S(2)}) %all-to-all-start.4) | async-done | bytes 8388640 | tf_op jit(solution)/shard_map/all_to_all | solution.py:43
  319.2 8.1 %fusion.87 = f32[1024,4,128]{2,0,1:T(8,128)S(1)} fusion(bf16[1024,4096,1]{1,0,2:T(8,128)(2,1)} %bitcast.51, bf16[4,4096,128]{2,1,0:T(8,128)(2,1)} %all-to-all-done.5), kind=kOutput, calls=%fused_computation.134 | convolution fusion | flops 4294967296 | bytes 14680064 | tf_op jit(solution)/shard_map/tc,ycr->tyr/dot_general | solution.py:297
  327.4 0.9 collective-permute-start.1
  328.4 12.5 %collective-permute-done.1 = bf16[1024,2,128]{2,0,1:T(8,128)(2,1)S(1)} collective-permute-done((bf16[1024,2,128]{2,0,1:T(8,128)(2,1)S(1)}, bf16[1024,2,128]{2,0,1:T(8,128)(2,1)S(1)}, u32[]{:S(2)}, u32[]{:S(2)}) %collective-permute-start.1) | collective-permute-done | bytes 524320 | tf_op jit(solution)/shard_map/ppermute | solution.py:85
  341.1 0.8 copy.99
  341.9 3.5 all-to-all-start.6
  345.7 10.0 %all-to-all-done.6 = bf16[8,128,2,128]{3,1,2,0:T(8,128)(2,1)S(1)} async-done(((bf16[8,128,2,128]{3,1,2,0:T(8,128)(2,1)}), bf16[8,128,2,128]{3,1,2,0:T(8,128)(2,1)S(1)}, u32[]{:S(2)}, u32[]{:S(2)}) %all-to-all-start.6) | async-done | bytes 524320 | tf_op jit(solution)/shard_map/all_to_all | solution.py:305
  356.1 1.3 collective-permute-start.2
  357.4 15.5 %collective-permute-done.2 = bf16[128,2048]{0,1:T(8,128)(2,1)S(1)} collective-permute-done((bf16[128,2048]{0,1:T(8,128)(2,1)S(1)}, bf16[128,2048]{0,1:T(8,128)(2,1)S(1)}, u32[]{:S(2)}, u32[]{:S(2)}) %collective-permute-start.2) | collective-permute-done | bytes 524320 | tf_op jit(solution)/shard_map/ppermute | solution.py:91
  373.1 1.0 copy.101
  (116 shorter events, 9.1 us)
Async XLA Ops:
  0.0 10.9 %copy-start = (bf16[128,4096]{1,0:T(8,128)(2,1)S(1)}, bf16[128,4096]{1,0:T(8,128)(2,1)}, u32[]{:S(2)}) copy-start(bf16[128,4096]{1,0:T(8,128)(2,1)} %param.18) | copy-start | bytes 3145732
  2.5 13.8 %all-to-all-start = ((f32[32,1,32]{2,1,0:T(1,128)}), f32[32,1,32]{2,1,0:T(1,128)S(1)}, u32[]{:S(2)}, u32[]{:S(2)}) async-start(f32[32,1,32]{2,1,0:T(1,128)} %broadcast_in_dim.227), calls=%async_computation | async-start | bytes 32768 | tf_op jit(solution)/shard_map/all_to_all | solution.py:43
  11.3 8.1 %copy-start.4 = (bf16[128,2048]{0,1:T(8,128)(2,1)}, bf16[128,2048]{0,1:T(8,128)(2,1)S(1)}, u32[]{:S(2)}) copy-start(bf16[128,2048]{0,1:T(8,128)(2,1)S(1)} %copy.86) | copy-start | bytes 1572868
  19.3 6.0 %copy-start.15 = (f32[64]{0:T(128)S(1)}, f32[64]{0:T(128)}, u32[]{:S(2)}) copy-start(f32[64]{0:T(128)} %param.24) | copy-start | bytes 772
  19.3 6.1 %copy-start.9 = (bf16[128,4096]{1,0:T(8,128)(2,1)S(1)}, bf16[128,4096]{1,0:T(8,128)(2,1)}, u32[]{:S(2)}) copy-start(bf16[128,4096]{1,0:T(8,128)(2,1)} %param.26) | copy-start | bytes 3145732
  19.3 54.3 %all-to-all-start.1 = ((bf16[8,1,32,64,128]{4,3,2,1,0:T(8,128)(2,1)}), bf16[8,1,32,64,128]{4,3,2,1,0:T(8,128)(2,1)}, u32[]{:S(2)}, u32[]{:S(2)}) async-start(bf16[8,1,32,64,128]{4,3,2,1,0:T(8,128)(2,1)} %broadcast_in_dim.233), calls=%async_computation.1 | async-start | bytes 8388608 | tf_op jit(solution)/shard_map/all_to_all | solution.py:43
  24.1 4.8 %copy-start.13 = (bf16[128,256]{1,0:T(8,128)(2,1)S(1)}, bf16[128,256]{1,0:T(8,128)(2,1)}, u32[]{:S(2)}) copy-start(bf16[128,256]{1,0:T(8,128)(2,1)} %param.28) | copy-start | bytes 196612
  24.1 4.8 %copy-start.14 = (bf16[128,256]{1,0:T(8,128)(2,1)S(1)}, bf16[128,256]{1,0:T(8,128)(2,1)}, u32[]{:S(2)}) copy-start(bf16[128,256]{1,0:T(8,128)(2,1)} %param.27) | copy-start | bytes 196612
  27.6 53.6 %copy-start.12 = (f32[128,64]{0,1:T(8,128)S(1)}, f32[128,64]{0,1:T(8,128)}, u32[]{:S(2)}) copy-start(f32[128,64]{0,1:T(8,128)} %param.22) | copy-start | bytes 98308
  27.6 53.7 %copy-start.10 = (bf16[128,256]{1,0:T(8,128)(2,1)S(1)}, bf16[128,256]{1,0:T(8,128)(2,1)}, u32[]{:S(2)}) copy-start(bf16[128,256]{1,0:T(8,128)(2,1)} %param.21) | copy-start | bytes 196612
  27.6 53.7 %copy-start.11 = (bf16[128,256]{1,0:T(8,128)(2,1)S(1)}, bf16[128,256]{1,0:T(8,128)(2,1)}, u32[]{:S(2)}) copy-start(bf16[128,256]{1,0:T(8,128)(2,1)} %param.20) | copy-start | bytes 196612
  27.9 53.6 %copy-start.5 = (bf16[128,2048]{0,1:T(8,128)(2,1)S(1)}, bf16[128,2048]{0,1:T(8,128)(2,1)}, u32[]{:S(2)}) copy-start(bf16[128,2048]{0,1:T(8,128)(2,1)} %copy-done.4) | copy-start | bytes 1572868
  75.3 32.3 %all-to-all-start.3 = ((bf16[32,128,256]{2,1,0:T(8,128)(2,1)}), bf16[32,128,256]{2,1,0:T(8,128)(2,1)S(1)}, u32[]{:S(2)}, u32[]{:S(2)}) async-start(bf16[32,128,256]{2,1,0:T(8,128)(2,1)} %broadcast_in_dim.246), calls=%async_computation.3 | async-start | bytes 4194304 | tf_op jit(solution)/shard_map/all_to_all | solution.py:43
  109.4 52.4 %all-to-all-start.2 = ((bf16[4,1,32,64,128]{4,3,2,1,0:T(8,128)(2,1)}), bf16[4,1,32,64,128]{4,3,2,1,0:T(8,128)(2,1)}, u32[]{:S(2)}, u32[]{:S(2)}) async-start(bf16[4,1,32,64,128]{4,3,2,1,0:T(8,128)(2,1)} %broadcast_in_dim.242), calls=%async_computation.2 | async-start | bytes 4194304 | tf_op jit(solution)/shard_map/all_to_all | solution.py:43
  118.6 43.2 %copy-start.6 = (bf16[1,4096,128]{2,1,0:T(8,128)(2,1)S(1)}, bf16[1,4096,128]{2,1,0:T(8,128)(2,1)}, u32[]{:S(2)}) copy-start(bf16[1,4096,128]{2,1,0:T(8,128)(2,1)} %param.29) | copy-start | bytes 3145732
  164.4 50.9 %all-to-all-start.5 = ((bf16[4,4096,128]{2,1,0:T(8,128)(2,1)}), bf16[4,4096,128]{2,1,0:T(8,128)(2,1)}, u32[]{:S(2)}, u32[]{:S(2)}) async-start(bf16[4,4096,128]{2,1,0:T(8,128)(2,1)} %broadcast_in_dim.249), calls=%async_computation.5 | async-start | bytes 8388608 | tf_op jit(solution)/shard_map/all_to_all | solution.py:43
  176.6 6.4 %copy-start.3 = (f32[128,2048]{0,1:T(8,128)S(1)}, f32[128,2048]{0,1:T(8,128)}, u32[]{:S(2)}) copy-start(f32[128,2048]{0,1:T(8,128)} %copy.93) | copy-start | bytes 3145732
  176.7 6.4 %copy-start.7 = (f32[128,1,32,64]{0,3,2,1:T(8,128)S(1)}, f32[128,1,32,64]{0,3,2,1:T(8,128)}, u32[]{:S(2)}) copy-start(f32[128,1,32,64]{0,3,2,1:T(8,128)} %fusion.39) | copy-start | bytes 3145732
  182.3 1.4 copy-start.2
  182.3 1.8 dynamic-slice-start
  184.7 15.1 %collective-permute-start = (bf16[128,2048]{0,1:T(8,128)(2,1)S(1)}, bf16[128,2048]{0,1:T(8,128)(2,1)S(1)}, u32[]{:S(2)}, u32[]{:S(2)}) collective-permute-start(bf16[128,2048]{0,1:T(8,128)(2,1)S(1)} %get-tuple-element.273), channel_id=1, source_target_pairs={{0,64},{64,0},{1,65},{65,1},{2,66},{66,2},{3,67},{67,3},{4,68},{68... | collective-permute-start | bytes 1572872 | tf_op jit(solution)/shard_map/ppermute | solution.py:85
  219.6 99.6 %all-to-all-start.4 = ((bf16[8,128,4096]{2,1,0:T(8,128)(2,1)}), bf16[8,128,4096]{2,1,0:T(8,128)(2,1)}, u32[]{:S(2)}, u32[]{:S(2)}) async-start(bf16[8,128,4096]{2,1,0:T(8,128)(2,1)} %broadcast_in_dim.247), calls=%async_computation.4 | async-start | bytes 16777216 | tf_op jit(solution)/shard_map/all_to_all | solution.py:43
  327.3 18.1 %copy-start.8 = (bf16[128,2048]{1,0:T(8,128)(2,1)S(1)}, bf16[128,2048]{1,0:T(8,128)(2,1)}, u32[]{:S(2)}) copy-start(bf16[128,2048]{1,0:T(8,128)(2,1)} %param.17) | copy-start | bytes 1572868
  327.4 13.5 %collective-permute-start.1 = (bf16[1024,2,128]{2,0,1:T(8,128)(2,1)S(1)}, bf16[1024,2,128]{2,0,1:T(8,128)(2,1)S(1)}, u32[]{:S(2)}, u32[]{:S(2)}) collective-permute-start(bf16[1024,2,128]{2,0,1:T(8,128)(2,1)S(1)} %select_convert_fusion), channel_id=1, source_target_pairs={{0,1},{1,0},{2,3},{3,2},{4,5},{5,4},{6,7},{7,6},{8,9},{9,8},{10,11... | collective-permute-start | bytes 1572872 | tf_op jit(solution)/shard_map/ppermute | solution.py:85
  341.0 33.0 %copy-start.1 = (bf16[128,4096]{1,0:T(8,128)(2,1)S(1)}, bf16[128,4096]{1,0:T(8,128)(2,1)}, u32[]{:S(2)}) copy-start(bf16[128,4096]{1,0:T(8,128)(2,1)} %param.18) | copy-start | bytes 3145732
  341.9 13.7 %all-to-all-start.6 = ((bf16[8,128,2,128]{3,1,2,0:T(8,128)(2,1)}), bf16[8,128,2,128]{3,1,2,0:T(8,128)(2,1)S(1)}, u32[]{:S(2)}, u32[]{:S(2)}) async-start(bf16[8,128,2,128]{3,1,2,0:T(8,128)(2,1)} %copy.99), calls=%async_computation.6 | async-start | bytes 1048576 | tf_op jit(solution)/shard_map/all_to_all | solution.py:305
  356.1 16.8 %collective-permute-start.2 = (bf16[128,2048]{0,1:T(8,128)(2,1)S(1)}, bf16[128,2048]{0,1:T(8,128)(2,1)S(1)}, u32[]{:S(2)}, u32[]{:S(2)}) collective-permute-start(bf16[128,2048]{0,1:T(8,128)(2,1)S(1)} %fusion.52), channel_id=1, source_target_pairs={{0,64},{1,65},{2,66},{3,67},{4,68},{5,69},{6,70},{7,71},{8,72},{9,... | collective-permute-start | bytes 1572872 | tf_op jit(solution)/shard_map/ppermute | solution.py:91

commit v4 on v1

--- a/solution.py
+++ b/solution.py
@@ -43,7 +43,7 @@
     return lax.all_to_all(spread, axis, 0, 0)
 
 
-def entering_states(through_log, local_state):
+def entering_states(through_log, local_state, riders):
     outer = lax.axis_size("y")
     inner = lax.axis_size("zc")
     peers = outer * inner
@@ -58,7 +58,13 @@
         return jnp.where((k < upto)[:, None, None], jnp.exp(summed), 0.0)
 
     first = lax.axis_index("y") * inner
-    near = gathered(local_state.astype(jnp.bfloat16), "zc").astype(jnp.float32)
+    state_size = local_state.size
+    payload = jnp.concatenate(
+        [local_state.astype(jnp.bfloat16).reshape(-1), riders.reshape(-1)]
+    )
+    near_all = gathered(payload, "zc")
+    near = near_all[:, :state_size].reshape((inner,) + local_state.shape).astype(jnp.float32)
+    near_riders = near_all[:, state_size:]
     near_ids = first + jnp.arange(inner, dtype=jnp.int32)
     own_part = jnp.einsum(
         "kgj,kgjpn->gjpn", span_weight(near_ids, rank), near, precision=exact_mode
@@ -67,12 +73,17 @@
     group_total = jnp.einsum(
         "kgj,kgjpn->gjpn", span_weight(near_ids, group_end), near, precision=exact_mode
     )
-    far = gathered(group_total.astype(jnp.bfloat16), "y").astype(jnp.float32)
+    payload = jnp.concatenate(
+        [group_total.astype(jnp.bfloat16).reshape(-1), near_riders.reshape(-1)]
+    )
+    far_all = gathered(payload, "y")
+    far = far_all[:, :state_size].reshape((outer,) + local_state.shape).astype(jnp.float32)
+    all_riders = far_all[:, state_size:].reshape((peers * riders.shape[0],) + riders.shape[1:])
     far_ends = (jnp.arange(outer, dtype=jnp.int32) + 1) * inner - 1
     far_weight = span_weight(far_ends, rank)
     far_weight = jnp.where((far_ends < first)[:, None, None], far_weight, 0.0)
     far_part = jnp.einsum("kgj,kgjpn->gjpn", far_weight, far, precision=exact_mode)
-    return own_part + far_part
+    return own_part + far_part, all_riders
 
 
 def from_partner(block, axis, distance):
@@ -135,7 +146,7 @@
 
 
 def mamba_mixer(
-    ssm_input, ssm_gate, ssm_in_b, ssm_out_c, step_size, decay_rate, skip_gain, norm_gain
+    ssm_input, ssm_gate, ssm_in_b, ssm_out_c, step_size, decay_rate, skip_gain, norm_gain, riders
 ):
     rows_here = ssm_input.shape[0]
     head_count = decay_rate.shape[0]
@@ -171,7 +182,9 @@
         ),
     )
     running = jnp.cumsum(log_decay, axis=0)
-    entering = entering_states(running[-1].reshape(groups, per_group), local_state)
+    entering, all_riders = entering_states(
+        running[-1].reshape(groups, per_group), local_state, riders
+    )
     output_all = ssm_out_c.astype(jnp.float32).reshape(rows_here, groups, STATE)
     carried = (
         jnp.einsum("tgn,gjpn->tgjp", output_all, entering, precision=exact_mode)
@@ -182,12 +195,12 @@
         * skip_gain.reshape(groups, per_group)[None, :, :, None]
     )
     values_y = pieces.reshape(rows_here, groups, per_group, MHEAD_DIM) + carried + skipped
-    return gate_norm(values_y.reshape(rows_here, -1), ssm_gate, norm_gain, groups)
-
-
-def attention(queries, keys, values, ctx_rank):
+    return gate_norm(values_y.reshape(rows_here, -1), ssm_gate, norm_gain, groups), all_riders
+
+
+def attention(queries, both, key_width, ctx_rank):
     rows_here = queries.shape[0]
-    kv_count = keys.shape[1] // HEAD_DIM
+    kv_count = key_width // HEAD_DIM
     per_key = queries.shape[1] // HEAD_DIM // kv_count
     query_groups = queries.reshape(rows_here, kv_count, per_key, HEAD_DIM)
     query_pos = ctx_rank * rows_here + jnp.arange(rows_here, dtype=jnp.int32)
@@ -228,10 +241,8 @@
         jnp.zeros((kv_count, per_key, rows_here, HEAD_DIM), jnp.float32),
     )
     running = start_state
-    both = gathered(jnp.concatenate([keys, values], axis=1), CTX)
-    both = both.reshape(-1, both.shape[-1])
-    key_piece = both[:, : keys.shape[1]]
-    value_piece = both[:, keys.shape[1] :]
+    key_piece = both[:, :key_width]
+    value_piece = both[:, key_width:]
     count = key_piece.shape[0]
     width = math.gcd(count, 1024)
     blocks = count // width
@@ -266,7 +277,9 @@
 ):
     section = lax.axis_index("pipe")
     ctx_rank = lax.axis_index("y") * lax.axis_size("zc") + lax.axis_index("zc")
-    mamba_part = mamba_mixer(
+    key_half = take_half(keys, 1, section)
+    value_half = take_half(values, 1, section)
+    mamba_part, both = mamba_mixer(
         take_half(ssm_input, 1, section),
         take_half(ssm_gate, 1, section),
         take_half(ssm_in_b, 1, section),
@@ -275,13 +288,9 @@
         take_half(decay_rate, 0, section),
         take_half(skip_gain, 0, section),
         take_half(norm_gain, 0, section),
-    )
-    attn_part = attention(
-        take_half(queries, 1, section),
-        take_half(keys, 1, section),
-        take_half(values, 1, section),
-        ctx_rank,
-    )
+        jnp.concatenate([key_half, value_half], axis=1),
+    )
+    attn_part = attention(take_half(queries, 1, section), both, key_half.shape[1], ctx_rank)
     outgoing = jnp.where(section == 0, attn_part, mamba_part)
     kept_half = jnp.where(section == 0, mamba_part, attn_part)
     incoming = from_partner(outgoing, "pipe", 0)

time: 295 us -> 426 us (1.44); the launches traced: 293 us -> 418 us
  local copies, waits for them, and re-layouts: 17.8 us -> 92.4 us
  other arithmetic: 17.4 us -> 76.7 us
  matrix products: 62 us -> 51.2 us
    broadcast_in_dim x0 -> x2, other arithmetic: none -> 58.8 us  [gathered(): spread = jnp.broadcast_to(x[None], (peers,) + x.shape)]
    unnamed x21 -> x30, local copies, waits for them, and re-layouts: 0.71 us -> 55.6 us
    all_gather x1, starting transfers between devices: 0.01 us -> 10.6 us  [per_device(): lax.all_gather(out_weights, CTX, axis=2, tiled=True)[0]]
    all_to_all x4 -> x3, starting transfers between devices: 27.7 us -> 18.4 us  [gathered(): return lax.all_to_all(spread, axis, 0, 0)]
    broadcast_in_dim x5, local copies, waits for them, and re-layouts: 7.14 us -> 12.9 us  [gathered(): spread = jnp.broadcast_to(x[None], (peers,) + x.shape)]
    reshape x0 -> x1, local copies, waits for them, and re-layouts: none -> 4.9 us  [entering_states(): far_all[:, state_size:]]
    all_to_all x4 -> x3, waiting for transfers between devices: 108 us -> 105 us  [gathered(): return lax.all_to_all(spread, axis, 0, 0)]
  transfers between devices with their start and end apart: 8 -> 7, of which waited for: 6 -> 5; matrix products, arithmetic and copies ran while one was open for 28% -> 48% of each run, Pallas kernels for 0% -> 0%
where the time goes in v4:
time: 426 us; the launch traced here: 418 us
  waiting for transfers between devices  146 us (34%)
  local copies, waits for them, and re-layouts  92.4 us (22%)
  other arithmetic  76.7 us (18%)
  matrix products  51.2 us (12%)
  starting transfers between devices  32.7 us (8%)
  between operations  14 us (3%)
  loops' own time  5.1 us (1%)
    all_to_all x3, waiting for transfers between devices, gathered(): return lax.all_to_all(spread, axis, 0, 0)  105 us
    broadcast_in_dim x2, other arithmetic, gathered(): spread = jnp.broadcast_to(x[None], (peers,) + x.shape)  58.8 us
    unnamed x30, local copies, waits for them, and re-layouts  55.6 us
    ppermute x2, waiting for transfers between devices, from_partner(): return lax.ppermute(block, axis, route)  26.1 us
    all_to_all x3, starting transfers between devices, gathered(): return lax.all_to_all(spread, axis, 0, 0)  18.4 us
    dot_general x4, matrix products, absorb(): jnp.einsum('gjqk,kgd->gjqd', weights_exp.astype(jnp.bfloat16), value_rows...  14.4 us
    ppermute x1, waiting for transfers between devices, shifted(): return lax.ppermute(x, axis, pairs)  14.3 us
    dot_general x1, matrix products, per_device(): jnp.dot(mixed_rows, lax.all_gather(out_weights, CTX, axis=2, tiled=True)[...  13.1 us
  transfers between devices with their start and end apart: 7, of which 5 were waited for; matrix products, arithmetic and copies ran while one was open for 48% of the time, Pallas kernels for 0%

profile of v4, /device:TPU:30, one launch (start us, length us, event | category | flops | bytes accessed | tf_op | source)
XLA Modules:
  0.0 417.9 jit_solution(2302690459869545491)
XLA Ops:
  6.5 0.8 constant_dynamic-slice_fusion.3
  7.4 0.7 dynamic_slice.71
  8.9 8.4 %all-to-all-start = ((f32[32,1,32]{2,1,0:T(1,128)}), f32[32,1,32]{2,1,0:T(1,128)S(1)}, u32[]{:S(2)}, u32[]{:S(2)}) async-start(f32[32,1,32]{2,1,0:T(1,128)} %broadcast_in_dim.208), calls=%async_computation | async-start | bytes 32768 | tf_op jit(solution)/shard_map/all_to_all | solution.py:43
  17.4 1.3 constant_dynamic-slice_fusion
  19.0 0.8 constant_dynamic-slice_fusion.1
  19.9 0.6 fusion.43
  20.6 6.2 %broadcast_in_dim.214 = bf16[8,1,294912]{2,1,0:T(2,128)(2,1)} broadcast(bf16[294912]{0:T(1024)(128)(2,1)S(1)} %pad_maximum_fusion.1), dimensions={2} | broadcast | bytes 5308416 | tf_op jit(solution)/shard_map/broadcast_in_dim | solution.py:42
  27.3 30.2 %reduce.11 = bf16[8,294912]{1,0:T(8,128)(2,1)} reduce(bf16[8,1,294912]{2,1,0:T(2,128)(2,1)} %broadcast_in_dim.214, bf16[]{:T(256)} %broadcast.376), dimensions={1}, to_apply=%broadcast_in_dim.214.reduce_sub_computation | reduce | bytes 9437186 | tf_op jit(solution)/shard_map/broadcast_in_dim | solution.py:42
  57.4 9.0 %reshape.511 = bf16[8,2,147456]{2,1,0:T(2,128)(2,1)} reshape(bf16[8,294912]{1,0:T(8,128)(2,1)} %reduce.11) | data formatting | bytes 9437184
  66.4 4.6 %all-to-all-start.1 = ((bf16[8,2,147456]{2,1,0:T(2,128)(2,1)}), bf16[8,2,147456]{2,1,0:T(2,128)(2,1)}, u32[]{:S(2)}, u32[]{:S(2)}) async-start(bf16[8,2,147456]{2,1,0:T(2,128)(2,1)} %reshape.511), calls=%async_computation.1 | async-start | bytes 9437184 | tf_op jit(solution)/shard_map/all_to_all | solution.py:43
  71.1 10.6 %all-gather.2.cloned.1.call-start = ((), (), s32[]{:S(2)}) async-start(), calls=%async_computation.3 | async-start | bytes 34603008 | tf_op jit(solution)/shard_map/all_gather | solution.py:304
  82.1 61.1 %all-to-all-done.1 = bf16[8,2,147456]{2,1,0:T(2,128)(2,1)} async-done(((bf16[8,2,147456]{2,1,0:T(2,128)(2,1)}), bf16[8,2,147456]{2,1,0:T(2,128)(2,1)}, u32[]{:S(2)}, u32[]{:S(2)}) %all-to-all-start.1) | async-done | bytes 4718624 | tf_op jit(solution)/shard_map/all_to_all | solution.py:43
  143.2 9.4 %reshape.512 = bf16[8,1,294912]{2,1,0:T(2,128)(2,1)} reshape(bf16[8,2,147456]{2,1,0:T(2,128)(2,1)} %all-to-all-done.1) | data formatting | bytes 9437184
  152.6 9.4 %copy.107 = bf16[8,1,294912]{2,0,1:T(8,128)(2,1)S(1)} copy(bf16[8,1,294912]{2,1,0:T(2,128)(2,1)} %reshape.512) | data formatting | bytes 9437184
  162.3 3.6 fusion.91
  166.2 5.6 %broadcast_in_dim.223 = bf16[4,1,524288]{2,1,0:T(2,128)(2,1)} broadcast(bf16[524288]{0:T(1024)(128)(2,1)S(1)} %pad_maximum_fusion), dimensions={2} | broadcast | bytes 5242880 | tf_op jit(solution)/shard_map/broadcast_in_dim | solution.py:42
  171.8 28.6 %reduce.12 = bf16[4,524288]{1,0:T(4,128)(2,1)} reduce(bf16[4,1,524288]{2,1,0:T(2,128)(2,1)} %broadcast_in_dim.223, bf16[]{:T(256)} %broadcast.376), dimensions={1}, to_apply=%broadcast_in_dim.223.reduce_sub_computation | reduce | bytes 8388610 | tf_op jit(solution)/shard_map/broadcast_in_dim | solution.py:42
  200.4 9.3 %reshape.513 = bf16[4,2,262144]{2,1,0:T(2,128)(2,1)} reshape(bf16[4,524288]{1,0:T(4,128)(2,1)} %reduce.12) | data formatting | bytes 8388608
  209.7 5.4 %all-to-all-start.2 = ((bf16[4,2,262144]{2,1,0:T(2,128)(2,1)}), bf16[4,2,262144]{2,1,0:T(2,128)(2,1)}, u32[]{:S(2)}, u32[]{:S(2)}) async-start(bf16[4,2,262144]{2,1,0:T(2,128)(2,1)} %reshape.513), calls=%async_computation.2 | async-start | bytes 8388608 | tf_op jit(solution)/shard_map/all_to_all | solution.py:43
  216.9 3.4 fusion.35
  220.8 5.6 %fusion.90 = f32[32,1,64,128]{3,1,2,0:T(1,128)S(1)} fusion(f32[8,32,1,1]{0,2,3,1:T(1,128)S(1)} %copy.89, bf16[8,32,64,128]{3,0,2,1:T(8,128)(2,1)} %bitcast.168), kind=kOutput, calls=%fused_computation.141 | convolution fusion | flops 25165824 | bytes 5243904 | tf_op jit(solution)/shard_map/kgj,kgjpn->gjpn/dot_general | solution.py:69
  226.4 44.4 %all-to-all-done.2 = bf16[4,2,262144]{2,1,0:T(2,128)(2,1)} async-done(((bf16[4,2,262144]{2,1,0:T(2,128)(2,1)}), bf16[4,2,262144]{2,1,0:T(2,128)(2,1)}, u32[]{:S(2)}, u32[]{:S(2)}) %all-to-all-start.2) | async-done | bytes 4194336 | tf_op jit(solution)/shard_map/all_to_all | solution.py:43
  270.8 7.4 %reshape.514 = bf16[4,1,524288]{2,1,0:T(2,128)(2,1)} reshape(bf16[4,2,262144]{2,1,0:T(2,128)(2,1)} %all-to-all-done.2) | data formatting | bytes 8388608
  278.3 10.3 %copy.108 = bf16[4,1,524288]{2,0,1:T(4,128)(2,1)S(1)} copy(bf16[4,1,524288]{2,1,0:T(2,128)(2,1)} %reshape.514) | data formatting | bytes 8388608
  288.6 2.5 fusion.87
  291.0 3.8 fusion.92
  294.8 0.7 fusion.42
  296.5 4.9 %reshape.495 = bf16[4096,256]{1,0:T(8,128)(2,1)} reshape(bf16[4,262144]{1,0:T(4,128)(2,1)} %get-tuple-element.273) | data formatting | bytes 4194304 | tf_op jit(solution)/shard_map/reshape | solution.py:81
  301.4 2.7 fusion.88
  304.0 1.1 broadcast_in_dim.226
  305.1 42.7 %while.4 = (s32[]{:T(128)}, f32[1,16,128]{2,1,0:T(8,128)S(1)}, f32[1,16,128]{2,1,0:T(8,128)S(1)}, f32[1,16,128,128]{3,2,1,0:T(8,128)}, s32[4]{0:T(128)S(1)}, /*i...) while((s32[]{:T(128)}, f32[1,16,128]{2,1,0:T(8,128)S(1)}, ...), condition=%wide.region_10.11_spmd.clone, body=%wide.region_5.10_spmd.clone.sunk | while | flops 1101667456 | bytes 37366608 | solution.py:252
  305.1 0.6 dynamic_slice.120
  307.0 8.9 %conditional.3 = ((f32[1,16,128]{2,1,0:T(8,128)S(1)}, f32[1,16,128]{2,1,0:T(8,128)S(1)}, f32[1,16,128,128]{3,2,1,0:T(8,128)})) conditional(s32[]{:T(128)} %convert_element_type.127, (f32[1,16,128]{2,1,0:T(8,128)S(1)}, f32[1,16,128]{2,1,0:T(8,128)S(1)}, f32[1,16,128,128]{3,2,1,0:T(8,128)}) %tuple.55, (s32[]{:T(128)}, s32[]{:T(128)}, ...), branch_computations={%region_6.6_spmd, %region_7.9_spmd} | conditional | flops 1101667456 | bytes 37365860 | solution.py:236
  307.8 1.3 fusion.2
  309.2 2.0 fusion.4
  311.2 3.6 fusion.12
  314.8 1.0 copy-done.4
  315.8 0.6 dynamic_slice.120
  317.6 8.8 %conditional.3 = ((f32[1,16,128]{2,1,0:T(8,128)S(1)}, f32[1,16,128]{2,1,0:T(8,128)S(1)}, f32[1,16,128,128]{3,2,1,0:T(8,128)})) conditional(s32[]{:T(128)} %convert_element_type.127, (f32[1,16,128]{2,1,0:T(8,128)S(1)}, f32[1,16,128]{2,1,0:T(8,128)S(1)}, f32[1,16,128,128]{3,2,1,0:T(8,128)}) %tuple.55, (s32[]{:T(128)}, s32[]{:T(128)}, ...), branch_computations={%region_6.6_spmd, %region_7.9_spmd} | conditional | flops 1101667456 | bytes 37365860 | solution.py:236
  318.5 1.3 fusion.2
  319.8 2.0 fusion.4
  321.9 3.6 fusion.12
  325.5 1.0 copy-done.4
  326.5 0.6 dynamic_slice.120
  328.3 8.8 %conditional.3 = ((f32[1,16,128]{2,1,0:T(8,128)S(1)}, f32[1,16,128]{2,1,0:T(8,128)S(1)}, f32[1,16,128,128]{3,2,1,0:T(8,128)})) conditional(s32[]{:T(128)} %convert_element_type.127, (f32[1,16,128]{2,1,0:T(8,128)S(1)}, f32[1,16,128]{2,1,0:T(8,128)S(1)}, f32[1,16,128,128]{3,2,1,0:T(8,128)}) %tuple.55, (s32[]{:T(128)}, s32[]{:T(128)}, ...), branch_computations={%region_6.6_spmd, %region_7.9_spmd} | conditional | flops 1101667456 | bytes 37365860 | solution.py:236
  329.2 1.3 fusion.2
  330.5 2.0 fusion.4
  332.6 3.6 fusion.12
  336.2 1.0 copy-done.4
  339.0 8.8 %conditional.3 = ((f32[1,16,128]{2,1,0:T(8,128)S(1)}, f32[1,16,128]{2,1,0:T(8,128)S(1)}, f32[1,16,128,128]{3,2,1,0:T(8,128)})) conditional(s32[]{:T(128)} %convert_element_type.127, (f32[1,16,128]{2,1,0:T(8,128)S(1)}, f32[1,16,128]{2,1,0:T(8,128)S(1)}, f32[1,16,128,128]{3,2,1,0:T(8,128)}) %tuple.55, (s32[]{:T(128)}, s32[]{:T(128)}, ...), branch_computations={%region_6.6_spmd, %region_7.9_spmd} | conditional | flops 1101667456 | bytes 37365860 | solution.py:236
  339.8 1.3 fusion.2
  341.2 2.0 fusion.4
  343.2 3.6 fusion.12
  346.8 1.0 copy-done.4
  347.8 1.7 fusion.67
  349.8 1.5 multiply_reduce_fusion
  352.0 1.5 collective-permute-start
  353.6 13.9 %collective-permute-done = bf16[128,2048]{1,0:T(8,128)(2,1)S(1)} collective-permute-done((bf16[128,2048]{1,0:T(8,128)(2,1)S(1)}, bf16[128,2048]{1,0:T(8,128)(2,1)S(1)}, u32[]{:S(2)}, u32[]{:S(2)}) %collective-permute-start) | collective-permute-done | bytes 524320 | tf_op jit(solution)/shard_map/ppermute | solution.py:96
  367.5 13.1 %fusion.27 = f32[128,4096]{1,0:T(8,128)S(1)} fusion(bf16[1,4096,4096]{2,1,0:T(8,128)(2,1)} %all-gather.2.cloned.1.call-done, bf16[128,2048]{1,0:T(8,128)(2,1)S(1)} %collective-permute-done, bf16[128,2048]{1,0:T(8,128)(2,1)S(1)} %get-tuple-element.274, pred[]{:T(512)S(6)} %eq.4), kind=kOutput, calls=%fused_computation.29 | convolution fusion | flops 4299685888 | bytes 36700160 | tf_op jit(solution)/shard_map/dot_general | solution.py:302
  380.7 0.9 collective-permute-start.1
  381.7 12.2 %collective-permute-done.1 = bf16[128,2048]{1,0:T(8,128)(2,1)S(1)} collective-permute-done((bf16[128,2048]{1,0:T(8,128)(2,1)S(1)}, bf16[128,2048]{1,0:T(8,128)(2,1)S(1)}, u32[]{:S(2)}, u32[]{:S(2)}) %collective-permute-start.1) | collective-permute-done | bytes 524320 | tf_op jit(solution)/shard_map/ppermute | solution.py:96
  394.1 1.3 collective-permute-start.2
  395.4 14.3 %collective-permute-done.2 = bf16[128,2048]{1,0:T(8,128)(2,1)S(1)} collective-permute-done((bf16[128,2048]{1,0:T(8,128)(2,1)S(1)}, bf16[128,2048]{1,0:T(8,128)(2,1)S(1)}, u32[]{:S(2)}, u32[]{:S(2)}) %collective-permute-start.2) | collective-permute-done | bytes 524320 | tf_op jit(solution)/shard_map/ppermute | solution.py:102
  409.7 1.2 fusion.64
  (119 shorter events, 11.5 us)
Async XLA Ops:
  6.5 210.2 %copy-start = (bf16[128,256]{1,0:T(8,128)(2,1)S(1)}, bf16[128,256]{1,0:T(8,128)(2,1)}, u32[]{:S(2)}) copy-start(bf16[128,256]{1,0:T(8,128)(2,1)} %param.21) | copy-start | bytes 196612
  6.5 13.3 %copy-start.8 = (bf16[128,256]{1,0:T(8,128)(2,1)S(1)}, bf16[128,256]{1,0:T(8,128)(2,1)}, u32[]{:S(2)}) copy-start(bf16[128,256]{1,0:T(8,128)(2,1)} %param.20) | copy-start | bytes 196612
  8.9 57.5 %all-to-all-start = ((f32[32,1,32]{2,1,0:T(1,128)}), f32[32,1,32]{2,1,0:T(1,128)S(1)}, u32[]{:S(2)}, u32[]{:S(2)}) async-start(f32[32,1,32]{2,1,0:T(1,128)} %broadcast_in_dim.208), calls=%async_computation | async-start | bytes 32768 | tf_op jit(solution)/shard_map/all_to_all | solution.py:43
  66.4 76.8 %all-to-all-start.1 = ((bf16[8,2,147456]{2,1,0:T(2,128)(2,1)}), bf16[8,2,147456]{2,1,0:T(2,128)(2,1)}, u32[]{:S(2)}, u32[]{:S(2)}) async-start(bf16[8,2,147456]{2,1,0:T(2,128)(2,1)} %reshape.511), calls=%async_computation.1 | async-start | bytes 9437184 | tf_op jit(solution)/shard_map/all_to_all | solution.py:43
  71.1 296.4 %all-gather.2.cloned.1.call-start = ((), (), s32[]{:S(2)}) async-start(), calls=%async_computation.3 | async-start | bytes 34603008 | tf_op jit(solution)/shard_map/all_gather | solution.py:304
  162.3 3.8 copy-start.2
  209.7 5.8 %copy-start.10 = (f32[64]{0:T(128)S(1)}, f32[64]{0:T(128)}, u32[]{:S(2)}) copy-start(f32[64]{0:T(128)} %param.24) | copy-start | bytes 772
  209.7 7.0 %copy-start.9 = (f32[128,64]{0,1:T(8,128)S(1)}, f32[128,64]{0,1:T(8,128)}, u32[]{:S(2)}) copy-start(f32[128,64]{0,1:T(8,128)} %param.22) | copy-start | bytes 98308
  209.7 61.1 %all-to-all-start.2 = ((bf16[4,2,262144]{2,1,0:T(2,128)(2,1)}), bf16[4,2,262144]{2,1,0:T(2,128)(2,1)}, u32[]{:S(2)}, u32[]{:S(2)}) async-start(bf16[4,2,262144]{2,1,0:T(2,128)(2,1)} %reshape.513), calls=%async_computation.2 | async-start | bytes 8388608 | tf_op jit(solution)/shard_map/all_to_all | solution.py:43
  291.0 4.4 %copy-start.5 = (f32[128,1,32,64]{0,3,2,1:T(8,128)S(1)}, f32[128,1,32,64]{0,3,2,1:T(8,128)}, u32[]{:S(2)}) copy-start(f32[128,1,32,64]{0,3,2,1:T(8,128)} %fusion.35) | copy-start | bytes 3145732
  309.2 2.0 copy-start.3
  314.8 1.0 copy-start.4
  319.8 2.0 copy-start.3
  325.5 1.0 copy-start.4
  330.5 2.0 copy-start.3
  336.2 1.0 copy-start.4
  341.2 2.0 copy-start.3
  346.8 1.0 copy-start.4
  347.8 3.5 copy-start.6
  347.8 3.6 dynamic-slice-start
  352.0 15.5 %collective-permute-start = (bf16[128,2048]{1,0:T(8,128)(2,1)S(1)}, bf16[128,2048]{1,0:T(8,128)(2,1)S(1)}, u32[]{:S(2)}, u32[]{:S(2)}) collective-permute-start(bf16[128,2048]{1,0:T(8,128)(2,1)S(1)} %get-tuple-element.275), channel_id=1, source_target_pairs={{0,64},{64,0},{1,65},{65,1},{2,66},{66,2},{3,67},{67,3},{4,68},{68... | collective-permute-start | bytes 1572872 | tf_op jit(solution)/shard_map/ppermute | solution.py:96
  367.5 26.3 %copy-start.7 = (bf16[128,2048]{1,0:T(8,128)(2,1)S(1)}, bf16[128,2048]{1,0:T(8,128)(2,1)}, u32[]{:S(2)}) copy-start(bf16[128,2048]{1,0:T(8,128)(2,1)} %param.17) | copy-start | bytes 1572868
  380.6 30.2 %copy-start.1 = (bf16[128,256]{1,0:T(8,128)(2,1)S(1)}, bf16[128,256]{1,0:T(8,128)(2,1)}, u32[]{:S(2)}) copy-start(bf16[128,256]{1,0:T(8,128)(2,1)} %param.21) | copy-start | bytes 196612
  380.7 13.1 %collective-permute-start.1 = (bf16[128,2048]{1,0:T(8,128)(2,1)S(1)}, bf16[128,2048]{1,0:T(8,128)(2,1)S(1)}, u32[]{:S(2)}, u32[]{:S(2)}) collective-permute-start(bf16[128,2048]{1,0:T(8,128)(2,1)S(1)} %select_convert_fusion), channel_id=1, source_target_pairs={{0,1},{1,0},{2,3},{3,2},{4,5},{5,4},{6,7},{7,6},{8,9},{9,8},{10,11... | collective-permute-start | bytes 1572872 | tf_op jit(solution)/shard_map/ppermute | solution.py:96
  394.1 15.6 %collective-permute-start.2 = (bf16[128,2048]{1,0:T(8,128)(2,1)S(1)}, bf16[128,2048]{1,0:T(8,128)(2,1)S(1)}, u32[]{:S(2)}, u32[]{:S(2)}) collective-permute-start(bf16[128,2048]{1,0:T(8,128)(2,1)S(1)} %add_convert_fusion.1), channel_id=1, source_target_pairs={{0,64},{1,65},{2,66},{3,67},{4,68},{5,69},{6,70},{7,71},{8,72},{9,... | collective-permute-start | bytes 1572872 | tf_op jit(solution)/shard_map/ppermute | solution.py:102
Sparse Core Ops, SparseCore 0:
  81.8 157.4 all-gather.1

commit v5 on v4

--- a/solution.py
+++ b/solution.py
@@ -58,13 +58,18 @@
         return jnp.where((k < upto)[:, None, None], jnp.exp(summed), 0.0)
 
     first = lax.axis_index("y") * inner
-    state_size = local_state.size
+    lanes = local_state.shape[-1]
+    state_rows = local_state.size // lanes
+    rider_rows = riders.size // lanes
     payload = jnp.concatenate(
-        [local_state.astype(jnp.bfloat16).reshape(-1), riders.reshape(-1)]
+        [
+            local_state.astype(jnp.bfloat16).reshape(state_rows, lanes),
+            riders.reshape(riders.shape[0], -1, lanes).reshape(rider_rows, lanes),
+        ]
     )
     near_all = gathered(payload, "zc")
-    near = near_all[:, :state_size].reshape((inner,) + local_state.shape).astype(jnp.float32)
-    near_riders = near_all[:, state_size:]
+    near = near_all[:, :state_rows].reshape((inner,) + local_state.shape).astype(jnp.float32)
+    near_riders = near_all[:, state_rows:].reshape(inner * rider_rows, lanes)
     near_ids = first + jnp.arange(inner, dtype=jnp.int32)
     own_part = jnp.einsum(
         "kgj,kgjpn->gjpn", span_weight(near_ids, rank), near, precision=exact_mode
@@ -74,11 +79,13 @@
         "kgj,kgjpn->gjpn", span_weight(near_ids, group_end), near, precision=exact_mode
     )
     payload = jnp.concatenate(
-        [group_total.astype(jnp.bfloat16).reshape(-1), near_riders.reshape(-1)]
+        [group_total.astype(jnp.bfloat16).reshape(state_rows, lanes), near_riders]
     )
     far_all = gathered(payload, "y")
-    far = far_all[:, :state_size].reshape((outer,) + local_state.shape).astype(jnp.float32)
-    all_riders = far_all[:, state_size:].reshape((peers * riders.shape[0],) + riders.shape[1:])
+    far = far_all[:, :state_rows].reshape((outer,) + local_state.shape).astype(jnp.float32)
+    all_riders = far_all[:, state_rows:].reshape(
+        (peers * riders.shape[0], -1, lanes)
+    ).reshape(peers * riders.shape[0], riders.shape[1])
     far_ends = (jnp.arange(outer, dtype=jnp.int32) + 1) * inner - 1
     far_weight = span_weight(far_ends, rank)
     far_weight = jnp.where((far_ends < first)[:, None, None], far_weight, 0.0)

time: 426 us -> 339 us (0.80); the launches traced: 418 us -> 338 us
  other arithmetic: 76.7 us -> 17.7 us
  local copies, waits for them, and re-layouts: 92.4 us -> 35.6 us
  waiting for transfers between devices: 146 us -> 186 us
  starting transfers between devices: 32.7 us -> 26.1 us
    broadcast_in_dim x2 -> x0, other arithmetic: 58.8 us -> none  [gathered(): spread = jnp.broadcast_to(x[None], (peers,) + x.shape)]
    unnamed x30 -> x25, local copies, waits for them, and re-layouts: 55.6 us -> 2.68 us
    all_to_all x3, waiting for transfers between devices: 105 us -> 148 us  [gathered(): return lax.all_to_all(spread, axis, 0, 0)]
    all_gather x1, starting transfers between devices: 10.6 us -> 0.03 us  [per_device(): lax.all_gather(out_weights, CTX, axis=2, tiled=True)[0]]
    broadcast_in_dim x5 -> x4, local copies, waits for them, and re-layouts: 12.9 us -> 5.96 us  [gathered(): spread = jnp.broadcast_to(x[None], (peers,) + x.shape)]
    reshape x1 -> x0, local copies, waits for them, and re-layouts: 4.9 us -> none  [entering_states(): far_all[:, state_size:]]
    slice x2 -> x3, local copies, waits for them, and re-layouts: 2.8 us -> 7.68 us  [the longest x1 4.09 us: entering_states(): far_all[:, :state_rows].reshape((outer,) + local_state.shape)]
  transfers between devices with their start and end apart: 7 -> 7, of which waited for: 5 -> 6; matrix products, arithmetic and copies ran while one was open for 48% -> 25% of each run, Pallas kernels for 0% -> 0%
where the time goes in v5:
time: 339 us; the launch traced here: 338 us
  waiting for transfers between devices  186 us (55%)
  matrix products  53.5 us (16%)
  local copies, waits for them, and re-layouts  35.6 us (11%)
  starting transfers between devices  26.1 us (8%)
  other arithmetic  17.7 us (5%)
  between operations  13.8 us (4%)
  loops' own time  5.42 us (2%)
    all_to_all x3, waiting for transfers between devices, gathered(): return lax.all_to_all(spread, axis, 0, 0)  148 us
    ppermute x2, waiting for transfers between devices, from_partner(): return lax.ppermute(block, axis, route)  24.5 us
    all_to_all x3, starting transfers between devices, gathered(): return lax.all_to_all(spread, axis, 0, 0)  22.3 us
    dot_general x4, matrix products, absorb(): jnp.einsum('gjqk,kgd->gjqd', weights_exp.astype(jnp.bfloat16), value_rows...  14.4 us
    ppermute x1, waiting for transfers between devices, shifted(): return lax.ppermute(x, axis, pairs)  13.5 us
    dot_general x1, matrix products, per_device(): jnp.dot(mixed_rows, lax.all_gather(out_weights, CTX, axis=2, tiled=True)[...  13 us
    reduce_sum x4, other arithmetic, absorb(): row_sum = row_sum * rescale + jnp.sum(weights_exp, axis=-1)  8.01 us
    dot_general x1, matrix products, entering_states(): jnp.einsum('kgj,kgjpn->gjpn', span_weight(near_ids, rank), near, precisio...  7.18 us
  transfers between devices with their start and end apart: 7, of which 6 were waited for; matrix products, arithmetic and copies ran while one was open for 25% of the time, Pallas kernels for 0%

profile of v5, /device:TPU:30, one launch (start us, length us, event | category | flops | bytes accessed | tf_op | source)
XLA Modules:
  0.0 338.4 jit_solution(10145964316424700718)
XLA Ops:
  6.6 0.7 all-gather.2.cloned.1.call-update
  7.3 0.7 constant_dynamic-slice_fusion.3
  8.1 0.7 dynamic_slice.71
  9.0 0.6 broadcast_in_dim.208
  9.6 8.4 %all-to-all-start = ((f32[32,1,32]{2,1,0:T(1,128)}), f32[32,1,32]{2,1,0:T(1,128)S(1)}, u32[]{:S(2)}, u32[]{:S(2)}) async-start(f32[32,1,32]{2,1,0:T(1,128)} %broadcast_in_dim.208), calls=%async_computation | async-start | bytes 32768 | tf_op jit(solution)/shard_map/all_to_all | solution.py:43
  18.1 1.3 constant_dynamic-slice_fusion
  19.8 0.7 fusion.49
  20.5 2.9 all-to-all-done
  23.4 2.9 broadcast_in_dim.214
  26.3 4.6 %all-to-all-start.1 = ((bf16[8,2304,128]{2,1,0:T(8,128)(2,1)}), bf16[8,2304,128]{2,1,0:T(8,128)(2,1)}, u32[]{:S(2)}, u32[]{:S(2)}) async-start(bf16[8,2304,128]{2,1,0:T(8,128)(2,1)} %broadcast_in_dim.214), calls=%async_computation.1 | async-start | bytes 9437184 | tf_op jit(solution)/shard_map/all_to_all | solution.py:43
  31.3 82.1 %all-to-all-done.1 = bf16[8,2304,128]{2,1,0:T(8,128)(2,1)} async-done(((bf16[8,2304,128]{2,1,0:T(8,128)(2,1)}), bf16[8,2304,128]{2,1,0:T(8,128)(2,1)}, u32[]{:S(2)}, u32[]{:S(2)}) %all-to-all-start.1) | async-done | bytes 4718624 | tf_op jit(solution)/shard_map/all_to_all | solution.py:43
  113.5 2.5 slice.46
  116.0 2.0 copy-done.2
  118.0 4.6 %fusion.29 = f32[32,1,64,128]{3,1,2,0:T(1,128)S(1)} fusion(f32[8,32,1,1]{0,2,3,1:T(1,128)S(1)} %copy.79, bf16[8,32,64,128]{3,2,1,0:T(8,128)(2,1)S(1)} %bitcast.153), kind=kOutput, calls=%fused_computation.31 | convolution fusion | flops 25165824 | bytes 5243904 | tf_op jit(solution)/shard_map/kgj,kgjpn->gjpn/dot_general | solution.py:78
  122.7 1.1 slice.47
  123.9 2.5 broadcast_in_dim.223
  126.4 9.3 %all-to-all-start.2 = ((bf16[4,4096,128]{2,1,0:T(8,128)(2,1)}), bf16[4,4096,128]{2,1,0:T(8,128)(2,1)}, u32[]{:S(2)}, u32[]{:S(2)}) async-start(bf16[4,4096,128]{2,1,0:T(8,128)(2,1)} %broadcast_in_dim.223), calls=%async_computation.2 | async-start | bytes 8388608 | tf_op jit(solution)/shard_map/all_to_all | solution.py:43
  136.7 0.7 slice.39
  137.6 3.4 %fusion.41 = f32[128,1,32,64]{0,3,2,1:T(8,128)} fusion(bf16[128,32,64]{0,2,1:T(8,128)(2,1)S(1)} %bitcast.164, f32[32,128]{1,0:T(8,128)S(1)} %fusion.100, f32[128,32]{0,1:T(8,128)S(1)} %copy.65, f32[128,128]{1,0:T(8,128)S(1)} %fusion.78, pred[128,128]{1,0:T(8,128)(4,1)S(1)} %iota_compare_fusion), kind=kOutput, calls=%fused_computation.44 | convolution fusion | flops 404750336 | bytes 1687552 | tf_op jit(solution)/shard_map/while/body/eval_jaxpr/gjts,sgjp->tgjp/dot_general | solution.py:126
  141.5 7.2 %fusion.31 = f32[32,1,64,128]{3,1,2,0:T(1,128)S(1)} fusion(f32[8,32,1,1]{0,2,3,1:T(1,128)S(1)} %copy.76, bf16[8,32,64,128]{3,2,1,0:T(8,128)(2,1)} %bitcast.154), kind=kOutput, calls=%fused_computation.33 | convolution fusion | flops 25165824 | bytes 5243904 | tf_op jit(solution)/shard_map/kgj,kgjpn->gjpn/dot_general | solution.py:74
  148.6 62.6 %all-to-all-done.2 = bf16[4,4096,128]{2,1,0:T(8,128)(2,1)} async-done(((bf16[4,4096,128]{2,1,0:T(8,128)(2,1)}), bf16[4,4096,128]{2,1,0:T(8,128)(2,1)}, u32[]{:S(2)}, u32[]{:S(2)}) %all-to-all-start.2) | async-done | bytes 4194336 | tf_op jit(solution)/shard_map/all_to_all | solution.py:43
  211.3 4.1 %fusion.93 = (bf16[4,2048,128]{2,1,0:T(8,128)(2,1)S(1)}, bf16[4,2048,128]{2,1,0:T(8,128)(2,1)}) fusion(bf16[4,4096,128]{2,1,0:T(8,128)(2,1)} %all-to-all-done.2), kind=kLoop, calls=%fused_computation.141 | loop fusion | bytes 8388608 | tf_op jit(solution)/shard_map/slice | solution.py:85
  215.4 3.7 %fusion.39 = f32[32,1,64,128]{3,1,2,0:T(1,128)S(1)} fusion(f32[4,32,1,1]{0,2,3,1:T(1,128)S(1)} %copy.81, bf16[4,32,64,128]{3,2,1,0:T(8,128)(2,1)S(1)} %bitcast.169), kind=kOutput, calls=%fused_computation.42 | convolution fusion | flops 12582912 | bytes 3146240 | tf_op jit(solution)/shard_map/kgj,kgjpn->gjpn/dot_general | solution.py:92
  219.1 0.7 fusion.48
  219.7 0.6 fusion.47
  220.7 4.1 %reshape_reshape.7 = bf16[4096,256]{1,0:T(8,128)(2,1)} reshape(bf16[4,2048,128]{2,1,0:T(8,128)(2,1)} %get-tuple-element.263) | data formatting | bytes 4194304 | tf_op jit(solution)/shard_map/reshape;reshape | solution.py:88
  224.8 2.6 fusion.94
  227.4 1.1 broadcast_in_dim.226
  228.5 42.5 %while.4 = (s32[]{:T(128)}, f32[1,16,128]{2,1,0:T(8,128)S(1)}, f32[1,16,128]{2,1,0:T(8,128)S(1)}, f32[1,16,128,128]{3,2,1,0:T(8,128)}, s32[4]{0:T(128)S(1)}, /*i...) while((s32[]{:T(128)}, f32[1,16,128]{2,1,0:T(8,128)S(1)}, ...), condition=%wide.region_10.11_spmd.clone, body=%wide.region_5.10_spmd.clone.sunk | while | flops 1101667456 | bytes 37366608 | solution.py:259
  228.5 0.6 dynamic_slice.120
  230.4 8.8 %conditional.3 = ((f32[1,16,128]{2,1,0:T(8,128)S(1)}, f32[1,16,128]{2,1,0:T(8,128)S(1)}, f32[1,16,128,128]{3,2,1,0:T(8,128)})) conditional(s32[]{:T(128)} %convert_element_type.127, (f32[1,16,128]{2,1,0:T(8,128)S(1)}, f32[1,16,128]{2,1,0:T(8,128)S(1)}, f32[1,16,128,128]{3,2,1,0:T(8,128)}) %tuple.54, (s32[]{:T(128)}, s32[]{:T(128)}, ...), branch_computations={%region_6.6_spmd, %region_7.9_spmd} | conditional | flops 1101667456 | bytes 37365860 | solution.py:243
  231.2 1.3 fusion.2
  232.5 2.0 fusion.4
  234.6 3.6 %fusion.12 = f32[1,16,128,128]{3,2,1,0:T(8,128)S(1)} fusion(f32[1024,128,16]{1,0,2:T(8,128)S(1)} %get-tuple-element.261, f32[16,128]{1,0:T(8,128)S(1)} %bitcast.161, pred[128,1024]{0,1:T(8,128)(4,1)S(1)} %broadcast_compare_fusion, f32[1,16,128,128]{3,2,1,0:T(8,128)S(1)} %copy-done.3, f32[16,128]{1,0:T(8,128)S(1)} %get-tuple-element.258, ...), kind=kOutput, calls=%fused_computation.10 | convolution fusion | flops 547880960 | bytes 10895872 | tf_op jit(solution)/shard_map/while/body/eval_jaxpr/cond/branch_1_fun/gjqk,kgd->gjqd/dot_general | solution.py:235
  238.2 1.0 copy-done.4
  239.2 0.6 dynamic_slice.120
  241.0 8.8 %conditional.3 = ((f32[1,16,128]{2,1,0:T(8,128)S(1)}, f32[1,16,128]{2,1,0:T(8,128)S(1)}, f32[1,16,128,128]{3,2,1,0:T(8,128)})) conditional(s32[]{:T(128)} %convert_element_type.127, (f32[1,16,128]{2,1,0:T(8,128)S(1)}, f32[1,16,128]{2,1,0:T(8,128)S(1)}, f32[1,16,128,128]{3,2,1,0:T(8,128)}) %tuple.54, (s32[]{:T(128)}, s32[]{:T(128)}, ...), branch_computations={%region_6.6_spmd, %region_7.9_spmd} | conditional | flops 1101667456 | bytes 37365860 | solution.py:243
  241.8 1.3 fusion.2
  243.2 2.0 fusion.4
  245.2 3.6 %fusion.12 = f32[1,16,128,128]{3,2,1,0:T(8,128)S(1)} fusion(f32[1024,128,16]{1,0,2:T(8,128)S(1)} %get-tuple-element.261, f32[16,128]{1,0:T(8,128)S(1)} %bitcast.161, pred[128,1024]{0,1:T(8,128)(4,1)S(1)} %broadcast_compare_fusion, f32[1,16,128,128]{3,2,1,0:T(8,128)S(1)} %copy-done.3, f32[16,128]{1,0:T(8,128)S(1)} %get-tuple-element.258, ...), kind=kOutput, calls=%fused_computation.10 | convolution fusion | flops 547880960 | bytes 10895872 | tf_op jit(solution)/shard_map/while/body/eval_jaxpr/cond/branch_1_fun/gjqk,kgd->gjqd/dot_general | solution.py:235
  248.8 1.0 copy-done.4
  249.8 0.6 dynamic_slice.120
  251.6 8.8 %conditional.3 = ((f32[1,16,128]{2,1,0:T(8,128)S(1)}, f32[1,16,128]{2,1,0:T(8,128)S(1)}, f32[1,16,128,128]{3,2,1,0:T(8,128)})) conditional(s32[]{:T(128)} %convert_element_type.127, (f32[1,16,128]{2,1,0:T(8,128)S(1)}, f32[1,16,128]{2,1,0:T(8,128)S(1)}, f32[1,16,128,128]{3,2,1,0:T(8,128)}) %tuple.54, (s32[]{:T(128)}, s32[]{:T(128)}, ...), branch_computations={%region_6.6_spmd, %region_7.9_spmd} | conditional | flops 1101667456 | bytes 37365860 | solution.py:243
  252.5 1.3 fusion.2
  253.8 2.0 fusion.4
  255.8 3.6 %fusion.12 = f32[1,16,128,128]{3,2,1,0:T(8,128)S(1)} fusion(f32[1024,128,16]{1,0,2:T(8,128)S(1)} %get-tuple-element.261, f32[16,128]{1,0:T(8,128)S(1)} %bitcast.161, pred[128,1024]{0,1:T(8,128)(4,1)S(1)} %broadcast_compare_fusion, f32[1,16,128,128]{3,2,1,0:T(8,128)S(1)} %copy-done.3, f32[16,128]{1,0:T(8,128)S(1)} %get-tuple-element.258, ...), kind=kOutput, calls=%fused_computation.10 | convolution fusion | flops 547880960 | bytes 10895872 | tf_op jit(solution)/shard_map/while/body/eval_jaxpr/cond/branch_1_fun/gjqk,kgd->gjqd/dot_general | solution.py:235
  259.4 1.0 copy-done.4
  260.4 0.6 dynamic_slice.120
  262.3 8.8 %conditional.3 = ((f32[1,16,128]{2,1,0:T(8,128)S(1)}, f32[1,16,128]{2,1,0:T(8,128)S(1)}, f32[1,16,128,128]{3,2,1,0:T(8,128)})) conditional(s32[]{:T(128)} %convert_element_type.127, (f32[1,16,128]{2,1,0:T(8,128)S(1)}, f32[1,16,128]{2,1,0:T(8,128)S(1)}, f32[1,16,128,128]{3,2,1,0:T(8,128)}) %tuple.54, (s32[]{:T(128)}, s32[]{:T(128)}, ...), branch_computations={%region_6.6_spmd, %region_7.9_spmd} | conditional | flops 1101667456 | bytes 37365860 | solution.py:243
  263.1 1.3 fusion.2
  264.4 2.0 fusion.4
  266.5 3.6 %fusion.12 = f32[1,16,128,128]{3,2,1,0:T(8,128)S(1)} fusion(f32[1024,128,16]{1,0,2:T(8,128)S(1)} %get-tuple-element.261, f32[16,128]{1,0:T(8,128)S(1)} %bitcast.161, pred[128,1024]{0,1:T(8,128)(4,1)S(1)} %broadcast_compare_fusion, f32[1,16,128,128]{3,2,1,0:T(8,128)S(1)} %copy-done.3, f32[16,128]{1,0:T(8,128)S(1)} %get-tuple-element.258, ...), kind=kOutput, calls=%fused_computation.10 | convolution fusion | flops 547880960 | bytes 10895872 | tf_op jit(solution)/shard_map/while/body/eval_jaxpr/cond/branch_1_fun/gjqk,kgd->gjqd/dot_general | solution.py:235
  270.1 1.0 copy-done.4
  271.1 1.7 fusion.73
  273.1 1.5 multiply_reduce_fusion
  274.6 0.6 bitcast_select_fusion.2
  275.3 1.5 collective-permute-start
  276.8 13.1 %collective-permute-done = bf16[128,2048]{1,0:T(8,128)(2,1)S(1)} collective-permute-done((bf16[128,2048]{1,0:T(8,128)(2,1)S(1)}, bf16[128,2048]{1,0:T(8,128)(2,1)S(1)}, u32[]{:S(2)}, u32[]{:S(2)}) %collective-permute-start) | collective-permute-done | bytes 524320 | tf_op jit(solution)/shard_map/ppermute | solution.py:103
  289.9 13.0 %fusion.27 = f32[128,4096]{1,0:T(8,128)S(1)} fusion(bf16[1,4096,4096]{2,1,0:T(8,128)(2,1)} %all-gather.2.cloned.1.call-done, bf16[128,2048]{1,0:T(8,128)(2,1)S(1)} %collective-permute-done, bf16[128,2048]{1,0:T(8,128)(2,1)S(1)} %get-tuple-element.264, pred[]{:T(512)S(6)} %eq.4), kind=kOutput, calls=%fused_computation.29 | convolution fusion | flops 4299685888 | bytes 36700160 | tf_op jit(solution)/shard_map/dot_general | solution.py:309
  303.0 0.9 collective-permute-start.1
  304.0 11.4 %collective-permute-done.1 = bf16[128,2048]{1,0:T(8,128)(2,1)S(1)} collective-permute-done((bf16[128,2048]{1,0:T(8,128)(2,1)S(1)}, bf16[128,2048]{1,0:T(8,128)(2,1)S(1)}, u32[]{:S(2)}, u32[]{:S(2)}) %collective-permute-start.1) | collective-permute-done | bytes 524320 | tf_op jit(solution)/shard_map/ppermute | solution.py:103
  315.6 1.3 collective-permute-start.2
  316.9 13.5 %collective-permute-done.2 = bf16[128,2048]{1,0:T(8,128)(2,1)S(1)} collective-permute-done((bf16[128,2048]{1,0:T(8,128)(2,1)S(1)}, bf16[128,2048]{1,0:T(8,128)(2,1)S(1)}, u32[]{:S(2)}, u32[]{:S(2)}) %collective-permute-start.2) | collective-permute-done | bytes 524320 | tf_op jit(solution)/shard_map/ppermute | solution.py:109
  330.4 1.2 fusion.70
  (113 shorter events, 7.3 us)
Async XLA Ops:
  6.5 130.9 %copy-start = (bf16[128,256]{1,0:T(8,128)(2,1)S(1)}, bf16[128,256]{1,0:T(8,128)(2,1)}, u32[]{:S(2)}) copy-start(bf16[128,256]{1,0:T(8,128)(2,1)} %param.21) | copy-start | bytes 196612
  6.5 13.1 %copy-start.11 = (bf16[128,256]{1,0:T(8,128)(2,1)S(1)}, bf16[128,256]{1,0:T(8,128)(2,1)}, u32[]{:S(2)}) copy-start(bf16[128,256]{1,0:T(8,128)(2,1)} %param.27) | copy-start | bytes 196612
  6.5 13.2 %copy-start.10 = (bf16[128,256]{1,0:T(8,128)(2,1)S(1)}, bf16[128,256]{1,0:T(8,128)(2,1)}, u32[]{:S(2)}) copy-start(bf16[128,256]{1,0:T(8,128)(2,1)} %param.28) | copy-start | bytes 196612
  6.5 13.2 %copy-start.8 = (bf16[128,256]{1,0:T(8,128)(2,1)S(1)}, bf16[128,256]{1,0:T(8,128)(2,1)}, u32[]{:S(2)}) copy-start(bf16[128,256]{1,0:T(8,128)(2,1)} %param.20) | copy-start | bytes 196612
  6.5 283.4 %all-gather.2.cloned.1.call-start = ((), (), s32[]{:S(2)}) async-start(), calls=%async_computation.3 | async-start | bytes 34603008 | tf_op jit(solution)/shard_map/all_gather | solution.py:311
  9.6 13.8 %all-to-all-start = ((f32[32,1,32]{2,1,0:T(1,128)}), f32[32,1,32]{2,1,0:T(1,128)S(1)}, u32[]{:S(2)}, u32[]{:S(2)}) async-start(f32[32,1,32]{2,1,0:T(1,128)} %broadcast_in_dim.208), calls=%async_computation | async-start | bytes 32768 | tf_op jit(solution)/shard_map/all_to_all | solution.py:43
  26.3 87.2 %all-to-all-start.1 = ((bf16[8,2304,128]{2,1,0:T(8,128)(2,1)}), bf16[8,2304,128]{2,1,0:T(8,128)(2,1)}, u32[]{:S(2)}, u32[]{:S(2)}) async-start(bf16[8,2304,128]{2,1,0:T(8,128)(2,1)} %broadcast_in_dim.214), calls=%async_computation.1 | async-start | bytes 9437184 | tf_op jit(solution)/shard_map/all_to_all | solution.py:43
  116.0 2.0 copy-start.2
  126.4 9.7 %copy-start.12 = (f32[64]{0:T(128)S(1)}, f32[64]{0:T(128)}, u32[]{:S(2)}) copy-start(f32[64]{0:T(128)} %param.24) | copy-start | bytes 772
  126.4 11.0 %copy-start.9 = (f32[128,64]{0,1:T(8,128)S(1)}, f32[128,64]{0,1:T(8,128)}, u32[]{:S(2)}) copy-start(f32[128,64]{0,1:T(8,128)} %param.22) | copy-start | bytes 98308
  126.4 84.9 %all-to-all-start.2 = ((bf16[4,4096,128]{2,1,0:T(8,128)(2,1)}), bf16[4,4096,128]{2,1,0:T(8,128)(2,1)}, u32[]{:S(2)}, u32[]{:S(2)}) async-start(bf16[4,4096,128]{2,1,0:T(8,128)(2,1)} %broadcast_in_dim.223), calls=%async_computation.2 | async-start | bytes 8388608 | tf_op jit(solution)/shard_map/all_to_all | solution.py:43
  215.4 4.3 %copy-start.5 = (f32[128,1,32,64]{0,3,2,1:T(8,128)S(1)}, f32[128,1,32,64]{0,3,2,1:T(8,128)}, u32[]{:S(2)}) copy-start(f32[128,1,32,64]{0,3,2,1:T(8,128)} %fusion.41) | copy-start | bytes 3145732
  232.5 2.0 copy-start.3
  238.2 1.0 copy-start.4
  243.2 2.0 copy-start.3
  248.8 1.0 copy-start.4
  253.8 2.0 copy-start.3
  259.4 1.0 copy-start.4
  264.4 2.0 copy-start.3
  270.1 1.0 copy-start.4
  271.1 3.5 %copy-start.6 = (bf16[128,4096]{1,0:T(8,128)(2,1)S(1)}, bf16[128,4096]{1,0:T(8,128)(2,1)}, u32[]{:S(2)}) copy-start(bf16[128,4096]{1,0:T(8,128)(2,1)} %param.19) | copy-start | bytes 3145732
  271.1 3.6 %dynamic-slice-start = ((f32[4096]{0:T(1024)}, s32[]{:T(128)}), f32[2048]{0:T(1024)S(1)}, s32[]{:S(2)}) async-start(f32[4096]{0:T(1024)} %param.25, s32[]{:T(128)} %select_n.140), calls=%async_computation.4 | async-start | bytes 16896 | tf_op jit(solution)/shard_map/dynamic_slice | solution.py:267
  275.3 14.7 %collective-permute-start = (bf16[128,2048]{1,0:T(8,128)(2,1)S(1)}, bf16[128,2048]{1,0:T(8,128)(2,1)S(1)}, u32[]{:S(2)}, u32[]{:S(2)}) collective-permute-start(bf16[128,2048]{1,0:T(8,128)(2,1)S(1)} %get-tuple-element.265), channel_id=1, source_target_pairs={{0,64},{64,0},{1,65},{65,1},{2,66},{66,2},{3,67},{67,3},{4,68},{68... | collective-permute-start | bytes 1572872 | tf_op jit(solution)/shard_map/ppermute | solution.py:103
  289.9 25.4 %copy-start.7 = (bf16[128,2048]{1,0:T(8,128)(2,1)S(1)}, bf16[128,2048]{1,0:T(8,128)(2,1)}, u32[]{:S(2)}) copy-start(bf16[128,2048]{1,0:T(8,128)(2,1)} %param.17) | copy-start | bytes 1572868
  302.9 28.7 %copy-start.1 = (bf16[128,256]{1,0:T(8,128)(2,1)S(1)}, bf16[128,256]{1,0:T(8,128)(2,1)}, u32[]{:S(2)}) copy-start(bf16[128,256]{1,0:T(8,128)(2,1)} %param.21) | copy-start | bytes 196612
  303.0 12.3 %collective-permute-start.1 = (bf16[128,2048]{1,0:T(8,128)(2,1)S(1)}, bf16[128,2048]{1,0:T(8,128)(2,1)S(1)}, u32[]{:S(2)}, u32[]{:S(2)}) collective-permute-start(bf16[128,2048]{1,0:T(8,128)(2,1)S(1)} %select_convert_fusion), channel_id=1, source_target_pairs={{0,1},{1,0},{2,3},{3,2},{4,5},{5,4},{6,7},{7,6},{8,9},{9,8},{10,11... | collective-permute-start | bytes 1572872 | tf_op jit(solution)/shard_map/ppermute | solution.py:103
  315.6 14.8 %collective-permute-start.2 = (bf16[128,2048]{1,0:T(8,128)(2,1)S(1)}, bf16[128,2048]{1,0:T(8,128)(2,1)S(1)}, u32[]{:S(2)}, u32[]{:S(2)}) collective-permute-start(bf16[128,2048]{1,0:T(8,128)(2,1)S(1)} %add_convert_fusion.1), channel_id=1, source_target_pairs={{0,64},{1,65},{2,66},{3,67},{4,68},{5,69},{6,70},{7,71},{8,72},{9,... | collective-permute-start | bytes 1572872 | tf_op jit(solution)/shard_map/ppermute | solution.py:109
Sparse Core Ops, SparseCore 0:
  9.5 204.6 all-gather.1

commit v6 on v5

--- a/solution.py
+++ b/solution.py
@@ -306,16 +306,20 @@
         jnp.concatenate([kept_half, incoming], axis=1),
         jnp.concatenate([incoming, kept_half], axis=1),
     )
-    partial_value = jnp.dot(
-        mixed_rows,
-        lax.all_gather(out_weights, CTX, axis=2, tiled=True)[0],
-        preferred_element_type=jnp.float32,
+    inner = lax.axis_size("zc")
+    tp_rank = lax.axis_index("tp")
+    rows = lax.all_gather(mixed_rows, "zc", axis=0, tiled=True)
+    columns = lax.all_gather(out_weights[0], "y", axis=0)
+    partial_value = jnp.einsum(
+        "tc,ycr->tyr", rows, columns, preferred_element_type=jnp.float32
     )
     half = partial_value.shape[1] // 2
-    tp_rank = lax.axis_index("tp")
     kept = jnp.where(tp_rank == 0, partial_value[:, :half], partial_value[:, half:])
     sent = jnp.where(tp_rank == 0, partial_value[:, half:], partial_value[:, :half])
-    projected = kept + from_partner(sent.astype(jnp.bfloat16), "tp", 0).astype(jnp.float32)
+    summed = kept + from_partner(sent.astype(jnp.bfloat16), "tp", 0).astype(jnp.float32)
+    pieces = summed.reshape((inner, -1) + summed.shape[1:]).astype(jnp.bfloat16)
+    pieces = lax.all_to_all(pieces, "zc", 0, 0)
+    projected = pieces.transpose(1, 2, 0, 3).reshape(pieces.shape[1], -1).astype(jnp.float32)
     own_section = (resid_in.astype(jnp.float32) + projected).astype(jnp.bfloat16)
     received = shifted(own_section, "pipe", 1)
     second_section = (received.astype(jnp.float32) + projected).astype(jnp.bfloat16)

time: 339 us -> 375 us (1.11)
  waiting for transfers between devices: 186 us -> 210 us
  blocking collectives: 0 us -> 13.5 us
  matrix products: 53.5 us -> 48.6 us
    all_gather x1 -> x2, waiting for transfers between devices: 0.01 us -> 48.4 us  [the longest x1 48.4 us: per_device(): rows = lax.all_gather(mixed_rows, 'zc', axis=0, tiled=True)]
    all_to_all x3, waiting for transfers between devices: 148 us -> 123 us  [gathered(): return lax.all_to_all(spread, axis, 0, 0)]
    all_to_all x0 -> x1, blocking collectives: none -> 13.5 us  [per_device(): pieces = lax.all_to_all(pieces, 'zc', 0, 0)]
    dot_general x1, matrix products: 13 us -> 8.14 us  [per_device(): jnp.einsum('tc,ycr->tyr', rows, columns, preferred_element_type=jnp.float32)]
  transfers between devices with their start and end apart: 7 -> 8, of which waited for: 6 -> 7; matrix products, arithmetic and copies ran while one was open for 25% -> 19% of each run, Pallas kernels for 0% -> 0%
where the time goes in v6:
time: 375 us; the launch traced here: 373 us
  waiting for transfers between devices  210 us (56%)
  matrix products  48.6 us (13%)
  local copies, waits for them, and re-layouts  37.4 us (10%)
  starting transfers between devices  23.9 us (6%)
  other arithmetic  20.2 us (5%)
  between operations  13.8 us (4%)
  blocking collectives  13.5 us (4%)
  loops' own time  5.62 us (1%)
    all_to_all x3, waiting for transfers between devices, gathered(): return lax.all_to_all(spread, axis, 0, 0)  123 us
    all_gather x1, waiting for transfers between devices, per_device(): rows = lax.all_gather(mixed_rows, 'zc', axis=0, tiled=True)  48.4 us
    ppermute x2, waiting for transfers between devices, from_partner(): return lax.ppermute(block, axis, route)  23 us
    all_to_all x3, starting transfers between devices, gathered(): return lax.all_to_all(spread, axis, 0, 0)  20 us
    ppermute x1, waiting for transfers between devices, shifted(): return lax.ppermute(x, axis, pairs)  15.4 us
    dot_general x4, matrix products, absorb(): jnp.einsum('gjqk,kgd->gjqd', weights_exp.astype(jnp.bfloat16), value_rows...  14.3 us
    all_to_all x1, blocking collectives, per_device(): pieces = lax.all_to_all(pieces, 'zc', 0, 0)  13.5 us
    dot_general x1, matrix products, per_device(): jnp.einsum('tc,ycr->tyr', rows, columns, preferred_element_type=jnp.float32)  8.14 us
  transfers between devices with their start and end apart: 8, of which 7 were waited for; matrix products, arithmetic and copies ran while one was open for 19% of the time, Pallas kernels for 0%

profile of v6, /device:TPU:30, one launch (start us, length us, event | category | flops | bytes accessed | tf_op | source)
XLA Modules:
  0.0 373.4 jit_solution(208323063482416711)
XLA Ops:
  6.5 0.8 constant_dynamic-slice_fusion.3
  7.4 0.7 dynamic_slice.71
  8.9 8.4 %all-to-all-start = ((f32[32,1,32]{2,1,0:T(1,128)}), f32[32,1,32]{2,1,0:T(1,128)S(1)}, u32[]{:S(2)}, u32[]{:S(2)}) async-start(f32[32,1,32]{2,1,0:T(1,128)} %broadcast_in_dim.208), calls=%async_computation | async-start | bytes 32768 | tf_op jit(solution)/shard_map/all_to_all | solution.py:43
  17.4 1.3 constant_dynamic-slice_fusion
  19.0 0.8 constant_dynamic-slice_fusion.1
  19.8 0.7 fusion.49
  20.5 2.2 all-to-all-done
  22.7 2.8 broadcast_in_dim.214
  25.5 4.6 %all-to-all-start.1 = ((bf16[8,2304,128]{2,1,0:T(8,128)(2,1)}), bf16[8,2304,128]{2,1,0:T(8,128)(2,1)}, u32[]{:S(2)}, u32[]{:S(2)}) async-start(bf16[8,2304,128]{2,1,0:T(8,128)(2,1)} %broadcast_in_dim.214), calls=%async_computation.1 | async-start | bytes 9437184 | tf_op jit(solution)/shard_map/all_to_all | solution.py:43
  30.6 54.8 %all-to-all-done.1 = bf16[8,2304,128]{2,1,0:T(8,128)(2,1)} async-done(((bf16[8,2304,128]{2,1,0:T(8,128)(2,1)}), bf16[8,2304,128]{2,1,0:T(8,128)(2,1)}, u32[]{:S(2)}, u32[]{:S(2)}) %all-to-all-start.1) | async-done | bytes 4718624 | tf_op jit(solution)/shard_map/all_to_all | solution.py:43
  85.4 2.5 slice.46
  87.9 1.9 copy-done.2
  89.8 4.6 %fusion.29 = f32[32,1,64,128]{3,1,2,0:T(1,128)S(1)} fusion(f32[8,32,1,1]{0,2,3,1:T(1,128)S(1)} %copy.86, bf16[8,32,64,128]{3,2,1,0:T(8,128)(2,1)S(1)} %bitcast.170), kind=kOutput, calls=%fused_computation.31 | convolution fusion | flops 25165824 | bytes 5243904 | tf_op jit(solution)/shard_map/kgj,kgjpn->gjpn/dot_general | solution.py:78
  94.6 1.1 slice.47
  95.7 2.5 broadcast_in_dim.223
  98.3 7.0 %all-to-all-start.2 = ((bf16[4,4096,128]{2,1,0:T(8,128)(2,1)}), bf16[4,4096,128]{2,1,0:T(8,128)(2,1)}, u32[]{:S(2)}, u32[]{:S(2)}) async-start(bf16[4,4096,128]{2,1,0:T(8,128)(2,1)} %broadcast_in_dim.223), calls=%async_computation.2 | async-start | bytes 8388608 | tf_op jit(solution)/shard_map/all_to_all | solution.py:43
  105.3 0.7 all-gather.5.cloned.1.call-update
  108.2 3.4 fusion.41
  112.0 7.2 %fusion.31 = f32[32,1,64,128]{3,1,2,0:T(1,128)S(1)} fusion(f32[8,32,1,1]{0,2,3,1:T(1,128)S(1)} %copy.83, bf16[8,32,64,128]{3,2,1,0:T(8,128)(2,1)} %bitcast.171), kind=kOutput, calls=%fused_computation.33 | convolution fusion | flops 25165824 | bytes 5243904 | tf_op jit(solution)/shard_map/kgj,kgjpn->gjpn/dot_general | solution.py:74
  119.2 65.8 %all-to-all-done.2 = bf16[4,4096,128]{2,1,0:T(8,128)(2,1)} async-done(((bf16[4,4096,128]{2,1,0:T(8,128)(2,1)}), bf16[4,4096,128]{2,1,0:T(8,128)(2,1)}, u32[]{:S(2)}, u32[]{:S(2)}) %all-to-all-start.2) | async-done | bytes 4194336 | tf_op jit(solution)/shard_map/all_to_all | solution.py:43
  185.0 3.9 %fusion.88 = (bf16[4,2048,128]{2,1,0:T(8,128)(2,1)S(1)}, bf16[4,2048,128]{2,1,0:T(8,128)(2,1)}) fusion(bf16[4,4096,128]{2,1,0:T(8,128)(2,1)} %all-to-all-done.2), kind=kLoop, calls=%fused_computation.137 | loop fusion | bytes 8388608 | tf_op jit(solution)/shard_map/slice | solution.py:85
  188.9 3.7 fusion.39
  192.6 0.7 fusion.48
  194.2 4.1 %reshape_reshape.7 = bf16[4096,256]{1,0:T(8,128)(2,1)} reshape(bf16[4,2048,128]{2,1,0:T(8,128)(2,1)} %get-tuple-element.263) | data formatting | bytes 4194304 | tf_op jit(solution)/shard_map/reshape;reshape | solution.py:88
  198.3 2.7 fusion.89
  201.0 1.1 broadcast_in_dim.226
  202.1 43.3 %while.4 = (s32[]{:T(128)}, f32[1,16,128]{2,1,0:T(8,128)S(1)}, f32[1,16,128]{2,1,0:T(8,128)S(1)}, f32[1,16,128,128]{3,2,1,0:T(8,128)}, s32[4]{0:T(128)S(1)}, /*i...) while((s32[]{:T(128)}, f32[1,16,128]{2,1,0:T(8,128)S(1)}, ...), condition=%wide.region_10.11_spmd.clone, body=%wide.region_5.10_spmd.clone.sunk | while | flops 1101667456 | bytes 37366608 | solution.py:259
  204.0 8.9 %conditional.3 = ((f32[1,16,128]{2,1,0:T(8,128)S(1)}, f32[1,16,128]{2,1,0:T(8,128)S(1)}, f32[1,16,128,128]{3,2,1,0:T(8,128)})) conditional(s32[]{:T(128)} %convert_element_type.147, (f32[1,16,128]{2,1,0:T(8,128)S(1)}, f32[1,16,128]{2,1,0:T(8,128)S(1)}, f32[1,16,128,128]{3,2,1,0:T(8,128)}) %tuple.54, (s32[]{:T(128)}, s32[]{:T(128)}, ...), branch_computations={%region_6.6_spmd, %region_7.9_spmd} | conditional | flops 1101667456 | bytes 37365860 | solution.py:243
  204.1 0.7 iota_add_fusion
  205.0 1.3 fusion.2
  206.3 2.0 fusion.4
  208.3 3.6 fusion.12
  211.9 1.0 copy-done.4
  214.9 8.9 %conditional.3 = ((f32[1,16,128]{2,1,0:T(8,128)S(1)}, f32[1,16,128]{2,1,0:T(8,128)S(1)}, f32[1,16,128,128]{3,2,1,0:T(8,128)})) conditional(s32[]{:T(128)} %convert_element_type.147, (f32[1,16,128]{2,1,0:T(8,128)S(1)}, f32[1,16,128]{2,1,0:T(8,128)S(1)}, f32[1,16,128,128]{3,2,1,0:T(8,128)}) %tuple.54, (s32[]{:T(128)}, s32[]{:T(128)}, ...), branch_computations={%region_6.6_spmd, %region_7.9_spmd} | conditional | flops 1101667456 | bytes 37365860 | solution.py:243
  214.9 0.7 iota_add_fusion
  215.8 1.3 fusion.2
  217.1 2.0 fusion.4
  219.2 3.6 fusion.12
  222.8 1.0 copy-done.4
  225.7 8.9 %conditional.3 = ((f32[1,16,128]{2,1,0:T(8,128)S(1)}, f32[1,16,128]{2,1,0:T(8,128)S(1)}, f32[1,16,128,128]{3,2,1,0:T(8,128)})) conditional(s32[]{:T(128)} %convert_element_type.147, (f32[1,16,128]{2,1,0:T(8,128)S(1)}, f32[1,16,128]{2,1,0:T(8,128)S(1)}, f32[1,16,128,128]{3,2,1,0:T(8,128)}) %tuple.54, (s32[]{:T(128)}, s32[]{:T(128)}, ...), branch_computations={%region_6.6_spmd, %region_7.9_spmd} | conditional | flops 1101667456 | bytes 37365860 | solution.py:243
  225.7 0.7 iota_add_fusion
  226.6 1.3 fusion.2
  227.9 2.0 fusion.4
  230.0 3.6 fusion.12
  233.6 1.0 copy-done.4
  236.5 8.9 %conditional.3 = ((f32[1,16,128]{2,1,0:T(8,128)S(1)}, f32[1,16,128]{2,1,0:T(8,128)S(1)}, f32[1,16,128,128]{3,2,1,0:T(8,128)})) conditional(s32[]{:T(128)} %convert_element_type.147, (f32[1,16,128]{2,1,0:T(8,128)S(1)}, f32[1,16,128]{2,1,0:T(8,128)S(1)}, f32[1,16,128,128]{3,2,1,0:T(8,128)}) %tuple.54, (s32[]{:T(128)}, s32[]{:T(128)}, ...), branch_computations={%region_6.6_spmd, %region_7.9_spmd} | conditional | flops 1101667456 | bytes 37365860 | solution.py:243
  236.5 0.7 iota_add_fusion
  237.4 1.3 fusion.2
  238.7 2.0 fusion.4
  240.8 3.6 fusion.12
  244.4 1.0 copy-done.4
  245.3 1.7 fusion.69
  247.4 1.5 multiply_reduce_fusion
  249.5 1.4 collective-permute-start
  251.0 9.8 %collective-permute-done = bf16[128,2048]{1,0:T(8,128)(2,1)S(1)} collective-permute-done((bf16[128,2048]{1,0:T(8,128)(2,1)S(1)}, bf16[128,2048]{1,0:T(8,128)(2,1)S(1)}, u32[]{:S(2)}, u32[]{:S(2)}) %collective-permute-start) | collective-permute-done | bytes 524320 | tf_op jit(solution)/shard_map/ppermute | solution.py:103
  260.8 1.3 maximum_select_fusion
  262.1 48.4 %all-gather.3.cloned.1.call-done = bf16[1024,4096]{1,0:T(8,128)(2,1)} async-done(((bf16[128,4096]{1,0:T(8,128)(2,1)}), bf16[1024,4096]{1,0:T(8,128)(2,1)}) %all-gather.3.cloned.1.call-update) | async-done | bytes 8388624 | tf_op jit(solution)/shard_map/all_gather | solution.py:311
  310.5 8.1 %fusion.27 = f32[1024,4,128]{2,0,1:T(8,128)S(1)} fusion(bf16[4,4096,128]{2,1,0:T(8,128)(2,1)} %all-gather.5.cloned.1.call-done, bf16[1024,4096]{1,0:T(8,128)(2,1)} %all-gather.3.cloned.1.call-done), kind=kOutput, calls=%fused_computation.29 | convolution fusion | flops 4294967296 | bytes 14680064 | tf_op jit(solution)/shard_map/tc,ycr->tyr/dot_general | solution.py:313
  318.8 0.9 collective-permute-start.1
  319.7 13.2 %collective-permute-done.1 = bf16[1024,2,128]{2,0,1:T(8,128)(2,1)S(1)} collective-permute-done((bf16[1024,2,128]{2,0,1:T(8,128)(2,1)S(1)}, bf16[1024,2,128]{2,0,1:T(8,128)(2,1)S(1)}, u32[]{:S(2)}, u32[]{:S(2)}) %collective-permute-start.1) | collective-permute-done | bytes 524320 | tf_op jit(solution)/shard_map/ppermute | solution.py:103
  333.6 13.5 %all_to_all.20 = bf16[8,128,2,128]{3,2,1,0:T(2,128)(2,1)S(1)} all-to-all(bf16[8,128,2,128]{3,2,1,0:T(2,128)(2,1)S(1)} %copy.80), channel_id=1, replica_groups=mesh['pipe'=2,'y'=4,'zc'=8,'tp'=2] {'zc'}, dimensions={0} | all-to-all | bytes 1048576 | tf_op jit(solution)/shard_map/all_to_all | solution.py:321
  348.6 1.3 collective-permute-start.2
  349.9 15.4 %collective-permute-done.2 = bf16[128,2048]{1,0:T(8,128)(2,1)S(1)} collective-permute-done((bf16[128,2048]{1,0:T(8,128)(2,1)S(1)}, bf16[128,2048]{1,0:T(8,128)(2,1)S(1)}, u32[]{:S(2)}, u32[]{:S(2)}) %collective-permute-start.2) | collective-permute-done | bytes 524320 | tf_op jit(solution)/shard_map/ppermute | solution.py:109
  365.3 1.3 fusion.66
  (118 shorter events, 12.2 us)
Async XLA Ops:
  6.5 101.5 %copy-start = (bf16[128,256]{1,0:T(8,128)(2,1)S(1)}, bf16[128,256]{1,0:T(8,128)(2,1)}, u32[]{:S(2)}) copy-start(bf16[128,256]{1,0:T(8,128)(2,1)} %param.21) | copy-start | bytes 196612
  6.5 13.3 %copy-start.8 = (bf16[128,256]{1,0:T(8,128)(2,1)S(1)}, bf16[128,256]{1,0:T(8,128)(2,1)}, u32[]{:S(2)}) copy-start(bf16[128,256]{1,0:T(8,128)(2,1)} %param.20) | copy-start | bytes 196612
  8.9 13.8 %all-to-all-start = ((f32[32,1,32]{2,1,0:T(1,128)}), f32[32,1,32]{2,1,0:T(1,128)S(1)}, u32[]{:S(2)}, u32[]{:S(2)}) async-start(f32[32,1,32]{2,1,0:T(1,128)} %broadcast_in_dim.208), calls=%async_computation | async-start | bytes 32768 | tf_op jit(solution)/shard_map/all_to_all | solution.py:43
  25.5 59.9 %all-to-all-start.1 = ((bf16[8,2304,128]{2,1,0:T(8,128)(2,1)}), bf16[8,2304,128]{2,1,0:T(8,128)(2,1)}, u32[]{:S(2)}, u32[]{:S(2)}) async-start(bf16[8,2304,128]{2,1,0:T(8,128)(2,1)} %broadcast_in_dim.214), calls=%async_computation.1 | async-start | bytes 9437184 | tf_op jit(solution)/shard_map/all_to_all | solution.py:43
  87.9 2.0 copy-start.2
  98.3 8.0 %copy-start.9 = (f32[128,64]{0,1:T(8,128)S(1)}, f32[128,64]{0,1:T(8,128)}, u32[]{:S(2)}) copy-start(f32[128,64]{0,1:T(8,128)} %param.22) | copy-start | bytes 98308
  98.3 8.4 %copy-start.10 = (f32[64]{0:T(128)S(1)}, f32[64]{0:T(128)}, u32[]{:S(2)}) copy-start(f32[64]{0:T(128)} %param.24) | copy-start | bytes 772
  98.3 86.8 %all-to-all-start.2 = ((bf16[4,4096,128]{2,1,0:T(8,128)(2,1)}), bf16[4,4096,128]{2,1,0:T(8,128)(2,1)}, u32[]{:S(2)}, u32[]{:S(2)}) async-start(bf16[4,4096,128]{2,1,0:T(8,128)(2,1)} %broadcast_in_dim.223), calls=%async_computation.2 | async-start | bytes 8388608 | tf_op jit(solution)/shard_map/all_to_all | solution.py:43
  105.3 156.8 %all-gather.5.cloned.1.call-start = ((), (), s32[]{:S(2)}) async-start(), calls=%async_computation.5 | async-start | bytes 5242880 | tf_op jit(solution)/shard_map/all_gather | solution.py:312
  106.0 204.4 %all-gather.3.cloned.1.call-start = ((), (), s32[]{:S(2)}) async-start(), calls=%async_computation.4 | async-start | bytes 9437184 | tf_op jit(solution)/shard_map/all_gather | solution.py:311
  188.9 4.3 %copy-start.5 = (f32[128,1,32,64]{0,3,2,1:T(8,128)S(1)}, f32[128,1,32,64]{0,3,2,1:T(8,128)}, u32[]{:S(2)}) copy-start(f32[128,1,32,64]{0,3,2,1:T(8,128)} %fusion.41) | copy-start | bytes 3145732
  206.3 2.0 copy-start.3
  211.9 1.0 copy-start.4
  217.1 2.0 copy-start.3
  222.7 1.0 copy-start.4
  227.9 2.0 copy-start.3
  233.6 1.0 copy-start.4
  238.7 2.0 copy-start.3
  244.4 1.0 copy-start.4
  245.3 3.5 copy-start.6
  245.3 3.6 dynamic-slice-start
  249.5 11.2 %collective-permute-start = (bf16[128,2048]{1,0:T(8,128)(2,1)S(1)}, bf16[128,2048]{1,0:T(8,128)(2,1)S(1)}, u32[]{:S(2)}, u32[]{:S(2)}) collective-permute-start(bf16[128,2048]{1,0:T(8,128)(2,1)S(1)} %get-tuple-element.265), channel_id=1, source_target_pairs={{0,64},{64,0},{1,65},{65,1},{2,66},{66,2},{3,67},{67,3},{4,68},{68... | collective-permute-start | bytes 1572872 | tf_op jit(solution)/shard_map/ppermute | solution.py:103
  318.7 29.3 %copy-start.7 = (bf16[128,2048]{1,0:T(8,128)(2,1)S(1)}, bf16[128,2048]{1,0:T(8,128)(2,1)}, u32[]{:S(2)}) copy-start(bf16[128,2048]{1,0:T(8,128)(2,1)} %param.17) | copy-start | bytes 1572868
  318.8 14.2 %collective-permute-start.1 = (bf16[1024,2,128]{2,0,1:T(8,128)(2,1)S(1)}, bf16[1024,2,128]{2,0,1:T(8,128)(2,1)S(1)}, u32[]{:S(2)}, u32[]{:S(2)}) collective-permute-start(bf16[1024,2,128]{2,0,1:T(8,128)(2,1)S(1)} %select_convert_fusion), channel_id=1, source_target_pairs={{0,1},{1,0},{2,3},{3,2},{4,5},{5,4},{6,7},{7,6},{8,9},{9,8},{10,11... | collective-permute-start | bytes 1572872 | tf_op jit(solution)/shard_map/ppermute | solution.py:103
  333.6 32.9 %copy-start.1 = (bf16[128,256]{1,0:T(8,128)(2,1)S(1)}, bf16[128,256]{1,0:T(8,128)(2,1)}, u32[]{:S(2)}) copy-start(bf16[128,256]{1,0:T(8,128)(2,1)} %param.21) | copy-start | bytes 196612
  348.6 16.7 %collective-permute-start.2 = (bf16[128,2048]{1,0:T(8,128)(2,1)S(1)}, bf16[128,2048]{1,0:T(8,128)(2,1)S(1)}, u32[]{:S(2)}, u32[]{:S(2)}) collective-permute-start(bf16[128,2048]{1,0:T(8,128)(2,1)S(1)} %fusion.54), channel_id=1, source_target_pairs={{0,64},{1,65},{2,66},{3,67},{4,68},{5,69},{6,70},{7,71},{8,72},{9,... | collective-permute-start | bytes 1572872 | tf_op jit(solution)/shard_map/ppermute | solution.py:109
Sparse Core Ops, SparseCore 0:
  107.8 77.6 all-gather.4
  262.2 48.2 all-gather.2

commit v7 on v1

--- a/solution.py
+++ b/solution.py
@@ -290,19 +290,27 @@
         jnp.concatenate([kept_half, incoming], axis=1),
         jnp.concatenate([incoming, kept_half], axis=1),
     )
-    partial_value = jnp.dot(
-        mixed_rows,
-        lax.all_gather(out_weights, CTX, axis=2, tiled=True)[0],
-        preferred_element_type=jnp.float32,
-    )
-    half = partial_value.shape[1] // 2
+    weights_all = lax.all_gather(out_weights, CTX, axis=2, tiled=True)[0]
+    half = weights_all.shape[1] // 2
     tp_rank = lax.axis_index("tp")
-    kept = jnp.where(tp_rank == 0, partial_value[:, :half], partial_value[:, half:])
-    sent = jnp.where(tp_rank == 0, partial_value[:, half:], partial_value[:, :half])
-    projected = kept + from_partner(sent.astype(jnp.bfloat16), "tp", 0).astype(jnp.float32)
-    own_section = (resid_in.astype(jnp.float32) + projected).astype(jnp.bfloat16)
-    received = shifted(own_section, "pipe", 1)
-    second_section = (received.astype(jnp.float32) + projected).astype(jnp.bfloat16)
+    sent_cols = lax.dynamic_slice_in_dim(weights_all, (1 - tp_rank) * half, half, 1)
+    kept_cols = lax.dynamic_slice_in_dim(weights_all, tp_rank * half, half, 1)
+    sent = jnp.dot(mixed_rows, sent_cols, preferred_element_type=jnp.float32).astype(jnp.bfloat16)
+    from_tp = from_partner(sent, "tp", 0)
+    kept = jnp.dot(mixed_rows, kept_cols, preferred_element_type=jnp.float32)
+    kept_low = kept.astype(jnp.bfloat16)
+    first_kept = shifted(kept_low, "pipe", 1)
+    first_sent = lax.ppermute(sent, ("pipe", "tp"), [(0, 3), (1, 2)])
+    base = resid_in.astype(jnp.float32)
+    own_section = (
+        (base + kept_low.astype(jnp.float32)) + from_tp.astype(jnp.float32)
+    ).astype(jnp.bfloat16)
+    rebuilt = (
+        (base + first_kept.astype(jnp.float32)) + first_sent.astype(jnp.float32)
+    ).astype(jnp.bfloat16)
+    second_section = (
+        rebuilt.astype(jnp.float32) + (kept + from_tp.astype(jnp.float32))
+    ).astype(jnp.bfloat16)
     return jnp.where(section == 0, own_section, second_section)[None]
 
 

time: 295 us -> 290 us (0.983)
  waiting for transfers between devices: 146 us -> 137 us
  matrix products: 62 us -> 65.2 us
    ppermute x0 -> x1, waiting for transfers between devices: none -> 14.7 us  [per_device(): first_sent = lax.ppermute(sent, ('pipe', 'tp'), [(0, 3), (1, 2)])]
    ppermute x1, waiting for transfers between devices: 13.2 us -> 0.01 us  [shifted(): return lax.ppermute(x, axis, pairs)]
    ppermute x2, waiting for transfers between devices: 24.3 us -> 13.7 us  [from_partner(): return lax.ppermute(block, axis, route)]
    dot_general x1 -> x2, matrix products: 13 us -> 16.2 us  [the longest x1 8.11 us: per_device(): kept = jnp.dot(mixed_rows, kept_cols, preferred_element_type=jnp.float32)]
  transfers between devices with their start and end apart: 8 -> 9, of which waited for: 6 -> 6; matrix products, arithmetic and copies ran while one was open for 28% -> 31% of each run, Pallas kernels for 0% -> 0%
where the time goes in v7:
time: 290 us; the launch traced here: 289 us
  waiting for transfers between devices  137 us (47%)
  matrix products  65.2 us (22%)
  starting transfers between devices  32.5 us (11%)
  local copies, waits for them, and re-layouts  17.8 us (6%)
  other arithmetic  17.2 us (6%)
  between operations  13.8 us (5%)
  loops' own time  5.47 us (2%)
    all_to_all x4, waiting for transfers between devices, gathered(): return lax.all_to_all(spread, axis, 0, 0)  108 us
    all_to_all x4, starting transfers between devices, gathered(): return lax.all_to_all(spread, axis, 0, 0)  27.7 us
    ppermute x1, waiting for transfers between devices, per_device(): first_sent = lax.ppermute(sent, ('pipe', 'tp'), [(0, 3), (1, 2)])  14.7 us
    dot_general x4, matrix products, absorb(): jnp.einsum('gjqk,kgd->gjqd', weights_exp.astype(jnp.bfloat16), value_rows...  14.4 us
    ppermute x2, waiting for transfers between devices, from_partner(): return lax.ppermute(block, axis, route)  13.7 us
    dot_general x4, matrix products, absorb(): jnp.einsum('qgjd,kgd->gjqk', query_groups, key_rows, preferred_element_ty...  9.06 us
    dot_general x1, matrix products, per_device(): kept = jnp.dot(mixed_rows, kept_cols, preferred_element_type=jnp.float32)  8.11 us
    dot_general x1, matrix products, per_device(): jnp.dot(mixed_rows, sent_cols, preferred_element_type=jnp.float32)  8.1 us
  transfers between devices with their start and end apart: 9, of which 6 were waited for; matrix products, arithmetic and copies ran while one was open for 31% of the time, Pallas kernels for 0%

profile of v7, /device:TPU:30, one launch (start us, length us, event | category | flops | bytes accessed | tf_op | source)
XLA Modules:
  0.0 288.6 jit_solution(16571032270590202225)
XLA Ops:
  6.5 0.7 all-gather.2.cloned.1.call-update
  7.3 0.7 constant_dynamic-slice_fusion.3
  8.1 0.7 dynamic_slice.81
  9.0 0.6 broadcast_in_dim.214
  9.6 8.4 %all-to-all-start = ((f32[32,1,32]{2,1,0:T(1,128)}), f32[32,1,32]{2,1,0:T(1,128)S(1)}, u32[]{:S(2)}, u32[]{:S(2)}) async-start(f32[32,1,32]{2,1,0:T(1,128)} %broadcast_in_dim.214), calls=%async_computation | async-start | bytes 32768 | tf_op jit(solution)/shard_map/all_to_all | solution.py:43
  18.1 1.3 constant_dynamic-slice_fusion
  19.7 0.7 fusion.56
  20.3 3.1 %all-to-all-done = f32[32,1,32]{2,1,0:T(1,128)S(1)} async-done(((f32[32,1,32]{2,1,0:T(1,128)}), f32[32,1,32]{2,1,0:T(1,128)S(1)}, u32[]{:S(2)}, u32[]{:S(2)}) %all-to-all-start) | async-done | bytes 4128 | tf_op jit(solution)/shard_map/all_to_all | solution.py:43
  23.4 3.1 %broadcast_in_dim.220 = bf16[8,1,32,64,128]{4,3,2,1,0:T(8,128)(2,1)} broadcast(bf16[32,64,128]{2,1,0:T(8,128)(2,1)S(1)} %fusion.56), dimensions={2,3,4} | broadcast | bytes 4718592 | tf_op jit(solution)/shard_map/broadcast_in_dim | solution.py:42
  26.5 4.7 %all-to-all-start.1 = ((bf16[8,1,32,64,128]{4,3,2,1,0:T(8,128)(2,1)}), bf16[8,1,32,64,128]{4,3,2,1,0:T(8,128)(2,1)}, u32[]{:S(2)}, u32[]{:S(2)}) async-start(bf16[8,1,32,64,128]{4,3,2,1,0:T(8,128)(2,1)} %broadcast_in_dim.220), calls=%async_computation.1 | async-start | bytes 8388608 | tf_op jit(solution)/shard_map/all_to_all | solution.py:43
  31.2 1.2 copy.70
  33.2 0.7 slice.16
  34.2 68.8 %all-to-all-done.1 = bf16[8,1,32,64,128]{4,3,2,1,0:T(8,128)(2,1)} async-done(((bf16[8,1,32,64,128]{4,3,2,1,0:T(8,128)(2,1)}), bf16[8,1,32,64,128]{4,3,2,1,0:T(8,128)(2,1)}, u32[]{:S(2)}, u32[]{:S(2)}) %all-to-all-start.1) | async-done | bytes 4194336 | tf_op jit(solution)/shard_map/all_to_all | solution.py:43
  103.0 1.5 broadcast_in_dim.233
  104.6 8.1 %all-to-all-start.3 = ((bf16[32,128,256]{2,1,0:T(8,128)(2,1)}), bf16[32,128,256]{2,1,0:T(8,128)(2,1)S(1)}, u32[]{:S(2)}, u32[]{:S(2)}) async-start(bf16[32,128,256]{2,1,0:T(8,128)(2,1)} %broadcast_in_dim.233), calls=%async_computation.3 | async-start | bytes 4194304 | tf_op jit(solution)/shard_map/all_to_all | solution.py:43
  112.7 3.4 %fusion.48 = f32[128,1,32,64]{0,3,2,1:T(8,128)} fusion(bf16[128,32,64]{0,2,1:T(8,128)(2,1)S(1)} %bitcast.168, f32[32,128]{1,0:T(8,128)S(1)} %fusion.109, f32[128,32]{0,1:T(8,128)S(1)} %copy.65, f32[128,128]{1,0:T(8,128)S(1)} %fusion.84, pred[128,128]{1,0:T(8,128)(4,1)S(1)} %iota_compare_fusion), kind=kOutput, calls=%fused_computation.49 | convolution fusion | flops 404750336 | bytes 1687552 | tf_op jit(solution)/shard_map/while/body/eval_jaxpr/gjts,sgjp->tgjp/dot_general | solution.py:108
  117.0 7.3 %fusion.33 = f32[32,1,64,128]{3,1,2,0:T(1,128)S(1)} fusion(f32[8,32,1,1]{0,2,3,1:T(1,128)S(1)} %copy.79, bf16[8,32,64,128]{3,2,1,0:T(8,128)(2,1)} %bitcast.28), kind=kOutput, calls=%fused_computation.35 | convolution fusion | flops 25165824 | bytes 5243904 | tf_op jit(solution)/shard_map/kgj,kgjpn->gjpn/dot_general | solution.py:67
  124.4 35.6 %all-to-all-done.3 = bf16[32,128,256]{2,1,0:T(8,128)(2,1)S(1)} async-done(((bf16[32,128,256]{2,1,0:T(8,128)(2,1)}), bf16[32,128,256]{2,1,0:T(8,128)(2,1)S(1)}, u32[]{:S(2)}, u32[]{:S(2)}) %all-to-all-start.3) | async-done | bytes 2097184 | tf_op jit(solution)/shard_map/all_to_all | solution.py:43
  160.0 1.9 broadcast_in_dim.229
  161.9 6.5 %all-to-all-start.2 = ((bf16[4,1,32,64,128]{4,3,2,1,0:T(8,128)(2,1)}), bf16[4,1,32,64,128]{4,3,2,1,0:T(8,128)(2,1)}, u32[]{:S(2)}, u32[]{:S(2)}) async-start(bf16[4,1,32,64,128]{4,3,2,1,0:T(8,128)(2,1)} %broadcast_in_dim.229), calls=%async_computation.2 | async-start | bytes 4194304 | tf_op jit(solution)/shard_map/all_to_all | solution.py:43
  168.5 1.5 fusion.102
  170.0 42.4 %while.4 = (s32[]{:T(128)}, f32[1,16,128]{2,1,0:T(8,128)S(1)}, f32[1,16,128]{2,1,0:T(8,128)S(1)}, f32[1,16,128,128]{3,2,1,0:T(8,128)S(1)}, s32[4]{0:T(128)S(1)},...) while((s32[]{:T(128)}, f32[1,16,128]{2,1,0:T(8,128)S(1)}, ...), condition=%wide.region_10.11_spmd.clone, body=%wide.region_5.10_spmd.clone.sunk | while | flops 1101667456 | bytes 28978456 | solution.py:241
  170.1 0.6 dynamic_slice.146
  171.9 8.7 %conditional.3 = ((f32[1,16,128]{2,1,0:T(8,128)S(1)}, f32[1,16,128]{2,1,0:T(8,128)S(1)}, f32[1,16,128,128]{3,2,1,0:T(8,128)S(1)})) conditional(s32[]{:T(128)} %convert_element_type.185, (f32[1,16,128]{2,1,0:T(8,128)S(1)}, f32[1,16,128]{2,1,0:T(8,128)S(1)}, f32[1,16,128,128]{3,2,1,0:T(8,128)S(1)}) %tuple.54, (s32[]{:T(128)}, s32[]{:T(128)}, ...), branch_computations={%region_6.6_spmd, %region_7.9_spmd} | conditional | flops 1101667456 | bytes 28977704 | solution.py:223
  171.9 0.6 iota_add_fusion
  172.7 2.3 fusion.2
  175.0 2.0 fusion.4
  177.0 3.6 %fusion.12 = f32[1,16,128,128]{3,2,1,0:T(8,128)S(1)} fusion(f32[1024,128,16]{1,0,2:T(8,128)S(1)} %get-tuple-element.261, f32[16,128]{1,0:T(8,128)S(1)} %bitcast.165, pred[128,1024]{0,1:T(8,128)(4,1)S(1)} %broadcast_compare_fusion, f32[1,16,128,128]{3,2,1,0:T(8,128)S(1)} %get-tuple-element.147, f32[16,128]{1,0:T(8,128)S(1)} %get-tuple-element.258, ...), kind=kOutput, calls=%fused_computation.10 | convolution fusion | flops 547880960 | bytes 10895872 | tf_op jit(solution)/shard_map/while/body/eval_jaxpr/cond/branch_1_fun/gjqk,kgd->gjqd/dot_general | solution.py:215
  180.6 0.6 dynamic_slice.146
  182.5 8.8 %conditional.3 = ((f32[1,16,128]{2,1,0:T(8,128)S(1)}, f32[1,16,128]{2,1,0:T(8,128)S(1)}, f32[1,16,128,128]{3,2,1,0:T(8,128)S(1)})) conditional(s32[]{:T(128)} %convert_element_type.185, (f32[1,16,128]{2,1,0:T(8,128)S(1)}, f32[1,16,128]{2,1,0:T(8,128)S(1)}, f32[1,16,128,128]{3,2,1,0:T(8,128)S(1)}) %tuple.54, (s32[]{:T(128)}, s32[]{:T(128)}, ...), branch_computations={%region_6.6_spmd, %region_7.9_spmd} | conditional | flops 1101667456 | bytes 28977704 | solution.py:223
  182.5 0.6 iota_add_fusion
  183.3 2.3 fusion.2
  185.6 2.0 fusion.4
  187.6 3.6 %fusion.12 = f32[1,16,128,128]{3,2,1,0:T(8,128)S(1)} fusion(f32[1024,128,16]{1,0,2:T(8,128)S(1)} %get-tuple-element.261, f32[16,128]{1,0:T(8,128)S(1)} %bitcast.165, pred[128,1024]{0,1:T(8,128)(4,1)S(1)} %broadcast_compare_fusion, f32[1,16,128,128]{3,2,1,0:T(8,128)S(1)} %get-tuple-element.147, f32[16,128]{1,0:T(8,128)S(1)} %get-tuple-element.258, ...), kind=kOutput, calls=%fused_computation.10 | convolution fusion | flops 547880960 | bytes 10895872 | tf_op jit(solution)/shard_map/while/body/eval_jaxpr/cond/branch_1_fun/gjqk,kgd->gjqd/dot_general | solution.py:215
  191.3 0.6 dynamic_slice.146
  193.1 8.7 %conditional.3 = ((f32[1,16,128]{2,1,0:T(8,128)S(1)}, f32[1,16,128]{2,1,0:T(8,128)S(1)}, f32[1,16,128,128]{3,2,1,0:T(8,128)S(1)})) conditional(s32[]{:T(128)} %convert_element_type.185, (f32[1,16,128]{2,1,0:T(8,128)S(1)}, f32[1,16,128]{2,1,0:T(8,128)S(1)}, f32[1,16,128,128]{3,2,1,0:T(8,128)S(1)}) %tuple.54, (s32[]{:T(128)}, s32[]{:T(128)}, ...), branch_computations={%region_6.6_spmd, %region_7.9_spmd} | conditional | flops 1101667456 | bytes 28977704 | solution.py:223
  193.1 0.6 iota_add_fusion
  193.9 2.3 fusion.2
  196.2 2.0 fusion.4
  198.2 3.6 %fusion.12 = f32[1,16,128,128]{3,2,1,0:T(8,128)S(1)} fusion(f32[1024,128,16]{1,0,2:T(8,128)S(1)} %get-tuple-element.261, f32[16,128]{1,0:T(8,128)S(1)} %bitcast.165, pred[128,1024]{0,1:T(8,128)(4,1)S(1)} %broadcast_compare_fusion, f32[1,16,128,128]{3,2,1,0:T(8,128)S(1)} %get-tuple-element.147, f32[16,128]{1,0:T(8,128)S(1)} %get-tuple-element.258, ...), kind=kOutput, calls=%fused_computation.10 | convolution fusion | flops 547880960 | bytes 10895872 | tf_op jit(solution)/shard_map/while/body/eval_jaxpr/cond/branch_1_fun/gjqk,kgd->gjqd/dot_general | solution.py:215
  201.8 0.6 dynamic_slice.146
  203.7 8.8 %conditional.3 = ((f32[1,16,128]{2,1,0:T(8,128)S(1)}, f32[1,16,128]{2,1,0:T(8,128)S(1)}, f32[1,16,128,128]{3,2,1,0:T(8,128)S(1)})) conditional(s32[]{:T(128)} %convert_element_type.185, (f32[1,16,128]{2,1,0:T(8,128)S(1)}, f32[1,16,128]{2,1,0:T(8,128)S(1)}, f32[1,16,128,128]{3,2,1,0:T(8,128)S(1)}) %tuple.54, (s32[]{:T(128)}, s32[]{:T(128)}, ...), branch_computations={%region_6.6_spmd, %region_7.9_spmd} | conditional | flops 1101667456 | bytes 28977704 | solution.py:223
  203.7 0.6 iota_add_fusion
  204.5 2.3 fusion.2
  206.8 2.0 fusion.4
  208.8 3.6 %fusion.12 = f32[1,16,128,128]{3,2,1,0:T(8,128)S(1)} fusion(f32[1024,128,16]{1,0,2:T(8,128)S(1)} %get-tuple-element.261, f32[16,128]{1,0:T(8,128)S(1)} %bitcast.165, pred[128,1024]{0,1:T(8,128)(4,1)S(1)} %broadcast_compare_fusion, f32[1,16,128,128]{3,2,1,0:T(8,128)S(1)} %get-tuple-element.147, f32[16,128]{1,0:T(8,128)S(1)} %get-tuple-element.258, ...), kind=kOutput, calls=%fused_computation.10 | convolution fusion | flops 547880960 | bytes 10895872 | tf_op jit(solution)/shard_map/while/body/eval_jaxpr/cond/branch_1_fun/gjqk,kgd->gjqd/dot_general | solution.py:215
  212.4 0.3 fusion.79
  212.8 0.3 copy.74
  213.1 7.1 %fusion.35 = f32[32,1,64,128]{3,1,2,0:T(1,128)S(1)} fusion(f32[8,32,1,1]{0,2,3,1:T(1,128)S(1)} %copy.76, bf16[8,32,64,128]{3,2,1,0:T(8,128)(2,1)} %bitcast.28), kind=kOutput, calls=%fused_computation.37 | convolution fusion | flops 25165824 | bytes 5243904 | tf_op jit(solution)/shard_map/kgj,kgjpn->gjpn/dot_general | solution.py:63
  220.3 5.6 %fusion.46 = f32[32,1,64,128]{3,1,2,0:T(1,128)S(1)} fusion(f32[4,32,1,1]{0,2,3,1:T(1,128)S(1)} %copy.81, bf16[4,32,64,128]{3,2,1,0:T(8,128)(2,1)} %bitcast.35), kind=kOutput, calls=%fused_computation.47 | convolution fusion | flops 12582912 | bytes 3146240 | tf_op jit(solution)/shard_map/kgj,kgjpn->gjpn/dot_general | solution.py:74
  226.0 0.7 fusion.55
  226.7 0.6 fusion.54
  227.6 1.5 multiply_reduce_fusion
  229.2 1.8 bitcast_select_fusion.2
  231.0 1.4 collective-permute-start
  232.4 13.1 %collective-permute-done = bf16[128,2048]{1,0:T(8,128)(2,1)S(1)} collective-permute-done((bf16[128,2048]{1,0:T(8,128)(2,1)S(1)}, bf16[128,2048]{1,0:T(8,128)(2,1)S(1)}, u32[]{:S(2)}, u32[]{:S(2)}) %collective-permute-start) | collective-permute-done | bytes 524320 | tf_op jit(solution)/shard_map/ppermute | solution.py:85
  245.5 8.1 %fusion.37 = bf16[128,2048]{1,0:T(8,128)(2,1)S(1)} fusion(bf16[1,4096,4096]{2,1,0:T(8,128)(2,1)} %all-gather.2.cloned.1.call-done, s32[]{:T(128)S(6)} %select_n.148, bf16[128,2048]{1,0:T(8,128)(2,1)S(1)} %collective-permute-done, bf16[128,2048]{1,0:T(8,128)(2,1)S(1)} %get-tuple-element.262, pred[]{:T(512)S(6)} %eq.2), kind=kOutput, calls=%fused_computation.39 | convolution fusion | flops 2152464384 | bytes 18350084 | tf_op jit(solution)/shard_map/dot_general | solution.py:298
  253.6 0.8 collective-permute-start.1
  254.4 1.3 collective-permute-start.3
  255.7 8.1 %fusion.104 = (bf16[128,2048]{1,0:T(8,128)(2,1)S(1)}, f32[128,2048]{1,0:T(8,128)S(1)}) fusion(bf16[1,4096,4096]{2,1,0:T(8,128)(2,1)} %all-gather.2.cloned.1.call-done, s32[]{:T(128)S(6)} %select_n.147, bf16[128,2048]{1,0:T(8,128)(2,1)S(1)} %collective-permute-done, bf16[128,2048]{1,0:T(8,128)(2,1)S(1)} %get-tuple-element.262, pred[]{:T(512)S(6)} %eq.2), kind=kOutput, calls=%fused_computation.148 | convolution fusion | flops 2152464384 | bytes 19398660 | tf_op jit(solution)/shard_map/dot_general | solution.py:300
  263.8 1.3 collective-permute-start.2
  265.1 0.6 collective-permute-done.1
  265.8 14.7 %collective-permute-done.3 = bf16[128,2048]{1,0:T(8,128)(2,1)S(1)} collective-permute-done((bf16[128,2048]{1,0:T(8,128)(2,1)S(1)}, bf16[128,2048]{1,0:T(8,128)(2,1)S(1)}, u32[]{:S(2)}, u32[]{:S(2)}) %collective-permute-start.3) | collective-permute-done | bytes 524320 | tf_op jit(solution)/shard_map/ppermute | solution.py:303
  280.4 1.3 fusion.76
  (90 shorter events, 4.0 us)
Async XLA Ops:
  6.5 27.4 %copy-start = (bf16[128,256]{1,0:T(8,128)(2,1)S(1)}, bf16[128,256]{1,0:T(8,128)(2,1)}, u32[]{:S(2)}) copy-start(bf16[128,256]{1,0:T(8,128)(2,1)} %param.21) | copy-start | bytes 196612
  6.5 13.1 %copy-start.4 = (bf16[128,256]{1,0:T(8,128)(2,1)S(1)}, bf16[128,256]{1,0:T(8,128)(2,1)}, u32[]{:S(2)}) copy-start(bf16[128,256]{1,0:T(8,128)(2,1)} %param.20) | copy-start | bytes 196612
  6.5 239.0 %all-gather.2.cloned.1.call-start = ((), (), s32[]{:S(2)}) async-start(), calls=%async_computation.4 | async-start | bytes 34603008 | tf_op jit(solution)/shard_map/all_gather | solution.py:293
  9.6 13.8 %all-to-all-start = ((f32[32,1,32]{2,1,0:T(1,128)}), f32[32,1,32]{2,1,0:T(1,128)S(1)}, u32[]{:S(2)}, u32[]{:S(2)}) async-start(f32[32,1,32]{2,1,0:T(1,128)} %broadcast_in_dim.214), calls=%async_computation | async-start | bytes 32768 | tf_op jit(solution)/shard_map/all_to_all | solution.py:43
  26.5 6.0 %copy-start.8 = (f32[64]{0:T(128)S(1)}, f32[64]{0:T(128)}, u32[]{:S(2)}) copy-start(f32[64]{0:T(128)} %param.24) | copy-start | bytes 772
  26.5 7.4 %copy-start.5 = (f32[128,64]{0,1:T(8,128)S(1)}, f32[128,64]{0,1:T(8,128)}, u32[]{:S(2)}) copy-start(f32[128,64]{0,1:T(8,128)} %param.22) | copy-start | bytes 98308
  26.5 7.6 %copy-start.6 = (bf16[128,256]{1,0:T(8,128)(2,1)S(1)}, bf16[128,256]{1,0:T(8,128)(2,1)}, u32[]{:S(2)}) copy-start(bf16[128,256]{1,0:T(8,128)(2,1)} %param.28) | copy-start | bytes 196612
  26.5 7.6 %copy-start.7 = (bf16[128,256]{1,0:T(8,128)(2,1)S(1)}, bf16[128,256]{1,0:T(8,128)(2,1)}, u32[]{:S(2)}) copy-start(bf16[128,256]{1,0:T(8,128)(2,1)} %param.27) | copy-start | bytes 196612
  26.5 76.5 %all-to-all-start.1 = ((bf16[8,1,32,64,128]{4,3,2,1,0:T(8,128)(2,1)}), bf16[8,1,32,64,128]{4,3,2,1,0:T(8,128)(2,1)}, u32[]{:S(2)}, u32[]{:S(2)}) async-start(bf16[8,1,32,64,128]{4,3,2,1,0:T(8,128)(2,1)} %broadcast_in_dim.220), calls=%async_computation.1 | async-start | bytes 8388608 | tf_op jit(solution)/shard_map/all_to_all | solution.py:43
  104.6 55.4 %all-to-all-start.3 = ((bf16[32,128,256]{2,1,0:T(8,128)(2,1)}), bf16[32,128,256]{2,1,0:T(8,128)(2,1)S(1)}, u32[]{:S(2)}, u32[]{:S(2)}) async-start(bf16[32,128,256]{2,1,0:T(8,128)(2,1)} %broadcast_in_dim.233), calls=%async_computation.3 | async-start | bytes 4194304 | tf_op jit(solution)/shard_map/all_to_all | solution.py:43
  161.9 58.4 %all-to-all-start.2 = ((bf16[4,1,32,64,128]{4,3,2,1,0:T(8,128)(2,1)}), bf16[4,1,32,64,128]{4,3,2,1,0:T(8,128)(2,1)}, u32[]{:S(2)}, u32[]{:S(2)}) async-start(bf16[4,1,32,64,128]{4,3,2,1,0:T(8,128)(2,1)} %broadcast_in_dim.229), calls=%async_computation.2 | async-start | bytes 4194304 | tf_op jit(solution)/shard_map/all_to_all | solution.py:43
  220.3 6.4 %copy-start.1 = (f32[128,2048]{0,1:T(8,128)S(1)}, f32[128,2048]{0,1:T(8,128)}, u32[]{:S(2)}) copy-start(f32[128,2048]{0,1:T(8,128)} %copy.70) | copy-start | bytes 3145732
  220.3 6.4 %copy-start.2 = (f32[128,1,32,64]{0,3,2,1:T(8,128)S(1)}, f32[128,1,32,64]{0,3,2,1:T(8,128)}, u32[]{:S(2)}) copy-start(f32[128,1,32,64]{0,3,2,1:T(8,128)} %fusion.48) | copy-start | bytes 3145732
  226.6 2.5 dynamic-slice-start
  231.0 14.5 %collective-permute-start = (bf16[128,2048]{1,0:T(8,128)(2,1)S(1)}, bf16[128,2048]{1,0:T(8,128)(2,1)S(1)}, u32[]{:S(2)}, u32[]{:S(2)}) collective-permute-start(bf16[128,2048]{1,0:T(8,128)(2,1)S(1)} %get-tuple-element.263), channel_id=1, source_target_pairs={{0,64},{64,0},{1,65},{65,1},{2,66},{66,2},{3,67},{67,3},{4,68},{68... | collective-permute-start | bytes 1572872 | tf_op jit(solution)/shard_map/ppermute | solution.py:85
  253.6 26.8 %copy-start.3 = (bf16[128,2048]{1,0:T(8,128)(2,1)S(1)}, bf16[128,2048]{1,0:T(8,128)(2,1)}, u32[]{:S(2)}) copy-start(bf16[128,2048]{1,0:T(8,128)(2,1)} %param.17) | copy-start | bytes 1572868
  253.6 12.1 %collective-permute-start.1 = (bf16[128,2048]{1,0:T(8,128)(2,1)S(1)}, bf16[128,2048]{1,0:T(8,128)(2,1)S(1)}, u32[]{:S(2)}, u32[]{:S(2)}) collective-permute-start(bf16[128,2048]{1,0:T(8,128)(2,1)S(1)} %fusion.37), channel_id=1, source_target_pairs={{0,1},{1,0},{2,3},{3,2},{4,5},{5,4},{6,7},{7,6},{8,9},{9,8},{10,11... | collective-permute-start | bytes 1572872 | tf_op jit(solution)/shard_map/ppermute | solution.py:85
  254.4 26.0 %collective-permute-start.3 = (bf16[128,2048]{1,0:T(8,128)(2,1)S(1)}, bf16[128,2048]{1,0:T(8,128)(2,1)S(1)}, u32[]{:S(2)}, u32[]{:S(2)}) collective-permute-start(bf16[128,2048]{1,0:T(8,128)(2,1)S(1)} %fusion.37), channel_id=1, source_target_pairs={{0,65},{1,64},{2,67},{3,66},{4,69},{5,68},{6,71},{7,70},{8,73},{9,... | collective-permute-start | bytes 1572872 | tf_op jit(solution)/shard_map/ppermute | solution.py:303
  263.8 16.6 %collective-permute-start.2 = (bf16[128,2048]{1,0:T(8,128)(2,1)S(1)}, bf16[128,2048]{1,0:T(8,128)(2,1)S(1)}, u32[]{:S(2)}, u32[]{:S(2)}) collective-permute-start(bf16[128,2048]{1,0:T(8,128)(2,1)S(1)} %get-tuple-element.270), channel_id=1, source_target_pairs={{0,64},{1,65},{2,66},{3,67},{4,68},{5,69},{6,70},{7,71},{8,72},{9,... | collective-permute-start | bytes 1572872 | tf_op jit(solution)/shard_map/ppermute | solution.py:91
Sparse Core Ops, SparseCore 0:
  9.5 201.1 all-gather.1

commit v8 on v7

--- a/solution.py
+++ b/solution.py
@@ -228,8 +228,7 @@
         jnp.zeros((kv_count, per_key, rows_here, HEAD_DIM), jnp.float32),
     )
     running = start_state
-    both = gathered(jnp.concatenate([keys, values], axis=1), CTX)
-    both = both.reshape(-1, both.shape[-1])
+    both = lax.all_gather(jnp.concatenate([keys, values], axis=1), CTX, axis=0, tiled=True)
     key_piece = both[:, : keys.shape[1]]
     value_piece = both[:, keys.shape[1] :]
     count = key_piece.shape[0]

time: 290 us -> 260 us (0.90)
  waiting for transfers between devices: 137 us -> 105 us
  starting transfers between devices: 32.5 us -> 27.5 us
  local copies, waits for them, and re-layouts: 17.8 us -> 22.2 us
    all_to_all x4 -> x3, waiting for transfers between devices: 108 us -> 59.6 us  [gathered(): return lax.all_to_all(spread, axis, 0, 0)]
    all_gather x1, waiting for transfers between devices: 0.01 us -> 16.5 us  [per_device(): weights_all = lax.all_gather(out_weights, CTX, axis=2, tiled=True)[0]]
    all_to_all x4 -> x3, starting transfers between devices: 27.7 us -> 22.2 us  [gathered(): return lax.all_to_all(spread, axis, 0, 0)]
    cond x4 -> x20, local copies, waits for them, and re-layouts: 0.01 us -> 3.91 us
    dot_general x4, matrix products: 9.06 us -> 5.23 us  [absorb(): jnp.einsum('qgjd,kgd->gjqk', query_groups, key_rows, preferred_element_ty...]
    broadcast_in_dim x5 -> x4, local copies, waits for them, and re-layouts: 7.15 us -> 5.55 us  [gathered(): spread = jnp.broadcast_to(x[None], (peers,) + x.shape)]
  transfers between devices with their start and end apart: 9 -> 9, of which waited for: 6 -> 6; matrix products, arithmetic and copies ran while one was open for 31% -> 35% of each run, Pallas kernels for 0% -> 0%
where the time goes in v8:
time: 260 us; the launch traced here: 257 us
  waiting for transfers between devices  105 us (40%)
  matrix products  63.5 us (24%)
  starting transfers between devices  27.5 us (11%)
  local copies, waits for them, and re-layouts  22.2 us (9%)
  other arithmetic  19.3 us (7%)
  between operations  13.7 us (5%)
  loops' own time  5.3 us (2%)
    all_to_all x3, waiting for transfers between devices, gathered(): return lax.all_to_all(spread, axis, 0, 0)  59.6 us
    all_to_all x3, starting transfers between devices, gathered(): return lax.all_to_all(spread, axis, 0, 0)  22.2 us
    all_gather x1, waiting for transfers between devices, per_device(): weights_all = lax.all_gather(out_weights, CTX, axis=2, tiled=True)[0]  16.5 us
    ppermute x1, waiting for transfers between devices, per_device(): first_sent = lax.ppermute(sent, ('pipe', 'tp'), [(0, 3), (1, 2)])  14.9 us
    dot_general x4, matrix products, absorb(): jnp.einsum('gjqk,kgd->gjqd', weights_exp.astype(jnp.bfloat16), value_rows...  14.5 us
    ppermute x2, waiting for transfers between devices, from_partner(): return lax.ppermute(block, axis, route)  13.6 us
    dot_general x1, matrix products, entering_states(): jnp.einsum('kgj,kgjpn->gjpn', span_weight(near_ids, rank), near, precisio...  9.39 us
    dot_general x1, matrix products, per_device(): kept = jnp.dot(mixed_rows, kept_cols, preferred_element_type=jnp.float32)  8.11 us
  transfers between devices with their start and end apart: 9, of which 6 were waited for; matrix products, arithmetic and copies ran while one was open for 35% of the time, Pallas kernels for 0%

profile of v8, /device:TPU:30, one launch (start us, length us, event | category | flops | bytes accessed | tf_op | source)
XLA Modules:
  0.0 256.7 jit_solution(15561698532046448180)
XLA Ops:
  6.5 0.8 constant_dynamic-slice_fusion.1
  7.4 0.6 pad_maximum_fusion
  8.1 0.7 all-gather.5.cloned.1.call-update
  8.8 0.7 constant_dynamic-slice_fusion.3
  9.6 0.7 dynamic_slice.81
  10.5 0.6 broadcast_in_dim.208
  11.1 8.4 %all-to-all-start = ((f32[32,1,32]{2,1,0:T(1,128)}), f32[32,1,32]{2,1,0:T(1,128)S(1)}, u32[]{:S(2)}, u32[]{:S(2)}) async-start(f32[32,1,32]{2,1,0:T(1,128)} %broadcast_in_dim.208), calls=%async_computation | async-start | bytes 32768 | tf_op jit(solution)/shard_map/all_to_all | solution.py:43
  19.6 1.3 constant_dynamic-slice_fusion
  21.2 0.6 fusion.56
  21.9 3.2 %all-to-all-done = f32[32,1,32]{2,1,0:T(1,128)S(1)} async-done(((f32[32,1,32]{2,1,0:T(1,128)}), f32[32,1,32]{2,1,0:T(1,128)S(1)}, u32[]{:S(2)}, u32[]{:S(2)}) %all-to-all-start) | async-done | bytes 4128 | tf_op jit(solution)/shard_map/all_to_all | solution.py:43
  25.0 3.0 %broadcast_in_dim.214 = bf16[8,1,32,64,128]{4,3,2,1,0:T(8,128)(2,1)} broadcast(bf16[32,64,128]{2,1,0:T(8,128)(2,1)S(1)} %fusion.56), dimensions={2,3,4} | broadcast | bytes 4718592 | tf_op jit(solution)/shard_map/broadcast_in_dim | solution.py:42
  28.1 4.7 %all-to-all-start.1 = ((bf16[8,1,32,64,128]{4,3,2,1,0:T(8,128)(2,1)}), bf16[8,1,32,64,128]{4,3,2,1,0:T(8,128)(2,1)}, u32[]{:S(2)}, u32[]{:S(2)}) async-start(bf16[8,1,32,64,128]{4,3,2,1,0:T(8,128)(2,1)} %broadcast_in_dim.214), calls=%async_computation.1 | async-start | bytes 8388608 | tf_op jit(solution)/shard_map/all_to_all | solution.py:43
  34.6 3.4 %fusion.48 = f32[128,1,32,64]{0,3,2,1:T(8,128)} fusion(bf16[128,32,64]{0,2,1:T(8,128)(2,1)S(1)} %bitcast.166, f32[32,128]{1,0:T(8,128)S(1)} %fusion.109, f32[128,32]{0,1:T(8,128)S(1)} %copy.65, f32[128,128]{1,0:T(8,128)S(1)} %fusion.84, pred[128,128]{1,0:T(8,128)(4,1)S(1)} %iota_compare_fusion), kind=kOutput, calls=%fused_computation.49 | convolution fusion | flops 404750336 | bytes 1687552 | tf_op jit(solution)/shard_map/while/body/eval_jaxpr/gjts,sgjp->tgjp/dot_general | solution.py:108
  38.9 56.4 %all-to-all-done.1 = bf16[8,1,32,64,128]{4,3,2,1,0:T(8,128)(2,1)} async-done(((bf16[8,1,32,64,128]{4,3,2,1,0:T(8,128)(2,1)}), bf16[8,1,32,64,128]{4,3,2,1,0:T(8,128)(2,1)}, u32[]{:S(2)}, u32[]{:S(2)}) %all-to-all-start.1) | async-done | bytes 4194336 | tf_op jit(solution)/shard_map/all_to_all | solution.py:43
  95.3 7.1 %fusion.33 = f32[32,1,64,128]{3,1,2,0:T(1,128)S(1)} fusion(f32[8,32,1,1]{0,2,3,1:T(1,128)S(1)} %copy.79, bf16[8,32,64,128]{3,2,1,0:T(8,128)(2,1)} %bitcast.28), kind=kOutput, calls=%fused_computation.35 | convolution fusion | flops 25165824 | bytes 5243904 | tf_op jit(solution)/shard_map/kgj,kgjpn->gjpn/dot_general | solution.py:67
  102.5 1.9 broadcast_in_dim.223
  104.4 9.1 %all-to-all-start.2 = ((bf16[4,1,32,64,128]{4,3,2,1,0:T(8,128)(2,1)}), bf16[4,1,32,64,128]{4,3,2,1,0:T(8,128)(2,1)}, u32[]{:S(2)}, u32[]{:S(2)}) async-start(bf16[4,1,32,64,128]{4,3,2,1,0:T(8,128)(2,1)} %broadcast_in_dim.223), calls=%async_computation.2 | async-start | bytes 4194304 | tf_op jit(solution)/shard_map/all_to_all | solution.py:43
  113.5 9.4 %fusion.35 = f32[32,1,64,128]{3,1,2,0:T(1,128)} fusion(f32[8,32,1,1]{0,2,3,1:T(1,128)S(1)} %copy.76, bf16[8,32,64,128]{3,2,1,0:T(8,128)(2,1)} %bitcast.28), kind=kOutput, calls=%fused_computation.37 | convolution fusion | flops 25165824 | bytes 5243904 | tf_op jit(solution)/shard_map/kgj,kgjpn->gjpn/dot_general | solution.py:63
  122.9 2.8 %fusion.102 = (bf16[4096,128]{1,0:T(8,128)(2,1)}, bf16[4096,128]{1,0:T(8,128)(2,1)S(1)}) fusion(bf16[4096,256]{1,0:T(8,128)(2,1)} %all-gather.3.cloned.1.call-done), kind=kLoop, calls=%fused_computation.146 | loop fusion | bytes 4194304 | tf_op jit(solution)/shard_map/slice | solution.py:233
  125.7 1.1 broadcast_in_dim.226
  126.8 42.8 %while.4 = (s32[]{:T(128)}, f32[1,16,128]{2,1,0:T(8,128)S(1)}, f32[1,16,128]{2,1,0:T(8,128)S(1)}, f32[1,16,128,128]{3,2,1,0:T(8,128)}, s32[4]{0:T(128)S(1)}, /*i...) while((s32[]{:T(128)}, f32[1,16,128]{2,1,0:T(8,128)S(1)}, ...), condition=%wide.region_10.11_spmd.clone, body=%wide.region_5.10_spmd.clone.sunk | while | flops 1101667456 | bytes 37366608 | solution.py:240
  126.8 0.6 dynamic_slice.146
  128.6 8.9 %conditional.3 = ((f32[1,16,128]{2,1,0:T(8,128)S(1)}, f32[1,16,128]{2,1,0:T(8,128)S(1)}, f32[1,16,128,128]{3,2,1,0:T(8,128)})) conditional(s32[]{:T(128)} %convert_element_type.185, (f32[1,16,128]{2,1,0:T(8,128)S(1)}, f32[1,16,128]{2,1,0:T(8,128)S(1)}, f32[1,16,128,128]{3,2,1,0:T(8,128)}) %tuple.54, (s32[]{:T(128)}, s32[]{:T(128)}, ...), branch_computations={%region_6.6_spmd, %region_7.9_spmd} | conditional | flops 1101667456 | bytes 37365860 | solution.py:223
  128.6 0.7 iota_add_fusion
  129.5 1.3 fusion.2
  130.8 2.0 fusion.4
  132.9 3.6 %fusion.12 = f32[1,16,128,128]{3,2,1,0:T(8,128)S(1)} fusion(f32[1024,128,16]{1,0,2:T(8,128)S(1)} %get-tuple-element.261, f32[16,128]{1,0:T(8,128)S(1)} %bitcast.163, pred[128,1024]{0,1:T(8,128)(4,1)S(1)} %broadcast_compare_fusion, f32[1,16,128,128]{3,2,1,0:T(8,128)S(1)} %copy-done.2, f32[16,128]{1,0:T(8,128)S(1)} %get-tuple-element.258, ...), kind=kOutput, calls=%fused_computation.10 | convolution fusion | flops 547880960 | bytes 10895872 | tf_op jit(solution)/shard_map/while/body/eval_jaxpr/cond/branch_1_fun/gjqk,kgd->gjqd/dot_general | solution.py:215
  136.5 1.0 copy-done.3
  139.2 8.9 %conditional.3 = ((f32[1,16,128]{2,1,0:T(8,128)S(1)}, f32[1,16,128]{2,1,0:T(8,128)S(1)}, f32[1,16,128,128]{3,2,1,0:T(8,128)})) conditional(s32[]{:T(128)} %convert_element_type.185, (f32[1,16,128]{2,1,0:T(8,128)S(1)}, f32[1,16,128]{2,1,0:T(8,128)S(1)}, f32[1,16,128,128]{3,2,1,0:T(8,128)}) %tuple.54, (s32[]{:T(128)}, s32[]{:T(128)}, ...), branch_computations={%region_6.6_spmd, %region_7.9_spmd} | conditional | flops 1101667456 | bytes 37365860 | solution.py:223
  139.3 0.7 iota_add_fusion
  140.1 1.3 fusion.2
  141.5 2.0 fusion.4
  143.5 3.6 %fusion.12 = f32[1,16,128,128]{3,2,1,0:T(8,128)S(1)} fusion(f32[1024,128,16]{1,0,2:T(8,128)S(1)} %get-tuple-element.261, f32[16,128]{1,0:T(8,128)S(1)} %bitcast.163, pred[128,1024]{0,1:T(8,128)(4,1)S(1)} %broadcast_compare_fusion, f32[1,16,128,128]{3,2,1,0:T(8,128)S(1)} %copy-done.2, f32[16,128]{1,0:T(8,128)S(1)} %get-tuple-element.258, ...), kind=kOutput, calls=%fused_computation.10 | convolution fusion | flops 547880960 | bytes 10895872 | tf_op jit(solution)/shard_map/while/body/eval_jaxpr/cond/branch_1_fun/gjqk,kgd->gjqd/dot_general | solution.py:215
  147.1 1.0 copy-done.3
  149.9 8.9 %conditional.3 = ((f32[1,16,128]{2,1,0:T(8,128)S(1)}, f32[1,16,128]{2,1,0:T(8,128)S(1)}, f32[1,16,128,128]{3,2,1,0:T(8,128)})) conditional(s32[]{:T(128)} %convert_element_type.185, (f32[1,16,128]{2,1,0:T(8,128)S(1)}, f32[1,16,128]{2,1,0:T(8,128)S(1)}, f32[1,16,128,128]{3,2,1,0:T(8,128)}) %tuple.54, (s32[]{:T(128)}, s32[]{:T(128)}, ...), branch_computations={%region_6.6_spmd, %region_7.9_spmd} | conditional | flops 1101667456 | bytes 37365860 | solution.py:223
  149.9 0.7 iota_add_fusion
  150.8 1.3 fusion.2
  152.2 2.0 fusion.4
  154.2 3.6 %fusion.12 = f32[1,16,128,128]{3,2,1,0:T(8,128)S(1)} fusion(f32[1024,128,16]{1,0,2:T(8,128)S(1)} %get-tuple-element.261, f32[16,128]{1,0:T(8,128)S(1)} %bitcast.163, pred[128,1024]{0,1:T(8,128)(4,1)S(1)} %broadcast_compare_fusion, f32[1,16,128,128]{3,2,1,0:T(8,128)S(1)} %copy-done.2, f32[16,128]{1,0:T(8,128)S(1)} %get-tuple-element.258, ...), kind=kOutput, calls=%fused_computation.10 | convolution fusion | flops 547880960 | bytes 10895872 | tf_op jit(solution)/shard_map/while/body/eval_jaxpr/cond/branch_1_fun/gjqk,kgd->gjqd/dot_general | solution.py:215
  157.8 1.0 copy-done.3
  158.8 0.6 dynamic_slice.146
  160.6 9.0 %conditional.3 = ((f32[1,16,128]{2,1,0:T(8,128)S(1)}, f32[1,16,128]{2,1,0:T(8,128)S(1)}, f32[1,16,128,128]{3,2,1,0:T(8,128)})) conditional(s32[]{:T(128)} %convert_element_type.185, (f32[1,16,128]{2,1,0:T(8,128)S(1)}, f32[1,16,128]{2,1,0:T(8,128)S(1)}, f32[1,16,128,128]{3,2,1,0:T(8,128)}) %tuple.54, (s32[]{:T(128)}, s32[]{:T(128)}, ...), branch_computations={%region_6.6_spmd, %region_7.9_spmd} | conditional | flops 1101667456 | bytes 37365860 | solution.py:223
  160.6 0.7 iota_add_fusion
  161.5 1.3 fusion.2
  162.9 2.0 fusion.4
  164.9 3.7 %fusion.12 = f32[1,16,128,128]{3,2,1,0:T(8,128)S(1)} fusion(f32[1024,128,16]{1,0,2:T(8,128)S(1)} %get-tuple-element.261, f32[16,128]{1,0:T(8,128)S(1)} %bitcast.163, pred[128,1024]{0,1:T(8,128)(4,1)S(1)} %broadcast_compare_fusion, f32[1,16,128,128]{3,2,1,0:T(8,128)S(1)} %copy-done.2, f32[16,128]{1,0:T(8,128)S(1)} %get-tuple-element.258, ...), kind=kOutput, calls=%fused_computation.10 | convolution fusion | flops 547880960 | bytes 10895872 | tf_op jit(solution)/shard_map/while/body/eval_jaxpr/cond/branch_1_fun/gjqk,kgd->gjqd/dot_general | solution.py:215
  168.6 1.0 copy-done.3
  169.6 1.7 fusion.79
  171.6 5.6 %fusion.46 = f32[32,1,64,128]{3,1,2,0:T(1,128)S(1)} fusion(f32[4,32,1,1]{0,2,3,1:T(1,128)S(1)} %copy.81, bf16[4,32,64,128]{3,2,1,0:T(8,128)(2,1)} %bitcast.35), kind=kOutput, calls=%fused_computation.47 | convolution fusion | flops 12582912 | bytes 3146240 | tf_op jit(solution)/shard_map/kgj,kgjpn->gjpn/dot_general | solution.py:74
  177.3 0.7 fusion.55
  178.0 0.6 fusion.54
  178.9 1.5 multiply_reduce_fusion
  180.5 1.6 bitcast_select_fusion.2
  182.1 1.5 collective-permute-start
  183.6 11.3 %collective-permute-done = bf16[128,2048]{1,0:T(8,128)(2,1)S(1)} collective-permute-done((bf16[128,2048]{1,0:T(8,128)(2,1)S(1)}, bf16[128,2048]{1,0:T(8,128)(2,1)S(1)}, u32[]{:S(2)}, u32[]{:S(2)}) %collective-permute-start) | collective-permute-done | bytes 524320 | tf_op jit(solution)/shard_map/ppermute | solution.py:85
  194.9 16.5 %all-gather.5.cloned.1.call-done = bf16[1,4096,4096]{2,1,0:T(8,128)(2,1)} async-done(((bf16[1,4096,128]{2,1,0:T(8,128)(2,1)}), bf16[1,4096,4096]{2,1,0:T(8,128)(2,1)}) %all-gather.5.cloned.1.call-update) | async-done | bytes 33554448 | tf_op jit(solution)/shard_map/all_gather | solution.py:292
  211.4 8.1 %fusion.37 = bf16[128,2048]{1,0:T(8,128)(2,1)S(1)} fusion(bf16[1,4096,4096]{2,1,0:T(8,128)(2,1)} %all-gather.5.cloned.1.call-done, s32[]{:T(128)S(6)} %select_n.148, bf16[128,2048]{1,0:T(8,128)(2,1)S(1)} %collective-permute-done, bf16[128,2048]{1,0:T(8,128)(2,1)S(1)} %get-tuple-element.262, pred[]{:T(512)S(6)} %eq.2), kind=kOutput, calls=%fused_computation.39 | convolution fusion | flops 2152464384 | bytes 18350084 | tf_op jit(solution)/shard_map/dot_general | solution.py:297
  219.5 0.9 collective-permute-start.1
  220.5 1.5 collective-permute-start.3
  222.0 8.1 %fusion.104 = (bf16[128,2048]{1,0:T(8,128)(2,1)S(1)}, f32[128,2048]{1,0:T(8,128)S(1)}) fusion(bf16[1,4096,4096]{2,1,0:T(8,128)(2,1)} %all-gather.5.cloned.1.call-done, s32[]{:T(128)S(6)} %select_n.147, bf16[128,2048]{1,0:T(8,128)(2,1)S(1)} %collective-permute-done, bf16[128,2048]{1,0:T(8,128)(2,1)S(1)} %get-tuple-element.262, pred[]{:T(512)S(6)} %eq.2), kind=kOutput, calls=%fused_computation.148 | convolution fusion | flops 2152464384 | bytes 19398660 | tf_op jit(solution)/shard_map/dot_general | solution.py:299
  230.1 1.3 collective-permute-start.2
  231.4 2.2 collective-permute-done.1
  233.7 14.9 %collective-permute-done.3 = bf16[128,2048]{1,0:T(8,128)(2,1)S(1)} collective-permute-done((bf16[128,2048]{1,0:T(8,128)(2,1)S(1)}, bf16[128,2048]{1,0:T(8,128)(2,1)S(1)}, u32[]{:S(2)}, u32[]{:S(2)}) %collective-permute-start.3) | collective-permute-done | bytes 524320 | tf_op jit(solution)/shard_map/ppermute | solution.py:302
  248.6 1.3 fusion.76
  (102 shorter events, 6.3 us)
Async XLA Ops:
  6.5 27.9 %copy-start = (bf16[128,256]{1,0:T(8,128)(2,1)S(1)}, bf16[128,256]{1,0:T(8,128)(2,1)}, u32[]{:S(2)}) copy-start(bf16[128,256]{1,0:T(8,128)(2,1)} %param.21) | copy-start | bytes 196612
  6.5 14.7 %copy-start.6 = (bf16[128,256]{1,0:T(8,128)(2,1)S(1)}, bf16[128,256]{1,0:T(8,128)(2,1)}, u32[]{:S(2)}) copy-start(bf16[128,256]{1,0:T(8,128)(2,1)} %param.20) | copy-start | bytes 196612
  6.5 116.4 %all-gather.3.cloned.1.call-start = ((), (), s32[]{:S(2)}) async-start(), calls=%async_computation.3 | async-start | bytes 2162688 | tf_op jit(solution)/shard_map/all_gather | solution.py:231
  8.0 203.4 %all-gather.5.cloned.1.call-start = ((), (), s32[]{:S(2)}) async-start(), calls=%async_computation.4 | async-start | bytes 34603008 | tf_op jit(solution)/shard_map/all_gather | solution.py:292
  11.1 13.9 %all-to-all-start = ((f32[32,1,32]{2,1,0:T(1,128)}), f32[32,1,32]{2,1,0:T(1,128)S(1)}, u32[]{:S(2)}, u32[]{:S(2)}) async-start(f32[32,1,32]{2,1,0:T(1,128)} %broadcast_in_dim.208), calls=%async_computation | async-start | bytes 32768 | tf_op jit(solution)/shard_map/all_to_all | solution.py:43
  28.1 5.0 %copy-start.8 = (f32[64]{0:T(128)S(1)}, f32[64]{0:T(128)}, u32[]{:S(2)}) copy-start(f32[64]{0:T(128)} %param.24) | copy-start | bytes 772
  28.1 6.4 %copy-start.7 = (f32[128,64]{0,1:T(8,128)S(1)}, f32[128,64]{0,1:T(8,128)}, u32[]{:S(2)}) copy-start(f32[128,64]{0,1:T(8,128)} %param.22) | copy-start | bytes 98308
  28.1 67.2 %all-to-all-start.1 = ((bf16[8,1,32,64,128]{4,3,2,1,0:T(8,128)(2,1)}), bf16[8,1,32,64,128]{4,3,2,1,0:T(8,128)(2,1)}, u32[]{:S(2)}, u32[]{:S(2)}) async-start(bf16[8,1,32,64,128]{4,3,2,1,0:T(8,128)(2,1)} %broadcast_in_dim.214), calls=%async_computation.1 | async-start | bytes 8388608 | tf_op jit(solution)/shard_map/all_to_all | solution.py:43
  104.4 67.2 %all-to-all-start.2 = ((bf16[4,1,32,64,128]{4,3,2,1,0:T(8,128)(2,1)}), bf16[4,1,32,64,128]{4,3,2,1,0:T(8,128)(2,1)}, u32[]{:S(2)}, u32[]{:S(2)}) async-start(bf16[4,1,32,64,128]{4,3,2,1,0:T(8,128)(2,1)} %broadcast_in_dim.223), calls=%async_computation.2 | async-start | bytes 4194304 | tf_op jit(solution)/shard_map/all_to_all | solution.py:43
  130.8 2.0 copy-start.2
  136.5 1.0 copy-start.3
  141.5 2.0 copy-start.2
  147.1 1.0 copy-start.3
  152.2 2.0 copy-start.2
  157.8 1.0 copy-start.3
  162.8 2.0 copy-start.2
  168.6 1.0 copy-start.3
  169.6 7.7 %copy-start.1 = (f32[32,1,64,128]{3,1,2,0:T(1,128)S(1)}, f32[32,1,64,128]{3,1,2,0:T(1,128)}, u32[]{:S(2)}) copy-start(f32[32,1,64,128]{3,1,2,0:T(1,128)} %fusion.35) | copy-start | bytes 3145732
  171.6 6.3 %copy-start.4 = (f32[128,1,32,64]{0,3,2,1:T(8,128)S(1)}, f32[128,1,32,64]{0,3,2,1:T(8,128)}, u32[]{:S(2)}) copy-start(f32[128,1,32,64]{0,3,2,1:T(8,128)} %fusion.48) | copy-start | bytes 3145732
  178.0 2.5 dynamic-slice-start
  182.1 12.8 %collective-permute-start = (bf16[128,2048]{1,0:T(8,128)(2,1)S(1)}, bf16[128,2048]{1,0:T(8,128)(2,1)S(1)}, u32[]{:S(2)}, u32[]{:S(2)}) collective-permute-start(bf16[128,2048]{1,0:T(8,128)(2,1)S(1)} %get-tuple-element.263), channel_id=1, source_target_pairs={{0,64},{64,0},{1,65},{65,1},{2,66},{66,2},{3,67},{67,3},{4,68},{68... | collective-permute-start | bytes 1572872 | tf_op jit(solution)/shard_map/ppermute | solution.py:85
  219.5 29.1 %copy-start.5 = (bf16[128,2048]{1,0:T(8,128)(2,1)S(1)}, bf16[128,2048]{1,0:T(8,128)(2,1)}, u32[]{:S(2)}) copy-start(bf16[128,2048]{1,0:T(8,128)(2,1)} %param.17) | copy-start | bytes 1572868
  219.5 14.2 %collective-permute-start.1 = (bf16[128,2048]{1,0:T(8,128)(2,1)S(1)}, bf16[128,2048]{1,0:T(8,128)(2,1)S(1)}, u32[]{:S(2)}, u32[]{:S(2)}) collective-permute-start(bf16[128,2048]{1,0:T(8,128)(2,1)S(1)} %fusion.37), channel_id=1, source_target_pairs={{0,1},{1,0},{2,3},{3,2},{4,5},{5,4},{6,7},{7,6},{8,9},{9,8},{10,11... | collective-permute-start | bytes 1572872 | tf_op jit(solution)/shard_map/ppermute | solution.py:85
  220.5 28.1 %collective-permute-start.3 = (bf16[128,2048]{1,0:T(8,128)(2,1)S(1)}, bf16[128,2048]{1,0:T(8,128)(2,1)S(1)}, u32[]{:S(2)}, u32[]{:S(2)}) collective-permute-start(bf16[128,2048]{1,0:T(8,128)(2,1)S(1)} %fusion.37), channel_id=1, source_target_pairs={{0,65},{1,64},{2,67},{3,66},{4,69},{5,68},{6,71},{7,70},{8,73},{9,... | collective-permute-start | bytes 1572872 | tf_op jit(solution)/shard_map/ppermute | solution.py:302
  230.1 18.5 %collective-permute-start.2 = (bf16[128,2048]{1,0:T(8,128)(2,1)S(1)}, bf16[128,2048]{1,0:T(8,128)(2,1)S(1)}, u32[]{:S(2)}, u32[]{:S(2)}) collective-permute-start(bf16[128,2048]{1,0:T(8,128)(2,1)S(1)} %get-tuple-element.270), channel_id=1, source_target_pairs={{0,64},{1,65},{2,66},{3,67},{4,68},{5,69},{6,70},{7,71},{8,72},{9,... | collective-permute-start | bytes 1572872 | tf_op jit(solution)/shard_map/ppermute | solution.py:91
Sparse Core Ops, SparseCore 0:
  9.6 47.7 all-gather.2
  59.6 151.7 all-gather.4

commit v9 on v8

--- a/solution.py
+++ b/solution.py
@@ -185,9 +185,9 @@
     return gate_norm(values_y.reshape(rows_here, -1), ssm_gate, norm_gain, groups)
 
 
-def attention(queries, keys, values, ctx_rank):
+def attention(queries, both, key_width, ctx_rank):
     rows_here = queries.shape[0]
-    kv_count = keys.shape[1] // HEAD_DIM
+    kv_count = key_width // HEAD_DIM
     per_key = queries.shape[1] // HEAD_DIM // kv_count
     query_groups = queries.reshape(rows_here, kv_count, per_key, HEAD_DIM)
     query_pos = ctx_rank * rows_here + jnp.arange(rows_here, dtype=jnp.int32)
@@ -228,9 +228,8 @@
         jnp.zeros((kv_count, per_key, rows_here, HEAD_DIM), jnp.float32),
     )
     running = start_state
-    both = lax.all_gather(jnp.concatenate([keys, values], axis=1), CTX, axis=0, tiled=True)
-    key_piece = both[:, : keys.shape[1]]
-    value_piece = both[:, keys.shape[1] :]
+    key_piece = both[:, :key_width]
+    value_piece = both[:, key_width:]
     count = key_piece.shape[0]
     width = math.gcd(count, 1024)
     blocks = count // width
@@ -275,11 +274,16 @@
         take_half(skip_gain, 0, section),
         take_half(norm_gain, 0, section),
     )
+    key_half = take_half(keys, 1, section)
+    kv_own = jnp.concatenate([key_half, take_half(values, 1, section)], axis=1)
+    weights_own = out_weights[0].T
+    channels = weights_own.shape[1]
+    joint = lax.all_gather(
+        jnp.concatenate([weights_own, kv_own], axis=1), CTX, axis=0, tiled=True
+    )
+    weights_t = joint[:, :channels]
     attn_part = attention(
-        take_half(queries, 1, section),
-        take_half(keys, 1, section),
-        take_half(values, 1, section),
-        ctx_rank,
+        take_half(queries, 1, section), joint[:, channels:], key_half.shape[1], ctx_rank
     )
     outgoing = jnp.where(section == 0, attn_part, mamba_part)
     kept_half = jnp.where(section == 0, mamba_part, attn_part)
@@ -289,14 +293,15 @@
         jnp.concatenate([kept_half, incoming], axis=1),
         jnp.concatenate([incoming, kept_half], axis=1),
     )
-    weights_all = lax.all_gather(out_weights, CTX, axis=2, tiled=True)[0]
-    half = weights_all.shape[1] // 2
+    half = weights_t.shape[0] // 2
     tp_rank = lax.axis_index("tp")
-    sent_cols = lax.dynamic_slice_in_dim(weights_all, (1 - tp_rank) * half, half, 1)
-    kept_cols = lax.dynamic_slice_in_dim(weights_all, tp_rank * half, half, 1)
-    sent = jnp.dot(mixed_rows, sent_cols, preferred_element_type=jnp.float32).astype(jnp.bfloat16)
+    sent_cols = lax.dynamic_slice_in_dim(weights_t, (1 - tp_rank) * half, half, 0)
+    kept_cols = lax.dynamic_slice_in_dim(weights_t, tp_rank * half, half, 0)
+    sent = jnp.einsum(
+        "tc,dc->td", mixed_rows, sent_cols, preferred_element_type=jnp.float32
+    ).astype(jnp.bfloat16)
     from_tp = from_partner(sent, "tp", 0)
-    kept = jnp.dot(mixed_rows, kept_cols, preferred_element_type=jnp.float32)
+    kept = jnp.einsum("tc,dc->td", mixed_rows, kept_cols, preferred_element_type=jnp.float32)
     kept_low = kept.astype(jnp.bfloat16)
     first_kept = shifted(kept_low, "pipe", 1)
     first_sent = lax.ppermute(sent, ("pipe", "tp"), [(0, 3), (1, 2)])

time: 260 us -> 318 us (1.22)
  waiting for transfers between devices: 105 us -> 140 us
  local copies, waits for them, and re-layouts: 22.2 us -> 50.1 us
    all_to_all x3, waiting for transfers between devices: 59.6 us -> 106 us  [gathered(): return lax.all_to_all(spread, axis, 0, 0)]
    slice x1 -> x4, local copies, waits for them, and re-layouts: 2.77 us -> 29.9 us  [the longest x1 22.9 us: per_device(): weights_t = joint[:, :channels]]
    ppermute x2, waiting for transfers between devices: 13.6 us -> 2.63 us  [from_partner(): return lax.ppermute(block, axis, route)]
    all_gather x2 -> x1, waiting for transfers between devices: 16.5 us -> 17.1 us  [per_device(): lax.all_gather(jnp.concatenate([weights_own, kv_own], axis=1), CTX, axis=...]
  transfers between devices with their start and end apart: 9 -> 8, of which waited for: 6 -> 6; matrix products, arithmetic and copies ran while one was open for 35% -> 22% of each run, Pallas kernels for 0% -> 0%
where the time goes in v9:
time: 318 us; the launch traced here: 317 us
  waiting for transfers between devices  140 us (44%)
  matrix products  61.6 us (19%)
  local copies, waits for them, and re-layouts  50.1 us (16%)
  starting transfers between devices  24.9 us (8%)
  other arithmetic  20.7 us (7%)
  between operations  13.8 us (4%)
  loops' own time  5.49 us (2%)
    all_to_all x3, waiting for transfers between devices, gathered(): return lax.all_to_all(spread, axis, 0, 0)  106 us
    slice x1, local copies, waits for them, and re-layouts, per_device(): weights_t = joint[:, :channels]  22.9 us
    all_to_all x3, starting transfers between devices, gathered(): return lax.all_to_all(spread, axis, 0, 0)  20.3 us
    all_gather x1, waiting for transfers between devices, per_device(): lax.all_gather(jnp.concatenate([weights_own, kv_own], axis=1), CTX, axis=...  17.1 us
    ppermute x1, waiting for transfers between devices, per_device(): first_sent = lax.ppermute(sent, ('pipe', 'tp'), [(0, 3), (1, 2)])  14.5 us
    dot_general x4, matrix products, absorb(): jnp.einsum('gjqk,kgd->gjqd', weights_exp.astype(jnp.bfloat16), value_rows...  14.4 us
    dot_general x1, matrix products, per_device(): jnp.einsum('tc,dc->td', mixed_rows, kept_cols, preferred_element_type=jnp...  8.15 us
    dot_general x1, matrix products, per_device(): jnp.einsum('tc,dc->td', mixed_rows, sent_cols, preferred_element_type=jnp...  8.11 us
  transfers between devices with their start and end apart: 8, of which 6 were waited for; matrix products, arithmetic and copies ran while one was open for 22% of the time, Pallas kernels for 0%

profile of v9, /device:TPU:30, one launch (start us, length us, event | category | flops | bytes accessed | tf_op | source)
XLA Modules:
  0.0 316.8 jit_solution(12531188397768244114)
XLA Ops:
  6.6 0.9 constant_dynamic-slice_fusion.1
  7.7 2.3 pad_maximum_fusion
  10.0 0.7 constant_dynamic-slice_fusion.3
  10.8 0.7 dynamic_slice.77
  12.4 8.4 %all-to-all-start = ((f32[32,1,32]{2,1,0:T(1,128)}), f32[32,1,32]{2,1,0:T(1,128)S(1)}, u32[]{:S(2)}, u32[]{:S(2)}) async-start(f32[32,1,32]{2,1,0:T(1,128)} %broadcast_in_dim.208), calls=%async_computation | async-start | bytes 32768 | tf_op jit(solution)/shard_map/all_to_all | solution.py:43
  20.8 1.2 constant_dynamic-slice_fusion
  22.3 0.7 fusion.54
  23.0 3.2 all-to-all-done
  26.2 3.1 broadcast_in_dim.214
  29.2 4.7 %all-to-all-start.1 = ((bf16[8,1,32,64,128]{4,3,2,1,0:T(8,128)(2,1)}), bf16[8,1,32,64,128]{4,3,2,1,0:T(8,128)(2,1)}, u32[]{:S(2)}, u32[]{:S(2)}) async-start(bf16[8,1,32,64,128]{4,3,2,1,0:T(8,128)(2,1)} %broadcast_in_dim.214), calls=%async_computation.1 | async-start | bytes 8388608 | tf_op jit(solution)/shard_map/all_to_all | solution.py:43
  36.1 70.3 %all-to-all-done.1 = bf16[8,1,32,64,128]{4,3,2,1,0:T(8,128)(2,1)} async-done(((bf16[8,1,32,64,128]{4,3,2,1,0:T(8,128)(2,1)}), bf16[8,1,32,64,128]{4,3,2,1,0:T(8,128)(2,1)}, u32[]{:S(2)}, u32[]{:S(2)}) %all-to-all-start.1) | async-done | bytes 4194336 | tf_op jit(solution)/shard_map/all_to_all | solution.py:43
  106.4 7.1 %fusion.31 = f32[32,1,64,128]{3,1,2,0:T(1,128)S(1)} fusion(f32[8,32,1,1]{0,2,3,1:T(1,128)S(1)} %copy.99, bf16[8,32,64,128]{3,2,1,0:T(8,128)(2,1)} %bitcast.28), kind=kOutput, calls=%fused_computation.33 | convolution fusion | flops 25165824 | bytes 5243904 | tf_op jit(solution)/shard_map/kgj,kgjpn->gjpn/dot_general | solution.py:67
  113.7 1.9 broadcast_in_dim.223
  115.6 7.2 %all-to-all-start.2 = ((bf16[4,1,32,64,128]{4,3,2,1,0:T(8,128)(2,1)}), bf16[4,1,32,64,128]{4,3,2,1,0:T(8,128)(2,1)}, u32[]{:S(2)}, u32[]{:S(2)}) async-start(bf16[4,1,32,64,128]{4,3,2,1,0:T(8,128)(2,1)} %broadcast_in_dim.223), calls=%async_computation.2 | async-start | bytes 4194304 | tf_op jit(solution)/shard_map/all_to_all | solution.py:43
  122.9 3.4 %fusion.46 = f32[128,1,32,64]{0,3,2,1:T(8,128)} fusion(bf16[128,32,64]{0,2,1:T(8,128)(2,1)S(1)} %bitcast.159, f32[32,128]{1,0:T(8,128)S(1)} %fusion.107, f32[128,32]{0,1:T(8,128)S(1)} %copy.81, f32[128,128]{1,0:T(8,128)S(1)} %fusion.82, pred[128,128]{1,0:T(8,128)(4,1)S(1)} %iota_compare_fusion), kind=kOutput, calls=%fused_computation.47 | convolution fusion | flops 404750336 | bytes 1687552 | tf_op jit(solution)/shard_map/while/body/eval_jaxpr/gjts,sgjp->tgjp/dot_general | solution.py:108
  126.8 7.3 %fusion.33 = f32[32,1,64,128]{3,1,2,0:T(1,128)S(1)} fusion(f32[8,32,1,1]{0,2,3,1:T(1,128)S(1)} %copy.96, bf16[8,32,64,128]{3,2,1,0:T(8,128)(2,1)} %bitcast.28), kind=kOutput, calls=%fused_computation.35 | convolution fusion | flops 25165824 | bytes 5243904 | tf_op jit(solution)/shard_map/kgj,kgjpn->gjpn/dot_general | solution.py:63
  134.1 32.5 %all-to-all-done.2 = bf16[4,1,32,64,128]{4,3,2,1,0:T(8,128)(2,1)} async-done(((bf16[4,1,32,64,128]{4,3,2,1,0:T(8,128)(2,1)}), bf16[4,1,32,64,128]{4,3,2,1,0:T(8,128)(2,1)}, u32[]{:S(2)}, u32[]{:S(2)}) %all-to-all-start.2) | async-done | bytes 2097184 | tf_op jit(solution)/shard_map/all_to_all | solution.py:43
  166.6 5.8 %fusion.44 = f32[32,1,64,128]{3,1,2,0:T(1,128)S(1)} fusion(f32[4,32,1,1]{0,2,3,1:T(1,128)S(1)} %copy.101, bf16[4,32,64,128]{3,2,1,0:T(8,128)(2,1)} %bitcast.35), kind=kOutput, calls=%fused_computation.45 | convolution fusion | flops 12582912 | bytes 3146240 | tf_op jit(solution)/shard_map/kgj,kgjpn->gjpn/dot_general | solution.py:74
  172.5 0.7 fusion.53
  174.1 1.5 multiply_reduce_fusion
  175.6 17.1 %all-gather.2.cloned.1.call-done = bf16[4096,4352]{0,1:T(8,128)(2,1)} async-done(((bf16[128,4352]{0,1:T(8,128)(2,1)}), bf16[4096,4352]{0,1:T(8,128)(2,1)}) %all-gather.2.cloned.1.call-update) | async-done | bytes 35651600 | tf_op jit(solution)/shard_map/all_gather | solution.py:281
  192.7 3.1 fusion.100
  195.9 1.6 copy.90
  197.5 2.3 copy.92
  199.8 1.1 broadcast_in_dim.226
  200.9 43.2 %while.4 = (s32[]{:T(128)}, f32[1,16,128]{2,1,0:T(8,128)S(1)}, f32[1,16,128]{2,1,0:T(8,128)S(1)}, f32[1,16,128,128]{3,2,1,0:T(8,128)}, s32[4]{0:T(128)S(1)}, /*i...) while((s32[]{:T(128)}, f32[1,16,128]{2,1,0:T(8,128)S(1)}, ...), condition=%wide.region_10.11_spmd.clone, body=%wide.region_5.10_spmd.clone.sunk | while | flops 1101667456 | bytes 37366608 | solution.py:239
  200.9 0.6 dynamic_slice.136
  202.8 8.9 %conditional.3 = ((f32[1,16,128]{2,1,0:T(8,128)S(1)}, f32[1,16,128]{2,1,0:T(8,128)S(1)}, f32[1,16,128,128]{3,2,1,0:T(8,128)})) conditional(s32[]{:T(128)} %convert_element_type.185, (f32[1,16,128]{2,1,0:T(8,128)S(1)}, f32[1,16,128]{2,1,0:T(8,128)S(1)}, f32[1,16,128,128]{3,2,1,0:T(8,128)}) %tuple.54, (s32[]{:T(128)}, s32[]{:T(128)}, ...), branch_computations={%region_6.6_spmd, %region_7.9_spmd} | conditional | flops 1101667456 | bytes 37365860 | solution.py:223
  202.8 0.6 iota_add_fusion
  203.7 1.3 fusion.2
  205.0 2.0 fusion.4
  207.1 3.6 %fusion.12 = f32[1,16,128,128]{3,2,1,0:T(8,128)S(1)} fusion(f32[1024,128,16]{1,0,2:T(8,128)S(1)} %get-tuple-element.261, f32[16,128]{1,0:T(8,128)S(1)} %bitcast.156, pred[128,1024]{0,1:T(8,128)(4,1)S(1)} %broadcast_compare_fusion, f32[1,16,128,128]{3,2,1,0:T(8,128)S(1)} %copy-done.2, f32[16,128]{1,0:T(8,128)S(1)} %get-tuple-element.258, ...), kind=kOutput, calls=%fused_computation.10 | convolution fusion | flops 547880960 | bytes 10895872 | tf_op jit(solution)/shard_map/while/body/eval_jaxpr/cond/branch_1_fun/gjqk,kgd->gjqd/dot_general | solution.py:215
  210.7 1.0 copy-done.3
  211.7 0.6 dynamic_slice.136
  213.6 8.9 %conditional.3 = ((f32[1,16,128]{2,1,0:T(8,128)S(1)}, f32[1,16,128]{2,1,0:T(8,128)S(1)}, f32[1,16,128,128]{3,2,1,0:T(8,128)})) conditional(s32[]{:T(128)} %convert_element_type.185, (f32[1,16,128]{2,1,0:T(8,128)S(1)}, f32[1,16,128]{2,1,0:T(8,128)S(1)}, f32[1,16,128,128]{3,2,1,0:T(8,128)}) %tuple.54, (s32[]{:T(128)}, s32[]{:T(128)}, ...), branch_computations={%region_6.6_spmd, %region_7.9_spmd} | conditional | flops 1101667456 | bytes 37365860 | solution.py:223
  213.6 0.6 iota_add_fusion
  214.5 1.3 fusion.2
  215.8 2.0 fusion.4
  217.9 3.6 %fusion.12 = f32[1,16,128,128]{3,2,1,0:T(8,128)S(1)} fusion(f32[1024,128,16]{1,0,2:T(8,128)S(1)} %get-tuple-element.261, f32[16,128]{1,0:T(8,128)S(1)} %bitcast.156, pred[128,1024]{0,1:T(8,128)(4,1)S(1)} %broadcast_compare_fusion, f32[1,16,128,128]{3,2,1,0:T(8,128)S(1)} %copy-done.2, f32[16,128]{1,0:T(8,128)S(1)} %get-tuple-element.258, ...), kind=kOutput, calls=%fused_computation.10 | convolution fusion | flops 547880960 | bytes 10895872 | tf_op jit(solution)/shard_map/while/body/eval_jaxpr/cond/branch_1_fun/gjqk,kgd->gjqd/dot_general | solution.py:215
  221.5 1.0 copy-done.3
  222.5 0.6 dynamic_slice.136
  224.4 8.9 %conditional.3 = ((f32[1,16,128]{2,1,0:T(8,128)S(1)}, f32[1,16,128]{2,1,0:T(8,128)S(1)}, f32[1,16,128,128]{3,2,1,0:T(8,128)})) conditional(s32[]{:T(128)} %convert_element_type.185, (f32[1,16,128]{2,1,0:T(8,128)S(1)}, f32[1,16,128]{2,1,0:T(8,128)S(1)}, f32[1,16,128,128]{3,2,1,0:T(8,128)}) %tuple.54, (s32[]{:T(128)}, s32[]{:T(128)}, ...), branch_computations={%region_6.6_spmd, %region_7.9_spmd} | conditional | flops 1101667456 | bytes 37365860 | solution.py:223
  225.3 1.3 fusion.2
  226.6 2.0 fusion.4
  228.7 3.6 %fusion.12 = f32[1,16,128,128]{3,2,1,0:T(8,128)S(1)} fusion(f32[1024,128,16]{1,0,2:T(8,128)S(1)} %get-tuple-element.261, f32[16,128]{1,0:T(8,128)S(1)} %bitcast.156, pred[128,1024]{0,1:T(8,128)(4,1)S(1)} %broadcast_compare_fusion, f32[1,16,128,128]{3,2,1,0:T(8,128)S(1)} %copy-done.2, f32[16,128]{1,0:T(8,128)S(1)} %get-tuple-element.258, ...), kind=kOutput, calls=%fused_computation.10 | convolution fusion | flops 547880960 | bytes 10895872 | tf_op jit(solution)/shard_map/while/body/eval_jaxpr/cond/branch_1_fun/gjqk,kgd->gjqd/dot_general | solution.py:215
  232.3 1.0 copy-done.3
  233.3 0.6 dynamic_slice.136
  235.2 8.9 %conditional.3 = ((f32[1,16,128]{2,1,0:T(8,128)S(1)}, f32[1,16,128]{2,1,0:T(8,128)S(1)}, f32[1,16,128,128]{3,2,1,0:T(8,128)})) conditional(s32[]{:T(128)} %convert_element_type.185, (f32[1,16,128]{2,1,0:T(8,128)S(1)}, f32[1,16,128]{2,1,0:T(8,128)S(1)}, f32[1,16,128,128]{3,2,1,0:T(8,128)}) %tuple.54, (s32[]{:T(128)}, s32[]{:T(128)}, ...), branch_computations={%region_6.6_spmd, %region_7.9_spmd} | conditional | flops 1101667456 | bytes 37365860 | solution.py:223
  235.2 0.6 iota_add_fusion
  236.1 1.3 fusion.2
  237.4 2.0 fusion.4
  239.5 3.6 %fusion.12 = f32[1,16,128,128]{3,2,1,0:T(8,128)S(1)} fusion(f32[1024,128,16]{1,0,2:T(8,128)S(1)} %get-tuple-element.261, f32[16,128]{1,0:T(8,128)S(1)} %bitcast.156, pred[128,1024]{0,1:T(8,128)(4,1)S(1)} %broadcast_compare_fusion, f32[1,16,128,128]{3,2,1,0:T(8,128)S(1)} %copy-done.2, f32[16,128]{1,0:T(8,128)S(1)} %get-tuple-element.258, ...), kind=kOutput, calls=%fused_computation.10 | convolution fusion | flops 547880960 | bytes 10895872 | tf_op jit(solution)/shard_map/while/body/eval_jaxpr/cond/branch_1_fun/gjqk,kgd->gjqd/dot_general | solution.py:215
  243.1 1.0 copy-done.3
  244.1 1.6 fusion.77
  246.0 1.6 bitcast_select_fusion.2
  247.7 1.5 collective-permute-start
  249.2 22.9 %slice.29 = bf16[4096,4096]{0,1:T(8,128)(2,1)} slice(bf16[4096,4352]{0,1:T(8,128)(2,1)} %all-gather.2.cloned.1.call-done), slice={[0:4096], [0:4096]} | slice | bytes 67108864 | tf_op jit(solution)/shard_map/slice | solution.py:284
  272.1 8.1 %fusion.35 = bf16[128,2048]{1,0:T(8,128)(2,1)S(1)} fusion(bf16[4096,4096]{0,1:T(8,128)(2,1)} %slice.29, s32[]{:T(128)S(6)} %select_n.148, bf16[128,2048]{1,0:T(8,128)(2,1)S(1)} %collective-permute-done, bf16[128,2048]{1,0:T(8,128)(2,1)S(1)} %get-tuple-element.264, pred[]{:T(512)S(6)} %eq.2), kind=kOutput, calls=%fused_computation.37 | convolution fusion | flops 2152464384 | bytes 18350084 | tf_op jit(solution)/shard_map/tc,dc->td/dot_general | solution.py:300
  280.4 1.7 collective-permute-start.3
  282.1 8.1 %fusion.102 = (bf16[128,2048]{1,0:T(8,128)(2,1)S(1)}, f32[128,2048]{1,0:T(8,128)S(1)}) fusion(bf16[4096,4096]{0,1:T(8,128)(2,1)} %slice.29, s32[]{:T(128)S(6)} %select_n.147, bf16[128,2048]{1,0:T(8,128)(2,1)S(1)} %collective-permute-done, bf16[128,2048]{1,0:T(8,128)(2,1)S(1)} %get-tuple-element.264, pred[]{:T(512)S(6)} %eq.2), kind=kOutput, calls=%fused_computation.146 | convolution fusion | flops 2152464384 | bytes 19398660 | tf_op jit(solution)/shard_map/tc,dc->td/dot_general | solution.py:304
  290.2 1.3 collective-permute-start.2
  291.5 2.6 collective-permute-done.1
  294.1 14.5 %collective-permute-done.3 = bf16[128,2048]{1,0:T(8,128)(2,1)S(1)} collective-permute-done((bf16[128,2048]{1,0:T(8,128)(2,1)S(1)}, bf16[128,2048]{1,0:T(8,128)(2,1)S(1)}, u32[]{:S(2)}, u32[]{:S(2)}) %collective-permute-start.3) | collective-permute-done | bytes 524320 | tf_op jit(solution)/shard_map/ppermute | solution.py:307
  308.6 1.3 fusion.74
  (106 shorter events, 7.3 us)
Async XLA Ops:
  6.5 116.2 %copy-start = (bf16[128,256]{1,0:T(8,128)(2,1)S(1)}, bf16[128,256]{1,0:T(8,128)(2,1)}, u32[]{:S(2)}) copy-start(bf16[128,256]{1,0:T(8,128)(2,1)} %param.21) | copy-start | bytes 196612
  6.5 14.3 %copy-start.6 = (bf16[128,4096]{1,0:T(8,128)(2,1)S(1)}, bf16[128,4096]{1,0:T(8,128)(2,1)}, u32[]{:S(2)}) copy-start(bf16[128,4096]{1,0:T(8,128)(2,1)} %param.26) | copy-start | bytes 3145732
  6.5 15.8 %copy-start.7 = (bf16[128,256]{1,0:T(8,128)(2,1)S(1)}, bf16[128,256]{1,0:T(8,128)(2,1)}, u32[]{:S(2)}) copy-start(bf16[128,256]{1,0:T(8,128)(2,1)} %param.20) | copy-start | bytes 196612
  6.5 186.2 %all-gather.2.cloned.1.call-start = ((), (), s32[]{:S(2)}) async-start(), calls=%async_computation.3 | async-start | bytes 36765696 | tf_op jit(solution)/shard_map/all_gather | solution.py:281
  12.4 13.8 %all-to-all-start = ((f32[32,1,32]{2,1,0:T(1,128)}), f32[32,1,32]{2,1,0:T(1,128)S(1)}, u32[]{:S(2)}, u32[]{:S(2)}) async-start(f32[32,1,32]{2,1,0:T(1,128)} %broadcast_in_dim.208), calls=%async_computation | async-start | bytes 32768 | tf_op jit(solution)/shard_map/all_to_all | solution.py:43
  29.2 5.1 %copy-start.9 = (f32[64]{0:T(128)S(1)}, f32[64]{0:T(128)}, u32[]{:S(2)}) copy-start(f32[64]{0:T(128)} %param.24) | copy-start | bytes 772
  29.2 6.4 %copy-start.8 = (f32[128,64]{0,1:T(8,128)S(1)}, f32[128,64]{0,1:T(8,128)}, u32[]{:S(2)}) copy-start(f32[128,64]{0,1:T(8,128)} %param.22) | copy-start | bytes 98308
  29.2 77.2 %all-to-all-start.1 = ((bf16[8,1,32,64,128]{4,3,2,1,0:T(8,128)(2,1)}), bf16[8,1,32,64,128]{4,3,2,1,0:T(8,128)(2,1)}, u32[]{:S(2)}, u32[]{:S(2)}) async-start(bf16[8,1,32,64,128]{4,3,2,1,0:T(8,128)(2,1)} %broadcast_in_dim.214), calls=%async_computation.1 | async-start | bytes 8388608 | tf_op jit(solution)/shard_map/all_to_all | solution.py:43
  115.6 51.0 %all-to-all-start.2 = ((bf16[4,1,32,64,128]{4,3,2,1,0:T(8,128)(2,1)}), bf16[4,1,32,64,128]{4,3,2,1,0:T(8,128)(2,1)}, u32[]{:S(2)}, u32[]{:S(2)}) async-start(bf16[4,1,32,64,128]{4,3,2,1,0:T(8,128)(2,1)} %broadcast_in_dim.223), calls=%async_computation.2 | async-start | bytes 4194304 | tf_op jit(solution)/shard_map/all_to_all | solution.py:43
  166.6 6.5 %copy-start.4 = (f32[128,1,32,64]{0,3,2,1:T(8,128)S(1)}, f32[128,1,32,64]{0,3,2,1:T(8,128)}, u32[]{:S(2)}) copy-start(f32[128,1,32,64]{0,3,2,1:T(8,128)} %fusion.46) | copy-start | bytes 3145732
  200.9 45.1 %dynamic-slice-start = ((f32[4096]{0:T(1024)}, s32[]{:T(128)}), f32[2048]{0:T(1024)S(1)}, s32[]{:S(2)}) async-start(f32[4096]{0:T(1024)} %param.25, s32[]{:T(128)} %select_n.133), calls=%async_computation.4 | async-start | bytes 16896 | tf_op jit(solution)/shard_map/dynamic_slice | solution.py:247
  205.0 2.0 copy-start.2
  210.7 1.0 copy-start.3
  215.8 2.0 copy-start.2
  221.5 1.0 copy-start.3
  226.6 2.0 copy-start.2
  232.3 1.0 copy-start.3
  237.4 2.0 copy-start.2
  243.1 1.0 copy-start.3
  247.7 24.5 %collective-permute-start = (bf16[128,2048]{1,0:T(8,128)(2,1)S(1)}, bf16[128,2048]{1,0:T(8,128)(2,1)S(1)}, u32[]{:S(2)}, u32[]{:S(2)}) collective-permute-start(bf16[128,2048]{1,0:T(8,128)(2,1)S(1)} %get-tuple-element.265), channel_id=1, source_target_pairs={{0,64},{64,0},{1,65},{65,1},{2,66},{66,2},{3,67},{67,3},{4,68},{68... | collective-permute-start | bytes 1572872 | tf_op jit(solution)/shard_map/ppermute | solution.py:85
  280.3 28.4 %copy-start.5 = (bf16[128,2048]{1,0:T(8,128)(2,1)S(1)}, bf16[128,2048]{1,0:T(8,128)(2,1)}, u32[]{:S(2)}) copy-start(bf16[128,2048]{1,0:T(8,128)(2,1)} %param.17) | copy-start | bytes 1572868
  280.3 13.9 %collective-permute-start.1 = (bf16[128,2048]{1,0:T(8,128)(2,1)S(1)}, bf16[128,2048]{1,0:T(8,128)(2,1)S(1)}, u32[]{:S(2)}, u32[]{:S(2)}) collective-permute-start(bf16[128,2048]{1,0:T(8,128)(2,1)S(1)} %fusion.35), channel_id=1, source_target_pairs={{0,1},{1,0},{2,3},{3,2},{4,5},{5,4},{6,7},{7,6},{8,9},{9,8},{10,11... | collective-permute-start | bytes 1572872 | tf_op jit(solution)/shard_map/ppermute | solution.py:85
  280.4 28.3 %collective-permute-start.3 = (bf16[128,2048]{1,0:T(8,128)(2,1)S(1)}, bf16[128,2048]{1,0:T(8,128)(2,1)S(1)}, u32[]{:S(2)}, u32[]{:S(2)}) collective-permute-start(bf16[128,2048]{1,0:T(8,128)(2,1)S(1)} %fusion.35), channel_id=1, source_target_pairs={{0,65},{1,64},{2,67},{3,66},{4,69},{5,68},{6,71},{7,70},{8,73},{9,... | collective-permute-start | bytes 1572872 | tf_op jit(solution)/shard_map/ppermute | solution.py:307
  282.1 27.9 %copy-start.1 = (bf16[128,256]{1,0:T(8,128)(2,1)S(1)}, bf16[128,256]{1,0:T(8,128)(2,1)}, u32[]{:S(2)}) copy-start(bf16[128,256]{1,0:T(8,128)(2,1)} %param.21) | copy-start | bytes 196612
  290.2 18.4 %collective-permute-start.2 = (bf16[128,2048]{1,0:T(8,128)(2,1)S(1)}, bf16[128,2048]{1,0:T(8,128)(2,1)S(1)}, u32[]{:S(2)}, u32[]{:S(2)}) collective-permute-start(bf16[128,2048]{1,0:T(8,128)(2,1)S(1)} %get-tuple-element.270), channel_id=1, source_target_pairs={{0,64},{1,65},{2,66},{3,67},{4,68},{5,69},{6,70},{7,71},{8,72},{9,... | collective-permute-start | bytes 1572872 | tf_op jit(solution)/shard_map/ppermute | solution.py:91
Sparse Core Ops, SparseCore 0:
  10.1 182.5 all-gather.1
